TPU v7x, 512 devices: a whole 4x4x16 slice. The times are simulated.
512 devices in a mesh: kx: 16 (over x_lo, y, core), ky: 32 (over z, x_hi).
Axes of the slice: x: 4 (x_hi: 2, x_lo: 2; x = x_hi * 2 + x_lo), y: 4, z: 16, core: 2. Of those that a mesh axis runs over, the one named last changes fastest.
Arguments:
- packed_state_matrix: float32 [16, 512, 4096], P(None, 'kx', 'ky'), may hold values from -1 to 1, as said below
- energies: float32 [4, 512, 4096], P(None, 'kx', 'ky'), may hold values from -2.4 to 2.4
- dipole_x: float32 [12, 512, 4096], P(None, 'kx', 'ky'), may hold values from -2.5 to 2.5
- dipole_y: float32 [12, 512, 4096], P(None, 'kx', 'ky'), may hold values from -2.5 to 2.5
- interaction: float32 [512, 4096], P('ky'), may hold values from 0.3 to 5, as said below
- driving_field: float32 [2], replicated, may hold values from 0.3 to 1
Outputs:
- section_slope: float32 [16, 512, 4096], P(None, 'kx', 'ky')
- field_next: float32 [2], replicated
Inputs may be any that keep to these rules, and one draw needn't show every extreme that they name: `packed_state_matrix`: components 0 to 3 lie in 0 to 1. interaction at (p, q) equals interaction at ((-p) mod 512, q) and at (p, (-q) mod 4096).
All inputs are finite; a program needn't handle non-finite values.
Results may differ from a plain program's by a relative error of at most 0.000054.
Values sent between devices are 32-bit elements; how exact they have to be, the bound alone decides.
No kernel may reach another device: no remote copies, remote signals or barrier semaphores. Data moves between devices by JAX's collectives and lax.ppermute only.
A program may use at most 64 MiB of HBM per device.

v0:
```python
from functools import partial
import math

import jax
import jax.numpy as jnp
from jax import lax
from jax.sharding import PartitionSpec as P

BAND_PAIRS = ((0, 1), (0, 2), (0, 3), (1, 2), (1, 3), (2, 3))
DEPHASING = 0.5
SHIELDING_LEVEL = 2.0
COUPLING = 40.0


def with_halo(array, sides, width):
    for axis, dim in sides:
        devices, length = (lax.axis_size(axis), array.shape[dim])
        up = [(i, (i + 1) % devices) for i in range(devices)]
        down = [(j, i) for i, j in up]
        last = lax.slice_in_dim(array, length - width, length, axis=dim)
        initial = lax.slice_in_dim(array, 0, width, axis=dim)
        before = lax.ppermute(last, axis, up)
        after = lax.ppermute(initial, axis, down)
        array = jnp.concatenate([before, array, after], axis=dim)
    return array


def unpack(packed):
    real_entries = []
    imaginary_entries = []
    for band_one in range(4):
        real_entries.append([None, None, None, None])
        imaginary_entries.append([None, None, None, None])
    for band_one in range(4):
        real_entries[band_one][band_one] = packed[band_one]
    for number, band_pair in enumerate(BAND_PAIRS):
        upper_band, lower_band = band_pair
        real_entries[upper_band][lower_band] = packed[4 + number]
        real_entries[lower_band][upper_band] = packed[4 + number]
        imaginary_entries[upper_band][lower_band] = packed[10 + number]
        imaginary_entries[lower_band][upper_band] = -packed[10 + number]
    return (real_entries, imaginary_entries)


def product_sum(terms):
    summed = None
    for factor, left_value, right_value in terms:
        if left_value is None or right_value is None:
            continue
        product = factor * left_value * right_value
        summed = product if summed is None else summed + product
    return summed


def commutator(coupled, packed_state_matrix):
    coupled_real, coupled_imaginary = unpack(coupled)
    state_real, state_imaginary = unpack(packed_state_matrix)

    def element(row_band, column_band):
        real_terms = []
        imaginary_terms = []
        for middle in range(4):
            real_terms.append(
                (1.0, coupled_real[row_band][middle], state_real[middle][column_band])
            )
            real_terms.append(
                (-1.0, coupled_imaginary[row_band][middle], state_imaginary[middle][column_band])
            )
            real_terms.append(
                (-1.0, state_real[row_band][middle], coupled_real[middle][column_band])
            )
            real_terms.append(
                (1.0, state_imaginary[row_band][middle], coupled_imaginary[middle][column_band])
            )
            imaginary_terms.append(
                (1.0, coupled_real[row_band][middle], state_imaginary[middle][column_band])
            )
            imaginary_terms.append(
                (1.0, coupled_imaginary[row_band][middle], state_real[middle][column_band])
            )
            imaginary_terms.append(
                (-1.0, state_real[row_band][middle], coupled_imaginary[middle][column_band])
            )
            imaginary_terms.append(
                (-1.0, state_imaginary[row_band][middle], coupled_real[middle][column_band])
            )
        return (product_sum(real_terms), product_sum(imaginary_terms))

    diagonal = []
    upper_real = []
    upper_imaginary = []
    for band_one in range(4):
        diagonal.append(element(band_one, band_one)[1])
    for upper_band, lower_band in BAND_PAIRS:
        real_value, imaginary_value = element(upper_band, lower_band)
        upper_real.append(imaginary_value)
        upper_imaginary.append(-real_value)
    return jnp.stack(diagonal + upper_real + upper_imaginary)


def slope_terms(
    packed_state_matrix,
    energies,
    self_energy,
    gradient_x,
    gradient_y,
    dipole_x,
    dipole_y,
    driving_field,
):
    field_x = driving_field[0]
    field_y = driving_field[1]
    coupled = jnp.concatenate(
        [energies + self_energy[0:4], self_energy[4:16] + field_x * dipole_x + field_y * dipole_y]
    )
    rotation = commutator(coupled, packed_state_matrix)
    drift = rotation + field_x * gradient_x + field_y * gradient_y
    return jnp.concatenate([drift[0:4], drift[4:16] - DEPHASING * packed_state_matrix[4:16]])


def angle_table(row_count, column_count, period, direction):
    row_index = lax.broadcasted_iota(jnp.int32, (row_count, column_count), 0)
    column_index = lax.broadcasted_iota(jnp.int32, (row_count, column_count), 1)
    phase_angle = (row_index * column_index % period).astype(jnp.float32) * (
        direction * 2.0 * math.pi / period
    )
    return (jnp.cos(phase_angle), jnp.sin(phase_angle))


def complex_contract(einsum_form, data_real, data_imaginary, table_real, table_imaginary):
    contract = partial(
        jnp.einsum, precision=lax.Precision.HIGHEST, preferred_element_type=jnp.float32
    )
    if data_imaginary is None:
        return (
            contract(einsum_form, data_real, table_real),
            contract(einsum_form, data_real, table_imaginary),
        )
    real_out = contract(einsum_form, data_real, table_real) - contract(
        einsum_form, data_imaginary, table_imaginary
    )
    imaginary_out = contract(einsum_form, data_real, table_imaginary) + contract(
        einsum_form, data_imaginary, table_real
    )
    return (real_out, imaginary_out)


def transform(data_real, data_imaginary, direction, along_last):
    length = data_real.shape[-1] if along_last else data_real.shape[-2]
    outer_size = 16
    inner_size = length // outer_size
    outer_cosine, outer_sine = angle_table(outer_size, outer_size, outer_size, direction)
    twist_cosine, twist_sine = angle_table(outer_size, inner_size, length, direction)
    inner_cosine, inner_sine = angle_table(inner_size, inner_size, inner_size, direction)
    if along_last:
        split_shape = data_real.shape[:-1] + (outer_size, inner_size)
        first_form = "...aq,ab->...bq"
        second_form = "...bq,qc->...cb"
    else:
        split_shape = data_real.shape[:-2] + (outer_size, inner_size, data_real.shape[-1])
        first_form = "...aqt,ab->...bqt"
        second_form = "...bqt,qc->...cbt"
        twist_cosine = twist_cosine[:, :, None]
        twist_sine = twist_sine[:, :, None]
    part_real = data_real.reshape(split_shape)
    part_imaginary = None if data_imaginary is None else data_imaginary.reshape(split_shape)
    section_real, section_imaginary = complex_contract(
        first_form, part_real, part_imaginary, outer_cosine, outer_sine
    )
    turned_real = section_real * twist_cosine - section_imaginary * twist_sine
    turned_imaginary = section_real * twist_sine + section_imaginary * twist_cosine
    final_real, final_imaginary = complex_contract(
        second_form, turned_real, turned_imaginary, inner_cosine, inner_sine
    )
    return (final_real.reshape(data_real.shape), final_imaginary.reshape(data_real.shape))


def convolve(source, interaction, primitive_tile_total):
    along_kx = lax.all_to_all(source, "kx", split_axis=0, concat_axis=1, tiled=True)
    broad_nonimaginary, wide_imaginary = transform(along_kx, None, -1.0, False)
    joined = jnp.stack([broad_nonimaginary, wide_imaginary])
    along_ky = lax.all_to_all(joined, "ky", split_axis=2, concat_axis=3, tiled=True)
    line_real, line_imaginary = transform(along_ky[0], along_ky[1], -1.0, True)
    line_real, line_imaginary = transform(
        line_real * interaction, line_imaginary * interaction, 1.0, True
    )
    returned = lax.all_to_all(
        jnp.stack([line_real, line_imaginary]), "ky", split_axis=3, concat_axis=2, tiled=True
    )
    final_real, final_imaginary = transform(returned[0], returned[1], 1.0, False)
    normalizer = 1.0 / primitive_tile_total
    return lax.all_to_all(final_real * normalizer, "kx", split_axis=1, concat_axis=0, tiled=True)


def collect_moments(local_sums, primitive_tile_total):
    return lax.psum(local_sums, ("kx", "ky")) / primitive_tile_total


def body(packed_state_matrix, energies, dipole_x, dipole_y, interaction, driving_field):
    rows_local = packed_state_matrix.shape[1]
    columns_local = packed_state_matrix.shape[2]
    primitive_tile_total = rows_local * columns_local * lax.axis_size("kx") * lax.axis_size("ky")
    stacked = jnp.concatenate([packed_state_matrix, energies])
    padded = with_halo(stacked, (("kx", 1), ("ky", 2)), 2)
    column_core = padded[:, :, 2:-2]
    row_core = padded[:, 2:-2, :]
    gradient_x = (
        8.0 * (column_core[:, 3:-1] - column_core[:, 1:-3])
        - (column_core[:, 4:] - column_core[:, :-4])
    ) / 12.0
    gradient_y = (
        8.0 * (row_core[:, :, 3:-1] - row_core[:, :, 1:-3])
        - (row_core[:, :, 4:] - row_core[:, :, :-4])
    ) / 12.0
    populations = packed_state_matrix[0:4]
    local_sums = jnp.stack(
        [
            jnp.sum(packed_state_matrix[2] + packed_state_matrix[3]),
            jnp.sum(gradient_x[16:20] * populations),
            jnp.sum(gradient_y[16:20] * populations),
        ]
    )
    totals = collect_moments(local_sums, primitive_tile_total)
    shielding_multiplier = 1.0 / (1.0 + SHIELDING_LEVEL * totals[0])
    self_energy = -convolve(
        packed_state_matrix * shielding_multiplier, interaction, primitive_tile_total
    )
    section_slope = slope_terms(
        packed_state_matrix,
        energies,
        self_energy,
        gradient_x[0:16],
        gradient_y[0:16],
        dipole_x,
        dipole_y,
        driving_field,
    )
    field_next = driving_field - COUPLING * totals[1:3]
    return (section_slope, field_next)


def solution(mesh):
    in_specs = (
        P(None, "kx", "ky"),
        P(None, "kx", "ky"),
        P(None, "kx", "ky"),
        P(None, "kx", "ky"),
        P("ky", None),
        P(),
    )
    out_specs = (P(None, "kx", "ky"), P())
    return jax.shard_map(body, mesh=mesh, in_specs=in_specs, out_specs=out_specs, check_vma=False)
```

profile of v0, /device:TPU:1, one launch (start us, length us, event | category | flops | bytes accessed | tf_op | source)
XLA Modules:
  0.0 350.0 jit_solution(518717469962296883)
XLA Ops:
  2.5 8.8 %collective-permute-start = (f32[20,2,128]{2,1,0:T(2,128)S(1)}, f32[20,2,128]{2,1,0:T(2,128)S(1)}, u32[]{:S(2)}, u32[]{:S(2)}) collective-permute-start(f32[20,2,128]{2,1,0:T(2,128)S(1)} %get-tuple-element.15), channel_id=1, source_target_pairs={{32,0},{64,32},{96,64},{128,96},{160,128},{192,160},{224,192},{256... | collective-permute-start | bytes 61448 | tf_op jit(solution)/shard_map/ppermute | solution.py:23
  14.9 10.5 %collective-permute-start.2 = (f32[20,36,2]{2,1,0:T(8,128)S(1)}, f32[20,36,2]{2,1,0:T(8,128)S(1)}, u32[]{:S(2)}, u32[]{:S(2)}) collective-permute-start(f32[20,36,2]{2,1,0:T(8,128)S(1)} %get-tuple-element.12), channel_id=1, source_target_pairs={{1,0},{2,1},{3,2},{4,3},{5,4},{6,5},{7,6},{8,7},{9,8},{10,9},{11,1... | collective-permute-start | bytes 17288 | tf_op jit(solution)/shard_map/ppermute | solution.py:23
  25.4 1.9 collective-permute-start.3
  27.5 2.8 collective-permute-done.2
  30.3 7.4 %collective-permute-done.3 = f32[20,36,2]{2,1,0:T(8,128)S(1)} collective-permute-done((f32[20,36,2]{2,1,0:T(8,128)S(1)}, f32[20,36,2]{2,1,0:T(8,128)S(1)}, u32[]{:S(2)}, u32[]{:S(2)}) %collective-permute-start.3) | collective-permute-done | bytes 5792 | tf_op jit(solution)/shard_map/ppermute | solution.py:22
  39.1 2.1 pad_maximum_fusion.12
  41.2 110.1 %psum.7 = f32[3]{0:T(128)S(1)} all-reduce(f32[3]{0:T(128)S(1)} %pad_maximum_fusion.12), channel_id=1, replica_groups=mesh['kx'=16,'ky'=32] {'kx','ky'}, use_global_device_ids=true, to_apply=%region_3.0 | all-reduce | flops 3 | bytes 24 | tf_op jit(solution)/shard_map/psum | solution.py:196
  152.6 4.3 %all-to-all-start = ((f32[16,32,128]{2,1,0:T(8,128)}), f32[16,32,128]{2,1,0:T(8,128)S(1)}, u32[]{:S(2)}, u32[]{:S(2)}) async-start(f32[16,32,128]{2,1,0:T(8,128)} %broadcast_multiply_fusion), calls=%async_computation | async-start | bytes 524288 | tf_op jit(solution)/shard_map/all_to_all | solution.py:179
  156.9 7.2 %all-to-all-done = f32[16,32,128]{2,1,0:T(8,128)S(1)} async-done(((f32[16,32,128]{2,1,0:T(8,128)}), f32[16,32,128]{2,1,0:T(8,128)S(1)}, u32[]{:S(2)}, u32[]{:S(2)}) %all-to-all-start) | async-done | bytes 262176 | tf_op jit(solution)/shard_map/all_to_all | solution.py:179
  168.8 7.4 %all-to-all-start.1 = ((f32[2,1,512,128]{3,1,0,2:T(1,128)}), f32[2,1,512,128]{3,1,0,2:T(1,128)S(1)}, u32[]{:S(2)}, u32[]{:S(2)}) async-start(f32[2,1,512,128]{3,1,0,2:T(1,128)} %copy.69), calls=%async_computation.1 | async-start | bytes 1048576 | tf_op jit(solution)/shard_map/all_to_all | solution.py:182
  177.0 29.3 %all-to-all-done.1 = f32[2,1,512,128]{3,1,0,2:T(1,128)S(1)} async-done(((f32[2,1,512,128]{3,1,0,2:T(1,128)}), f32[2,1,512,128]{3,1,0,2:T(1,128)S(1)}, u32[]{:S(2)}, u32[]{:S(2)}) %all-to-all-start.1) | async-done | bytes 524320 | tf_op jit(solution)/shard_map/all_to_all | solution.py:182
  209.9 2.1 fusion.34
  215.5 3.2 fusion.5
  226.2 2.1 fusion.26
  231.9 3.1 fusion.1
  238.2 6.8 %copy.77 = f32[2,1,16,4096]{2,1,0,3:T(1,128)} copy(f32[2,1,16,4096]{3,2,1,0:T(8,128)S(1)} %pad_maximum_fusion.1) | data formatting | bytes 1048576 | tf_op jit(solution)/shard_map/stack | solution.py:188
  245.5 16.6 %reduce.1 = f32[4096,2,16]{2,1,0:T(2,128)} reduce(f32[4096,2,1,16]{3,2,1,0:T(1,128)} %bitcast.173, f32[]{:T(128)} %broadcast.599), dimensions={2}, to_apply=%bitcast.157.reduce_sub_computation | reduce | bytes 1048580
  262.1 7.9 %reshape.309 = f32[32,1,4096]{2,1,0:T(1,128)} reshape(f32[4096,2,16]{2,1,0:T(2,128)} %reduce.1) | data formatting | bytes 1048576
  270.0 7.0 %all-to-all-start.2 = ((f32[32,1,4096]{2,1,0:T(1,128)}), f32[32,1,4096]{2,1,0:T(1,128)S(1)}, u32[]{:S(2)}, u32[]{:S(2)}) async-start(f32[32,1,4096]{2,1,0:T(1,128)} %reshape.309), calls=%async_computation.2 | async-start | bytes 1048576 | tf_op jit(solution)/shard_map/all_to_all | solution.py:187
  277.2 30.4 %all-to-all-done.2 = f32[32,1,4096]{2,1,0:T(1,128)S(1)} async-done(((f32[32,1,4096]{2,1,0:T(1,128)}), f32[32,1,4096]{2,1,0:T(1,128)S(1)}, u32[]{:S(2)}, u32[]{:S(2)}) %all-to-all-start.2) | async-done | bytes 524320 | tf_op jit(solution)/shard_map/all_to_all | solution.py:187
  309.5 9.3 %reshape.310 = f32[4096,2,1,16]{3,2,1,0:T(1,128)} reshape(f32[32,4096]{1,0:T(8,128)S(1)} %reduce.2) | data formatting | bytes 1048576
  318.7 8.1 %copy.78 = f32[2,1,16,4096]{3,1,2,0:T(1,128)S(1)} copy(f32[2,1,16,4096]{2,1,0,3:T(1,128)} %bitcast.172) | data formatting | bytes 1048576 | tf_op jit(solution)/shard_map/all_to_all | solution.py:187
  331.3 7.0 %all-to-all-start.3 = ((f32[1,512,128]{2,0,1:T(1,128)}), f32[1,512,128]{2,0,1:T(1,128)S(1)}, u32[]{:S(2)}, u32[]{:S(2)}) async-start(f32[1,512,128]{2,0,1:T(1,128)} %bitcast.51), calls=%async_computation.3 | async-start | bytes 524288 | tf_op jit(solution)/shard_map/all_to_all | solution.py:192
  339.5 6.0 %all-to-all-done.3 = f32[1,512,128]{2,0,1:T(1,128)S(1)} async-done(((f32[1,512,128]{2,0,1:T(1,128)}), f32[1,512,128]{2,0,1:T(1,128)S(1)}, u32[]{:S(2)}, u32[]{:S(2)}) %all-to-all-start.3) | async-done | bytes 262176 | tf_op jit(solution)/shard_map/all_to_all | solution.py:192
  (121 shorter events, 47.0 us)
Async XLA Ops:
  2.5 12.1 %collective-permute-start = (f32[20,2,128]{2,1,0:T(2,128)S(1)}, f32[20,2,128]{2,1,0:T(2,128)S(1)}, u32[]{:S(2)}, u32[]{:S(2)}) collective-permute-start(f32[20,2,128]{2,1,0:T(2,128)S(1)} %get-tuple-element.15), channel_id=1, source_target_pairs={{32,0},{64,32},{96,64},{128,96},{160,128},{192,160},{224,192},{256... | collective-permute-start | bytes 61448 | tf_op jit(solution)/shard_map/ppermute | solution.py:23
  11.3 3.4 collective-permute-start.1
  14.7 23.8 %copy-start = (f32[16,32,128]{2,1,0:T(8,128)S(1)}, f32[16,32,128]{2,1,0:T(8,128)}, u32[]{:S(2)}) copy-start(f32[16,32,128]{2,1,0:T(8,128)} %param.6) | copy-start | bytes 786436
  14.9 15.4 %collective-permute-start.2 = (f32[20,36,2]{2,1,0:T(8,128)S(1)}, f32[20,36,2]{2,1,0:T(8,128)S(1)}, u32[]{:S(2)}, u32[]{:S(2)}) collective-permute-start(f32[20,36,2]{2,1,0:T(8,128)S(1)} %get-tuple-element.12), channel_id=1, source_target_pairs={{1,0},{2,1},{3,2},{4,3},{5,4},{6,5},{7,6},{8,7},{9,8},{10,9},{11,1... | collective-permute-start | bytes 17288 | tf_op jit(solution)/shard_map/ppermute | solution.py:23
  25.4 12.3 %collective-permute-start.3 = (f32[20,36,2]{2,1,0:T(8,128)S(1)}, f32[20,36,2]{2,1,0:T(8,128)S(1)}, u32[]{:S(2)}, u32[]{:S(2)}) collective-permute-start(f32[20,36,2]{2,1,0:T(8,128)S(1)} %get-tuple-element.13), channel_id=1, source_target_pairs={{0,1},{1,2},{2,3},{3,4},{4,5},{5,6},{6,7},{7,8},{8,9},{9,10},{10,1... | collective-permute-start | bytes 17288 | tf_op jit(solution)/shard_map/ppermute | solution.py:22
  151.2 0.5 copy-start.10
  152.6 11.5 %all-to-all-start = ((f32[16,32,128]{2,1,0:T(8,128)}), f32[16,32,128]{2,1,0:T(8,128)S(1)}, u32[]{:S(2)}, u32[]{:S(2)}) async-start(f32[16,32,128]{2,1,0:T(8,128)} %broadcast_multiply_fusion), calls=%async_computation | async-start | bytes 524288 | tf_op jit(solution)/shard_map/all_to_all | solution.py:179
  168.8 37.5 %all-to-all-start.1 = ((f32[2,1,512,128]{3,1,0,2:T(1,128)}), f32[2,1,512,128]{3,1,0,2:T(1,128)S(1)}, u32[]{:S(2)}, u32[]{:S(2)}) async-start(f32[2,1,512,128]{3,1,0,2:T(1,128)} %copy.69), calls=%async_computation.1 | async-start | bytes 1048576 | tf_op jit(solution)/shard_map/all_to_all | solution.py:182
  176.3 35.6 %copy-start.7 = (f32[16,256]{1,0:T(8,128)}, f32[16,256]{1,0:T(8,128)S(1)}, u32[]{:S(2)}) copy-start(f32[16,256]{1,0:T(8,128)S(1)} %get-tuple-element.22) | copy-start | bytes 49156
  176.3 35.6 %copy-start.8 = (f32[16,256]{1,0:T(8,128)}, f32[16,256]{1,0:T(8,128)S(1)}, u32[]{:S(2)}) copy-start(f32[16,256]{1,0:T(8,128)S(1)} %get-tuple-element.23) | copy-start | bytes 49156
  208.5 3.5 copy-start.1
  222.8 2.1 copy-start.6
  224.8 3.5 copy-start.2
  270.0 37.5 %all-to-all-start.2 = ((f32[32,1,4096]{2,1,0:T(1,128)}), f32[32,1,4096]{2,1,0:T(1,128)S(1)}, u32[]{:S(2)}, u32[]{:S(2)}) async-start(f32[32,1,4096]{2,1,0:T(1,128)} %reshape.309), calls=%async_computation.2 | async-start | bytes 1048576 | tf_op jit(solution)/shard_map/all_to_all | solution.py:187
  328.3 10.0 %copy-start.9 = (f32[2]{0:T(128)S(1)}, f32[2]{0:T(128)}, u32[]{:S(2)}) copy-start(f32[2]{0:T(128)} %param.11) | copy-start | bytes 28
  328.3 10.6 %copy-start.11 = (f32[3]{0:T(128)S(1)}, f32[3]{0:T(128)}, u32[]{:S(2)}) copy-start(f32[3]{0:T(128)} %copy-done.10) | copy-start | bytes 40
  328.8 16.9 %copy-start.4 = (f32[12,32,128]{2,1,0:T(8,128)S(1)}, f32[12,32,128]{2,1,0:T(8,128)}, u32[]{:S(2)}) copy-start(f32[12,32,128]{2,1,0:T(8,128)} %param.9) | copy-start | bytes 589828
  328.8 16.9 %copy-start.5 = (f32[12,32,128]{2,1,0:T(8,128)S(1)}, f32[12,32,128]{2,1,0:T(8,128)}, u32[]{:S(2)}) copy-start(f32[12,32,128]{2,1,0:T(8,128)} %param.8) | copy-start | bytes 589828
  329.9 17.3 %copy-start.3 = (f32[4,32,128]{2,1,0:T(8,128)S(1)}, f32[4,32,128]{2,1,0:T(8,128)}, u32[]{:S(2)}) copy-start(f32[4,32,128]{2,1,0:T(8,128)} %param.7) | copy-start | bytes 196612
  331.3 14.2 %all-to-all-start.3 = ((f32[1,512,128]{2,0,1:T(1,128)}), f32[1,512,128]{2,0,1:T(1,128)S(1)}, u32[]{:S(2)}, u32[]{:S(2)}) async-start(f32[1,512,128]{2,0,1:T(1,128)} %bitcast.51), calls=%async_computation.3 | async-start | bytes 524288 | tf_op jit(solution)/shard_map/all_to_all | solution.py:192
where the time goes:
time: 356 us; the launch traced here: 350 us
  blocking collectives  110 us (31%)
  waiting for transfers between devices  83 us (23%)
  local copies, waits for them, and re-layouts  49.8 us (14%)
  starting transfers between devices  48.9 us (14%)
  other arithmetic  31 us (9%)
  matrix products  25.5 us (7%)
    psum x1, blocking collectives, collect_moments(): return lax.psum(local_sums, ('kx', 'ky')) / primitive_tile_total  110 us
    all_to_all x1, waiting for transfers between devices, convolve(): lax.all_to_all(jnp.stack([line_real, line_imaginary]), 'ky', split_axis=3...  30.4 us
    all_to_all x1, waiting for transfers between devices, convolve(): lax.all_to_all(joined, 'ky', split_axis=2, concat_axis=3, tiled=True)  29.3 us
    unnamed x30, local copies, waits for them, and re-layouts  19.4 us
    ppermute x2, starting transfers between devices, with_halo(): after = lax.ppermute(initial, axis, down)  19.3 us
    unnamed x16, other arithmetic  17.1 us
    another operation x3, local copies, waits for them, and re-layouts, convolve(): jnp.stack([line_real, line_imaginary])  9.92 us
    dot_general x6, matrix products, complex_contract(): contract(einsum_form, data_imaginary, table_real)  8.2 us
  transfers between devices with their start and end apart: 8, of which 6 were waited for; matrix products, arithmetic and copies ran while one was open for 1% of the time, Pallas kernels for 0%

commit v1 on v0

--- a/solution.py
+++ b/solution.py
@@ -1,4 +1,3 @@
-from functools import partial
 import math
 
 import jax
@@ -10,19 +9,6 @@
 DEPHASING = 0.5
 SHIELDING_LEVEL = 2.0
 COUPLING = 40.0
-
-
-def with_halo(array, sides, width):
-    for axis, dim in sides:
-        devices, length = (lax.axis_size(axis), array.shape[dim])
-        up = [(i, (i + 1) % devices) for i in range(devices)]
-        down = [(j, i) for i, j in up]
-        last = lax.slice_in_dim(array, length - width, length, axis=dim)
-        initial = lax.slice_in_dim(array, 0, width, axis=dim)
-        before = lax.ppermute(last, axis, up)
-        after = lax.ppermute(initial, axis, down)
-        array = jnp.concatenate([before, array, after], axis=dim)
-    return array
 
 
 def unpack(packed):
@@ -118,82 +104,96 @@
     return jnp.concatenate([drift[0:4], drift[4:16] - DEPHASING * packed_state_matrix[4:16]])
 
 
-def angle_table(row_count, column_count, period, direction):
+def contract(einsum_form, left, right):
+    return jnp.einsum(
+        einsum_form, left, right, precision=lax.Precision.HIGHEST, preferred_element_type=jnp.float32
+    )
+
+
+def angles(row_count, column_count, period):
     row_index = lax.broadcasted_iota(jnp.int32, (row_count, column_count), 0)
     column_index = lax.broadcasted_iota(jnp.int32, (row_count, column_count), 1)
-    phase_angle = (row_index * column_index % period).astype(jnp.float32) * (
-        direction * 2.0 * math.pi / period
-    )
-    return (jnp.cos(phase_angle), jnp.sin(phase_angle))
-
-
-def complex_contract(einsum_form, data_real, data_imaginary, table_real, table_imaginary):
-    contract = partial(
-        jnp.einsum, precision=lax.Precision.HIGHEST, preferred_element_type=jnp.float32
-    )
-    if data_imaginary is None:
-        return (
-            contract(einsum_form, data_real, table_real),
-            contract(einsum_form, data_real, table_imaginary),
-        )
-    real_out = contract(einsum_form, data_real, table_real) - contract(
-        einsum_form, data_imaginary, table_imaginary
-    )
-    imaginary_out = contract(einsum_form, data_real, table_imaginary) + contract(
-        einsum_form, data_imaginary, table_real
-    )
-    return (real_out, imaginary_out)
-
-
-def transform(data_real, data_imaginary, direction, along_last):
-    length = data_real.shape[-1] if along_last else data_real.shape[-2]
-    outer_size = 16
-    inner_size = length // outer_size
-    outer_cosine, outer_sine = angle_table(outer_size, outer_size, outer_size, direction)
-    twist_cosine, twist_sine = angle_table(outer_size, inner_size, length, direction)
-    inner_cosine, inner_sine = angle_table(inner_size, inner_size, inner_size, direction)
-    if along_last:
-        split_shape = data_real.shape[:-1] + (outer_size, inner_size)
-        first_form = "...aq,ab->...bq"
-        second_form = "...bq,qc->...cb"
-    else:
-        split_shape = data_real.shape[:-2] + (outer_size, inner_size, data_real.shape[-1])
-        first_form = "...aqt,ab->...bqt"
-        second_form = "...bqt,qc->...cbt"
-        twist_cosine = twist_cosine[:, :, None]
-        twist_sine = twist_sine[:, :, None]
-    part_real = data_real.reshape(split_shape)
-    part_imaginary = None if data_imaginary is None else data_imaginary.reshape(split_shape)
-    section_real, section_imaginary = complex_contract(
-        first_form, part_real, part_imaginary, outer_cosine, outer_sine
-    )
-    turned_real = section_real * twist_cosine - section_imaginary * twist_sine
-    turned_imaginary = section_real * twist_sine + section_imaginary * twist_cosine
-    final_real, final_imaginary = complex_contract(
-        second_form, turned_real, turned_imaginary, inner_cosine, inner_sine
-    )
-    return (final_real.reshape(data_real.shape), final_imaginary.reshape(data_real.shape))
+    return (row_index * column_index % period).astype(jnp.float32) * (2.0 * math.pi / period)
+
+
+def hartley_tables(x_length, groups, group_length):
+    x_angle = angles(x_length, x_length, x_length)
+    group_angle = angles(groups, groups, groups)
+    twist_angle = angles(groups, group_length, groups * group_length)
+    inner_angle = angles(group_length, group_length, group_length)
+    return dict(
+        cas_x=jnp.cos(x_angle) + jnp.sin(x_angle),
+        group_cos=jnp.cos(group_angle),
+        group_sin=jnp.sin(group_angle),
+        twist_cos=jnp.cos(twist_angle)[None, :, None, :],
+        twist_sin=jnp.sin(twist_angle)[None, :, None, :],
+        inner_plus=jnp.cos(inner_angle) + jnp.sin(inner_angle),
+        inner_minus=jnp.cos(inner_angle) - jnp.sin(inner_angle),
+    )
+
+
+def hartley_y(data, tables):
+    first_real = contract("ka,capb->ckpb", tables["group_cos"], data)
+    first_imaginary = -contract("ka,capb->ckpb", tables["group_sin"], data)
+    turned_real = first_real * tables["twist_cos"] + first_imaginary * tables["twist_sin"]
+    turned_imaginary = first_imaginary * tables["twist_cos"] - first_real * tables["twist_sin"]
+    return contract("ckpb,bq->ckpq", turned_real, tables["inner_plus"]) - contract(
+        "ckpb,bq->ckpq", turned_imaginary, tables["inner_minus"]
+    )
+
+
+def hartley_y_transposed(data, tables):
+    turned_real = contract("ckpq,bq->ckpb", data, tables["inner_plus"])
+    turned_imaginary = -contract("ckpq,bq->ckpb", data, tables["inner_minus"])
+    first_real = turned_real * tables["twist_cos"] - turned_imaginary * tables["twist_sin"]
+    first_imaginary = turned_real * tables["twist_sin"] + turned_imaginary * tables["twist_cos"]
+    return contract("ka,ckpb->capb", tables["group_cos"], first_real) - contract(
+        "ka,ckpb->capb", tables["group_sin"], first_imaginary
+    )
 
 
 def convolve(source, interaction, primitive_tile_total):
+    kx_devices = lax.axis_size("kx")
+    ky_devices = lax.axis_size("ky")
     along_kx = lax.all_to_all(source, "kx", split_axis=0, concat_axis=1, tiled=True)
-    broad_nonimaginary, wide_imaginary = transform(along_kx, None, -1.0, False)
-    joined = jnp.stack([broad_nonimaginary, wide_imaginary])
-    along_ky = lax.all_to_all(joined, "ky", split_axis=2, concat_axis=3, tiled=True)
-    line_real, line_imaginary = transform(along_ky[0], along_ky[1], -1.0, True)
-    line_real, line_imaginary = transform(
-        line_real * interaction, line_imaginary * interaction, 1.0, True
-    )
-    returned = lax.all_to_all(
-        jnp.stack([line_real, line_imaginary]), "ky", split_axis=3, concat_axis=2, tiled=True
-    )
-    final_real, final_imaginary = transform(returned[0], returned[1], 1.0, False)
-    normalizer = 1.0 / primitive_tile_total
-    return lax.all_to_all(final_real * normalizer, "kx", split_axis=1, concat_axis=0, tiled=True)
+    components, x_length, column_count = along_kx.shape
+    row_count = x_length // ky_devices
+    tables = hartley_tables(x_length, ky_devices, column_count)
+    rows_x = contract("px,cxy->cpy", tables["cas_x"], along_kx)
+    split = rows_x.reshape(components, ky_devices, row_count, column_count)
+    along_ky = lax.all_to_all(split, "ky", split_axis=1, concat_axis=1, tiled=True)
+    spectrum = hartley_y(along_ky, tables)
+    weight = interaction.reshape(row_count, column_count, ky_devices).transpose(2, 0, 1)
+    weighted = spectrum * (weight * (1.0 / primitive_tile_total))[None]
+    back_y = hartley_y_transposed(weighted, tables)
+    returned = lax.all_to_all(back_y, "ky", split_axis=1, concat_axis=1, tiled=True)
+    returned = returned.reshape(components, x_length, column_count)
+    final = contract("px,cpy->cxy", tables["cas_x"], returned)
+    final = final.reshape(components, kx_devices, x_length // kx_devices, column_count)
+    back = lax.all_to_all(final, "kx", split_axis=1, concat_axis=0, tiled=True)
+    return back.reshape(components * kx_devices, x_length // kx_devices, column_count)
+
+
+def group_sum(values, axis):
+    devices = lax.axis_size(axis)
+    spread = jnp.broadcast_to(values[None], (devices,) + values.shape)
+    gathered = lax.all_to_all(spread, axis, split_axis=0, concat_axis=0, tiled=True)
+    return jnp.sum(gathered, axis=0)
 
 
 def collect_moments(local_sums, primitive_tile_total):
-    return lax.psum(local_sums, ("kx", "ky")) / primitive_tile_total
+    return group_sum(group_sum(local_sums, "ky"), "kx") / primitive_tile_total
+
+
+def neighbours(array, axis, dim, width):
+    devices, length = (lax.axis_size(axis), array.shape[dim])
+    up = [(i, (i + 1) % devices) for i in range(devices)]
+    down = [(j, i) for i, j in up]
+    last = lax.slice_in_dim(array, length - width, length, axis=dim)
+    initial = lax.slice_in_dim(array, 0, width, axis=dim)
+    before = lax.ppermute(last, axis, up)
+    after = lax.ppermute(initial, axis, down)
+    return jnp.concatenate([before, array, after], axis=dim)
 
 
 def body(packed_state_matrix, energies, dipole_x, dipole_y, interaction, driving_field):
@@ -201,9 +201,8 @@
     columns_local = packed_state_matrix.shape[2]
     primitive_tile_total = rows_local * columns_local * lax.axis_size("kx") * lax.axis_size("ky")
     stacked = jnp.concatenate([packed_state_matrix, energies])
-    padded = with_halo(stacked, (("kx", 1), ("ky", 2)), 2)
-    column_core = padded[:, :, 2:-2]
-    row_core = padded[:, 2:-2, :]
+    column_core = neighbours(stacked, "kx", 1, 2)
+    row_core = neighbours(stacked, "ky", 2, 2)
     gradient_x = (
         8.0 * (column_core[:, 3:-1] - column_core[:, 1:-3])
         - (column_core[:, 4:] - column_core[:, :-4])
@@ -222,9 +221,8 @@
     )
     totals = collect_moments(local_sums, primitive_tile_total)
     shielding_multiplier = 1.0 / (1.0 + SHIELDING_LEVEL * totals[0])
-    self_energy = -convolve(
-        packed_state_matrix * shielding_multiplier, interaction, primitive_tile_total
-    )
+    convolved = convolve(packed_state_matrix, interaction, primitive_tile_total)
+    self_energy = -shielding_multiplier * convolved
     section_slope = slope_terms(
         packed_state_matrix,
         energies,

time: 356 us -> 158 us (0.44); the launches traced: 350 us -> 158 us
  blocking collectives: 110 us -> 0 us
  local copies, waits for them, and re-layouts: 49.8 us -> 6.19 us
  waiting for transfers between devices: 83 us -> 57.6 us
  other arithmetic: 31 us -> 8.76 us
  starting transfers between devices: 48.9 us -> 66.7 us
  matrix products: 25.5 us -> 17.3 us
    psum x1 -> x0, blocking collectives: 110 us -> none  [collect_moments(): return lax.psum(local_sums, ('kx', 'ky')) / primitive_tile_total]
    unnamed x30 -> x13, local copies, waits for them, and re-layouts: 19.4 us -> 1.82 us
    all_to_all x3 -> x5, starting transfers between devices: 21.5 us -> 38.7 us  [the longest x2 18.9 us: group_sum(): lax.all_to_all(spread, axis, split_axis=0, concat_axis=0, tiled=True)]
    unnamed x16 -> x15, other arithmetic: 17.1 us -> 0.48 us
    all_to_all x3 -> x5, waiting for transfers between devices: 65.7 us -> 51.5 us  [the longest x1 20.3 us: convolve(): lax.all_to_all(back_y, 'ky', split_axis=1, concat_axis=1, tiled=True)]
    another operation x6 -> x0, local copies, waits for them, and re-layouts: 11.4 us -> none  [the longest x3 9.92 us: convolve(): jnp.stack([line_real, line_imaginary])]
    dot_general x28 -> x10, matrix products: 25.5 us -> 17.3 us  [contract(): jnp.einsum(einsum_form, left, right, precision=lax.Precision.HIGHEST, pre...]
    all_to_all x2 -> x0, local copies, waits for them, and re-layouts: 8.17 us -> none  [the longest x1 8.14 us: convolve(): lax.all_to_all(jnp.stack([line_real, line_imaginary]), 'ky', split_axis=3...]
  transfers between devices with their start and end apart: 8 -> 10, of which waited for: 6 -> 5; matrix products, arithmetic and copies ran while one was open for 1% -> 12% of each run, Pallas kernels for 0% -> 0%
where the time goes in v1:
time: 158 us
  starting transfers between devices  66.7 us (42%)
  waiting for transfers between devices  57.6 us (36%)
  matrix products  17.3 us (11%)
  other arithmetic  8.76 us (6%)
  local copies, waits for them, and re-layouts  6.19 us (4%)
    all_to_all x1, waiting for transfers between devices, convolve(): lax.all_to_all(back_y, 'ky', split_axis=1, concat_axis=1, tiled=True)  20.3 us
    all_to_all x2, starting transfers between devices, group_sum(): lax.all_to_all(spread, axis, split_axis=0, concat_axis=0, tiled=True)  18.9 us
    all_to_all x1, waiting for transfers between devices, convolve(): lax.all_to_all(split, 'ky', split_axis=1, concat_axis=1, tiled=True)  18.4 us
    dot_general x10, matrix products, contract(): jnp.einsum(einsum_form, left, right, precision=lax.Precision.HIGHEST, pre...  17.3 us
    ppermute x2, starting transfers between devices, neighbours(): after = lax.ppermute(initial, axis, down)  12.3 us
    all_to_all x1, starting transfers between devices, convolve(): lax.all_to_all(source, 'kx', split_axis=0, concat_axis=1, tiled=True)  10.3 us
    all_to_all x1, starting transfers between devices, convolve(): lax.all_to_all(split, 'ky', split_axis=1, concat_axis=1, tiled=True)  7.9 us
    all_to_all x1, waiting for transfers between devices, convolve(): back = lax.all_to_all(final, 'kx', split_axis=1, concat_axis=0, tiled=True)  6.5 us
  transfers between devices with their start and end apart: 10, of which 5 were waited for; matrix products, arithmetic and copies ran while one was open for 12% of the time, Pallas kernels for 0%

profile of v1, /device:TPU:1, one launch (start us, length us, event | category | flops | bytes accessed | tf_op | source)
XLA Modules:
  0.0 157.6 jit_solution(2784811431793207097)
XLA Ops:
  0.6 10.3 %all-to-all-start.2 = ((f32[16,32,128]{2,1,0:T(8,128)}), f32[16,32,128]{2,1,0:T(8,128)S(1)}, u32[]{:S(2)}, u32[]{:S(2)}) async-start(f32[16,32,128]{2,1,0:T(8,128)} %param.6), calls=%async_computation.2 | async-start | bytes 524288 | tf_op jit(solution)/shard_map/all_to_all | solution.py:158
  11.0 0.8 copy-done.1
  12.0 10.0 %collective-permute-start.2 = (f32[20,32,2]{2,1,0:T(8,128)S(1)}, f32[20,32,2]{2,1,0:T(8,128)S(1)}, u32[]{:S(2)}, u32[]{:S(2)}) collective-permute-start(f32[20,32,2]{2,1,0:T(8,128)S(1)} %get-tuple-element.12), channel_id=1, source_target_pairs={{1,0},{2,1},{3,2},{4,3},{5,4},{6,5},{7,6},{8,7},{9,8},{10,9},{11,1... | collective-permute-start | bytes 15368 | tf_op jit(solution)/shard_map/ppermute | solution.py:195
  22.0 1.9 %collective-permute-start.3 = (f32[20,32,2]{2,1,0:T(8,128)S(1)}, f32[20,32,2]{2,1,0:T(8,128)S(1)}, u32[]{:S(2)}, u32[]{:S(2)}) collective-permute-start(f32[20,32,2]{2,1,0:T(8,128)S(1)} %get-tuple-element.13), channel_id=1, source_target_pairs={{0,1},{1,2},{2,3},{3,4},{4,5},{5,6},{6,7},{7,8},{8,9},{9,10},{10,1... | collective-permute-start | bytes 15368 | tf_op jit(solution)/shard_map/ppermute | solution.py:194
  24.0 2.3 %collective-permute-start = (f32[20,2,128]{2,1,0:T(2,128)S(1)}, f32[20,2,128]{2,1,0:T(2,128)S(1)}, u32[]{:S(2)}, u32[]{:S(2)}) collective-permute-start(f32[20,2,128]{2,1,0:T(2,128)S(1)} %get-tuple-element.10), channel_id=1, source_target_pairs={{32,0},{64,32},{96,64},{128,96},{160,128},{192,160},{224,192},{256... | collective-permute-start | bytes 61448 | tf_op jit(solution)/shard_map/ppermute | solution.py:195
  26.3 3.4 %collective-permute-start.1 = (f32[20,2,128]{2,1,0:T(2,128)S(1)}, f32[20,2,128]{2,1,0:T(2,128)S(1)}, u32[]{:S(2)}, u32[]{:S(2)}) collective-permute-start(f32[20,2,128]{2,1,0:T(2,128)S(1)} %get-tuple-element.11), channel_id=1, source_target_pairs={{0,32},{32,64},{64,96},{96,128},{128,160},{160,192},{192,224},{224... | collective-permute-start | bytes 61448 | tf_op jit(solution)/shard_map/ppermute | solution.py:194
  30.4 6.1 %collective-permute-done.3 = f32[20,32,2]{2,1,0:T(8,128)S(1)} collective-permute-done((f32[20,32,2]{2,1,0:T(8,128)S(1)}, f32[20,32,2]{2,1,0:T(8,128)S(1)}, u32[]{:S(2)}, u32[]{:S(2)}) %collective-permute-start.3) | collective-permute-done | bytes 5152 | tf_op jit(solution)/shard_map/ppermute | solution.py:194
  37.9 2.0 %pad_maximum_fusion.5 = f32[3]{0:T(128)S(1)} fusion(f32[1]{0:T(128)} %bitcast.2, f32[1]{0:T(128)} %bitcast.1, f32[1]{0:T(128)} %bitcast), kind=kLoop, calls=%fused_computation.144 | loop fusion | flops 6 | bytes 24 | tf_op jit(solution)/shard_map/stack | solution.py:215
  40.5 10.6 %all-to-all-start = ((f32[32,1,3]{2,1,0:T(1,128)}), f32[32,1,3]{2,1,0:T(1,128)S(1)}, u32[]{:S(2)}, u32[]{:S(2)}) async-start(f32[32,1,3]{2,1,0:T(1,128)} %broadcast_in_dim.4), calls=%async_computation | async-start | bytes 32768 | tf_op jit(solution)/shard_map/all_to_all | solution.py:180
  51.1 7.3 %fusion.9 = f32[512,128]{1,0:T(8,128)} fusion(f32[512,128]{1,0:T(8,128)S(1)} %bitcast.94), kind=kOutput, calls=%fused_computation.23 | convolution fusion | flops 406585344 | bytes 524288 | tf_op jit(solution)/shard_map/px,cxy->cpy/dot_general | solution.py:108
  58.4 6.3 %all-to-all-done = f32[32,1,3]{2,1,0:T(1,128)S(1)} async-done(((f32[32,1,3]{2,1,0:T(1,128)}), f32[32,1,3]{2,1,0:T(1,128)S(1)}, u32[]{:S(2)}, u32[]{:S(2)}) %all-to-all-start) | async-done | bytes 416 | tf_op jit(solution)/shard_map/all_to_all | solution.py:180
  64.7 7.9 %all-to-all-start.3 = ((f32[1,32,16,128]{3,2,0,1:T(8,128)}), f32[1,32,16,128]{3,2,0,1:T(8,128)S(1)}, u32[]{:S(2)}, u32[]{:S(2)}) async-start(f32[1,32,16,128]{3,2,0,1:T(8,128)} %bitcast.9), calls=%async_computation.3 | async-start | bytes 524288 | tf_op jit(solution)/shard_map/all_to_all | solution.py:164
  73.4 18.4 %all-to-all-done.3 = f32[1,32,16,128]{3,2,0,1:T(8,128)S(1)} async-done(((f32[1,32,16,128]{3,2,0,1:T(8,128)}), f32[1,32,16,128]{3,2,0,1:T(8,128)S(1)}, u32[]{:S(2)}, u32[]{:S(2)}) %all-to-all-start.3) | async-done | bytes 262176 | tf_op jit(solution)/shard_map/all_to_all | solution.py:164
  92.4 8.3 %all-to-all-start.1 = ((f32[16,1,3]{2,1,0:T(1,128)}), f32[16,1,3]{2,1,0:T(1,128)S(1)}, u32[]{:S(2)}, u32[]{:S(2)}) async-start(f32[16,1,3]{2,1,0:T(1,128)} %broadcast_in_dim.5), calls=%async_computation.1 | async-start | bytes 16384 | tf_op jit(solution)/shard_map/all_to_all | solution.py:180
  105.5 0.9 copy.78
  106.3 5.4 %all-to-all-start.4 = ((f32[1,32,16,128]{3,2,0,1:T(8,128)}), f32[1,32,16,128]{3,2,0,1:T(8,128)S(1)}, u32[]{:S(2)}, u32[]{:S(2)}) async-start(f32[1,32,16,128]{3,2,0,1:T(8,128)} %copy.78), calls=%async_computation.4 | async-start | bytes 524288 | tf_op jit(solution)/shard_map/all_to_all | solution.py:169
  112.4 20.3 %all-to-all-done.4 = f32[1,32,16,128]{3,2,0,1:T(8,128)S(1)} async-done(((f32[1,32,16,128]{3,2,0,1:T(8,128)}), f32[1,32,16,128]{3,2,0,1:T(8,128)S(1)}, u32[]{:S(2)}, u32[]{:S(2)}) %all-to-all-start.4) | async-done | bytes 262176 | tf_op jit(solution)/shard_map/all_to_all | solution.py:169
  132.8 5.3 %convolution_bitcast_fusion = f32[1,512,128]{1,2,0:T(8,128)S(1)} fusion(f32[512,128]{1,0:T(8,128)S(1)} %bitcast.95), kind=kOutput, calls=%fused_computation.7 | convolution fusion | flops 406585344 | bytes 524288 | tf_op jit(solution)/shard_map/px,cpy->cxy/dot_general | solution.py:108
  138.1 0.8 copy.79
  138.9 6.4 %all-to-all-start.5 = ((f32[1,16,32,128]{3,2,0,1:T(8,128)}), f32[1,16,32,128]{3,2,0,1:T(8,128)S(1)}, u32[]{:S(2)}, u32[]{:S(2)}) async-start(f32[1,16,32,128]{3,2,0,1:T(8,128)} %bitcast.32), calls=%async_computation.5 | async-start | bytes 524288 | tf_op jit(solution)/shard_map/all_to_all | solution.py:173
  146.0 6.5 %all-to-all-done.5 = f32[1,16,32,128]{3,2,0,1:T(8,128)S(1)} async-done(((f32[1,16,32,128]{3,2,0,1:T(8,128)}), f32[1,16,32,128]{3,2,0,1:T(8,128)S(1)}, u32[]{:S(2)}, u32[]{:S(2)}) %all-to-all-start.5) | async-done | bytes 262176 | tf_op jit(solution)/shard_map/all_to_all | solution.py:173
  152.6 0.9 copy-done.3
  153.6 1.3 fusion.37
  155.5 1.3 fusion.24
  (63 shorter events, 11.7 us)
Async XLA Ops:
  0.6 10.4 %copy-start = (f32[16,32,128]{2,1,0:T(8,128)S(1)}, f32[16,32,128]{2,1,0:T(8,128)}, u32[]{:S(2)}) copy-start(f32[16,32,128]{2,1,0:T(8,128)} %param.6) | copy-start | bytes 786436
  0.6 39.2 %all-to-all-start.2 = ((f32[16,32,128]{2,1,0:T(8,128)}), f32[16,32,128]{2,1,0:T(8,128)S(1)}, u32[]{:S(2)}, u32[]{:S(2)}) async-start(f32[16,32,128]{2,1,0:T(8,128)} %param.6), calls=%async_computation.2 | async-start | bytes 524288 | tf_op jit(solution)/shard_map/all_to_all | solution.py:158
  11.0 0.8 copy-start.1
  12.0 18.4 %collective-permute-start.2 = (f32[20,32,2]{2,1,0:T(8,128)S(1)}, f32[20,32,2]{2,1,0:T(8,128)S(1)}, u32[]{:S(2)}, u32[]{:S(2)}) collective-permute-start(f32[20,32,2]{2,1,0:T(8,128)S(1)} %get-tuple-element.12), channel_id=1, source_target_pairs={{1,0},{2,1},{3,2},{4,3},{5,4},{6,5},{7,6},{8,7},{9,8},{10,9},{11,1... | collective-permute-start | bytes 15368 | tf_op jit(solution)/shard_map/ppermute | solution.py:195
  22.0 14.4 %collective-permute-start.3 = (f32[20,32,2]{2,1,0:T(8,128)S(1)}, f32[20,32,2]{2,1,0:T(8,128)S(1)}, u32[]{:S(2)}, u32[]{:S(2)}) collective-permute-start(f32[20,32,2]{2,1,0:T(8,128)S(1)} %get-tuple-element.13), channel_id=1, source_target_pairs={{0,1},{1,2},{2,3},{3,4},{4,5},{5,6},{6,7},{7,8},{8,9},{9,10},{10,1... | collective-permute-start | bytes 15368 | tf_op jit(solution)/shard_map/ppermute | solution.py:194
  24.0 12.5 %collective-permute-start = (f32[20,2,128]{2,1,0:T(2,128)S(1)}, f32[20,2,128]{2,1,0:T(2,128)S(1)}, u32[]{:S(2)}, u32[]{:S(2)}) collective-permute-start(f32[20,2,128]{2,1,0:T(2,128)S(1)} %get-tuple-element.10), channel_id=1, source_target_pairs={{32,0},{64,32},{96,64},{128,96},{160,128},{192,160},{224,192},{256... | collective-permute-start | bytes 61448 | tf_op jit(solution)/shard_map/ppermute | solution.py:195
  26.3 10.2 %collective-permute-start.1 = (f32[20,2,128]{2,1,0:T(2,128)S(1)}, f32[20,2,128]{2,1,0:T(2,128)S(1)}, u32[]{:S(2)}, u32[]{:S(2)}) collective-permute-start(f32[20,2,128]{2,1,0:T(2,128)S(1)} %get-tuple-element.11), channel_id=1, source_target_pairs={{0,32},{32,64},{64,96},{96,128},{128,160},{160,192},{192,224},{224... | collective-permute-start | bytes 61448 | tf_op jit(solution)/shard_map/ppermute | solution.py:194
  40.5 24.2 %all-to-all-start = ((f32[32,1,3]{2,1,0:T(1,128)}), f32[32,1,3]{2,1,0:T(1,128)S(1)}, u32[]{:S(2)}, u32[]{:S(2)}) async-start(f32[32,1,3]{2,1,0:T(1,128)} %broadcast_in_dim.4), calls=%async_computation | async-start | bytes 32768 | tf_op jit(solution)/shard_map/all_to_all | solution.py:180
  64.7 7.9 %copy-start.2 = (f32[16,4096]{1,0:T(8,128)S(1)}, f32[16,4096]{1,0:T(8,128)}, u32[]{:S(2)}) copy-start(f32[16,4096]{1,0:T(8,128)} %param.10) | copy-start | bytes 786436
  64.7 27.1 %all-to-all-start.3 = ((f32[1,32,16,128]{3,2,0,1:T(8,128)}), f32[1,32,16,128]{3,2,0,1:T(8,128)S(1)}, u32[]{:S(2)}, u32[]{:S(2)}) async-start(f32[1,32,16,128]{3,2,0,1:T(8,128)} %bitcast.9), calls=%async_computation.3 | async-start | bytes 524288 | tf_op jit(solution)/shard_map/all_to_all | solution.py:164
  92.4 13.9 %all-to-all-start.1 = ((f32[16,1,3]{2,1,0:T(1,128)}), f32[16,1,3]{2,1,0:T(1,128)S(1)}, u32[]{:S(2)}, u32[]{:S(2)}) async-start(f32[16,1,3]{2,1,0:T(1,128)} %broadcast_in_dim.5), calls=%async_computation.1 | async-start | bytes 16384 | tf_op jit(solution)/shard_map/all_to_all | solution.py:180
  106.3 5.4 %copy-start.5 = (f32[2]{0:T(128)S(1)}, f32[2]{0:T(128)}, u32[]{:S(2)}) copy-start(f32[2]{0:T(128)} %param.11) | copy-start | bytes 28
  106.3 26.4 %all-to-all-start.4 = ((f32[1,32,16,128]{3,2,0,1:T(8,128)}), f32[1,32,16,128]{3,2,0,1:T(8,128)S(1)}, u32[]{:S(2)}, u32[]{:S(2)}) async-start(f32[1,32,16,128]{3,2,0,1:T(8,128)} %copy.78), calls=%async_computation.4 | async-start | bytes 524288 | tf_op jit(solution)/shard_map/all_to_all | solution.py:169
  138.9 13.6 %all-to-all-start.5 = ((f32[1,16,32,128]{3,2,0,1:T(8,128)}), f32[1,16,32,128]{3,2,0,1:T(8,128)S(1)}, u32[]{:S(2)}, u32[]{:S(2)}) async-start(f32[1,16,32,128]{3,2,0,1:T(8,128)} %bitcast.32), calls=%async_computation.5 | async-start | bytes 524288 | tf_op jit(solution)/shard_map/all_to_all | solution.py:173
  152.6 0.9 copy-start.3
  152.6 1.0 copy-start.4

commit v2 on v1

--- a/solution.py
+++ b/solution.py
@@ -1,6 +1,7 @@
 import math
 
 import jax
+import numpy as np
 import jax.numpy as jnp
 from jax import lax
 from jax.sharding import PartitionSpec as P
@@ -111,9 +112,13 @@
 
 
 def angles(row_count, column_count, period):
-    row_index = lax.broadcasted_iota(jnp.int32, (row_count, column_count), 0)
-    column_index = lax.broadcasted_iota(jnp.int32, (row_count, column_count), 1)
-    return (row_index * column_index % period).astype(jnp.float32) * (2.0 * math.pi / period)
+    row_index = np.arange(row_count, dtype=np.int64)[:, None]
+    column_index = np.arange(column_count, dtype=np.int64)[None, :]
+    return (row_index * column_index % period).astype(np.float64) * (2.0 * math.pi / period)
+
+
+def table(values):
+    return jnp.asarray(values.astype(np.float32))
 
 
 def hartley_tables(x_length, groups, group_length):
@@ -122,13 +127,13 @@
     twist_angle = angles(groups, group_length, groups * group_length)
     inner_angle = angles(group_length, group_length, group_length)
     return dict(
-        cas_x=jnp.cos(x_angle) + jnp.sin(x_angle),
-        group_cos=jnp.cos(group_angle),
-        group_sin=jnp.sin(group_angle),
-        twist_cos=jnp.cos(twist_angle)[None, :, None, :],
-        twist_sin=jnp.sin(twist_angle)[None, :, None, :],
-        inner_plus=jnp.cos(inner_angle) + jnp.sin(inner_angle),
-        inner_minus=jnp.cos(inner_angle) - jnp.sin(inner_angle),
+        cas_x=table(np.cos(x_angle) + np.sin(x_angle)),
+        group_cos=table(np.cos(group_angle)),
+        group_sin=table(np.sin(group_angle)),
+        twist_cos=table(np.cos(twist_angle)[None, :, None, :]),
+        twist_sin=table(np.sin(twist_angle)[None, :, None, :]),
+        inner_plus=table(np.cos(inner_angle) + np.sin(inner_angle)),
+        inner_minus=table(np.cos(inner_angle) - np.sin(inner_angle)),
     )
 
 
@@ -191,8 +196,9 @@
     down = [(j, i) for i, j in up]
     last = lax.slice_in_dim(array, length - width, length, axis=dim)
     initial = lax.slice_in_dim(array, 0, width, axis=dim)
-    before = lax.ppermute(last, axis, up)
-    after = lax.ppermute(initial, axis, down)
+    dense = (-1, 128) if last.size % 128 == 0 else last.shape
+    before = lax.ppermute(last.reshape(dense), axis, up).reshape(last.shape)
+    after = lax.ppermute(initial.reshape(dense), axis, down).reshape(initial.shape)
     return jnp.concatenate([before, array, after], axis=dim)
 
 

time: 158 us -> 147 us (0.930)
  matrix products: 17.3 us -> 5.98 us
  waiting for transfers between devices: 57.6 us -> 54.3 us
  local copies, waits for them, and re-layouts: 6.19 us -> 8.94 us
    dot_general x10, matrix products: 17.3 us -> 5.98 us  [contract(): jnp.einsum(einsum_form, left, right, precision=lax.Precision.HIGHEST, pre...]
    ppermute x4, waiting for transfers between devices: 6.1 us -> 0.01 us  [the longest x2 0.01 us: neighbours(): lax.ppermute(initial.reshape(dense), axis, down).reshape(initial.shape)]
    all_to_all x2, waiting for transfers between devices: 6.26 us -> 12 us  [group_sum(): lax.all_to_all(spread, axis, split_axis=0, concat_axis=0, tiled=True)]
    all_to_all x1, starting transfers between devices: 7.9 us -> 4 us  [convolve(): lax.all_to_all(split, 'ky', split_axis=1, concat_axis=1, tiled=True)]
    all_to_all x2, starting transfers between devices: 18.9 us -> 22.6 us  [group_sum(): lax.all_to_all(spread, axis, split_axis=0, concat_axis=0, tiled=True)]
    all_to_all x1, waiting for transfers between devices: 18.4 us -> 16.1 us  [convolve(): lax.all_to_all(split, 'ky', split_axis=1, concat_axis=1, tiled=True)]
    unnamed x13 -> x29, local copies, waits for them, and re-layouts: 1.82 us -> 3.63 us
  transfers between devices with their start and end apart: 10 -> 10, of which waited for: 5 -> 5; matrix products, arithmetic and copies ran while one was open for 12% -> 10% of each run, Pallas kernels for 0% -> 0%
where the time goes in v2:
time: 147 us; the launch traced here: 146 us
  starting transfers between devices  65.9 us (45%)
  waiting for transfers between devices  54.3 us (37%)
  other arithmetic  9.33 us (6%)
  local copies, waits for them, and re-layouts  8.94 us (6%)
  matrix products  5.98 us (4%)
    all_to_all x2, starting transfers between devices, group_sum(): lax.all_to_all(spread, axis, split_axis=0, concat_axis=0, tiled=True)  22.6 us
    all_to_all x1, waiting for transfers between devices, convolve(): lax.all_to_all(back_y, 'ky', split_axis=1, concat_axis=1, tiled=True)  19.7 us
    all_to_all x1, waiting for transfers between devices, convolve(): lax.all_to_all(split, 'ky', split_axis=1, concat_axis=1, tiled=True)  16.1 us
    all_to_all x2, waiting for transfers between devices, group_sum(): lax.all_to_all(spread, axis, split_axis=0, concat_axis=0, tiled=True)  12 us
    ppermute x2, starting transfers between devices, neighbours(): lax.ppermute(initial.reshape(dense), axis, down).reshape(initial.shape)  11.9 us
    all_to_all x1, starting transfers between devices, convolve(): lax.all_to_all(source, 'kx', split_axis=0, concat_axis=1, tiled=True)  10.3 us
    all_to_all x1, starting transfers between devices, convolve(): back = lax.all_to_all(final, 'kx', split_axis=1, concat_axis=0, tiled=True)  6.58 us
    all_to_all x1, waiting for transfers between devices, convolve(): back = lax.all_to_all(final, 'kx', split_axis=1, concat_axis=0, tiled=True)  6.5 us
  transfers between devices with their start and end apart: 10, of which 5 were waited for; matrix products, arithmetic and copies ran while one was open for 10% of the time, Pallas kernels for 0%

profile of v2, /device:TPU:1, one launch (start us, length us, event | category | flops | bytes accessed | tf_op | source)
XLA Modules:
  0.0 145.5 jit_solution(8562063476738795404)
XLA Ops:
  0.6 10.3 %all-to-all-start.2 = ((f32[16,32,128]{2,1,0:T(8,128)}), f32[16,32,128]{2,1,0:T(8,128)S(1)}, u32[]{:S(2)}, u32[]{:S(2)}) async-start(f32[16,32,128]{2,1,0:T(8,128)} %param.13), calls=%async_computation.2 | async-start | bytes 524288 | tf_op jit(solution)/shard_map/all_to_all | solution.py:163
  11.0 0.8 copy-done.4
  11.9 3.5 %collective-permute-start.1 = (f32[40,128]{1,0:T(8,128)S(1)}, f32[40,128]{1,0:T(8,128)S(1)}, u32[]{:S(2)}, u32[]{:S(2)}) collective-permute-start(f32[40,128]{1,0:T(8,128)S(1)} %bitcast.91), channel_id=1, source_target_pairs={{0,32},{32,64},{64,96},{96,128},{128,160},{160,192},{192,224},{224... | collective-permute-start | bytes 61448 | tf_op jit(solution)/shard_map/ppermute | solution.py:200
  15.4 1.9 %collective-permute-start = (f32[40,128]{1,0:T(8,128)S(1)}, f32[40,128]{1,0:T(8,128)S(1)}, u32[]{:S(2)}, u32[]{:S(2)}) collective-permute-start(f32[40,128]{1,0:T(8,128)S(1)} %bitcast.90), channel_id=1, source_target_pairs={{32,0},{64,32},{96,64},{128,96},{160,128},{192,160},{224,192},{256... | collective-permute-start | bytes 61448 | tf_op jit(solution)/shard_map/ppermute | solution.py:201
  17.7 1.9 %collective-permute-start.3 = (f32[10,128]{1,0:T(8,128)S(1)}, f32[10,128]{1,0:T(8,128)S(1)}, u32[]{:S(2)}, u32[]{:S(2)}) collective-permute-start(f32[10,128]{1,0:T(8,128)S(1)} %reshape.127), channel_id=1, source_target_pairs={{0,1},{1,2},{2,3},{3,4},{4,5},{5,6},{6,7},{7,8},{8,9},{9,10},{10,1... | collective-permute-start | bytes 15368 | tf_op jit(solution)/shard_map/ppermute | solution.py:200
  19.8 10.0 %collective-permute-start.2 = (f32[10,128]{1,0:T(8,128)S(1)}, f32[10,128]{1,0:T(8,128)S(1)}, u32[]{:S(2)}, u32[]{:S(2)}) collective-permute-start(f32[10,128]{1,0:T(8,128)S(1)} %reshape.125), channel_id=1, source_target_pairs={{1,0},{2,1},{3,2},{4,3},{5,4},{6,5},{7,6},{8,7},{9,8},{10,9},{11,1... | collective-permute-start | bytes 15368 | tf_op jit(solution)/shard_map/ppermute | solution.py:201
  31.1 0.8 fusion.7
  32.5 2.0 %pad_maximum_fusion.5 = f32[3]{0:T(128)S(1)} fusion(f32[1]{0:T(128)} %bitcast.6, f32[1]{0:T(128)} %bitcast.5, f32[1]{0:T(128)} %bitcast), kind=kLoop, calls=%fused_computation.89 | loop fusion | flops 6 | bytes 24 | tf_op jit(solution)/shard_map/stack | solution.py:221
  35.1 11.7 %all-to-all-start = ((f32[32,1,3]{2,1,0:T(1,128)}), f32[32,1,3]{2,1,0:T(1,128)S(1)}, u32[]{:S(2)}, u32[]{:S(2)}) async-start(f32[32,1,3]{2,1,0:T(1,128)} %broadcast_in_dim.4), calls=%async_computation | async-start | bytes 32768 | tf_op jit(solution)/shard_map/all_to_all | solution.py:185
  46.8 1.7 %fusion.39 = f32[512,128]{1,0:T(8,128)} fusion(f32[512,512]{1,0:T(8,128)S(1)} %copy-done.1, f32[512,128]{1,0:T(8,128)S(1)} %bitcast.88), kind=kOutput, calls=%fused_computation.95 | convolution fusion | flops 402653184 | bytes 1572864 | tf_op jit(solution)/shard_map/px,cxy->cpy/dot_general | solution.py:109
  48.5 11.9 %all-to-all-done = f32[32,1,3]{2,1,0:T(1,128)S(1)} async-done(((f32[32,1,3]{2,1,0:T(1,128)}), f32[32,1,3]{2,1,0:T(1,128)S(1)}, u32[]{:S(2)}, u32[]{:S(2)}) %all-to-all-start) | async-done | bytes 416 | tf_op jit(solution)/shard_map/all_to_all | solution.py:185
  60.3 4.0 %all-to-all-start.3 = ((f32[1,32,16,128]{3,2,0,1:T(8,128)}), f32[1,32,16,128]{3,2,0,1:T(8,128)S(1)}, u32[]{:S(2)}, u32[]{:S(2)}) async-start(f32[1,32,16,128]{3,2,0,1:T(8,128)} %bitcast.13), calls=%async_computation.3 | async-start | bytes 524288 | tf_op jit(solution)/shard_map/all_to_all | solution.py:169
  65.1 16.1 %all-to-all-done.3 = f32[1,32,16,128]{3,2,0,1:T(8,128)S(1)} async-done(((f32[1,32,16,128]{3,2,0,1:T(8,128)}), f32[1,32,16,128]{3,2,0,1:T(8,128)S(1)}, u32[]{:S(2)}, u32[]{:S(2)}) %all-to-all-start.3) | async-done | bytes 262176 | tf_op jit(solution)/shard_map/all_to_all | solution.py:169
  81.8 10.9 %all-to-all-start.1 = ((f32[16,1,3]{2,1,0:T(1,128)}), f32[16,1,3]{2,1,0:T(1,128)}, u32[]{:S(2)}, u32[]{:S(2)}) async-start(f32[16,1,3]{2,1,0:T(1,128)} %broadcast_in_dim.5), calls=%async_computation.1 | async-start | bytes 16384 | tf_op jit(solution)/shard_map/all_to_all | solution.py:185
  97.3 0.9 copy.85
  98.3 5.0 %all-to-all-start.4 = ((f32[1,32,16,128]{3,2,0,1:T(8,128)}), f32[1,32,16,128]{3,2,0,1:T(8,128)S(1)}, u32[]{:S(2)}, u32[]{:S(2)}) async-start(f32[1,32,16,128]{3,2,0,1:T(8,128)} %copy.85), calls=%async_computation.4 | async-start | bytes 524288 | tf_op jit(solution)/shard_map/all_to_all | solution.py:174
  104.7 19.7 %all-to-all-done.4 = f32[1,32,16,128]{3,2,0,1:T(8,128)S(1)} async-done(((f32[1,32,16,128]{3,2,0,1:T(8,128)}), f32[1,32,16,128]{3,2,0,1:T(8,128)S(1)}, u32[]{:S(2)}, u32[]{:S(2)}) %all-to-all-start.4) | async-done | bytes 262176 | tf_op jit(solution)/shard_map/all_to_all | solution.py:174
  125.1 0.8 copy.86
  126.0 6.6 %all-to-all-start.5 = ((f32[1,16,32,128]{3,2,0,1:T(8,128)}), f32[1,16,32,128]{3,2,0,1:T(8,128)S(1)}, u32[]{:S(2)}, u32[]{:S(2)}) async-start(f32[1,16,32,128]{3,2,0,1:T(8,128)} %bitcast.36), calls=%async_computation.5 | async-start | bytes 524288 | tf_op jit(solution)/shard_map/all_to_all | solution.py:178
  133.2 6.5 %all-to-all-done.5 = f32[1,16,32,128]{3,2,0,1:T(8,128)S(1)} async-done(((f32[1,16,32,128]{3,2,0,1:T(8,128)}), f32[1,16,32,128]{3,2,0,1:T(8,128)S(1)}, u32[]{:S(2)}, u32[]{:S(2)}) %all-to-all-start.5) | async-done | bytes 262176 | tf_op jit(solution)/shard_map/all_to_all | solution.py:178
  139.7 0.9 copy-done.7
  140.7 1.3 fusion.30
  142.2 0.8 copy-done.5
  143.4 1.3 fusion.17
  (82 shorter events, 13.1 us)
Async XLA Ops:
  0.6 10.4 %copy-start = (f32[16,32,128]{2,1,0:T(8,128)S(1)}, f32[16,32,128]{2,1,0:T(8,128)}, u32[]{:S(2)}) copy-start(f32[16,32,128]{2,1,0:T(8,128)} %param.13) | copy-start | bytes 786436
  0.6 33.8 %all-to-all-start.2 = ((f32[16,32,128]{2,1,0:T(8,128)}), f32[16,32,128]{2,1,0:T(8,128)S(1)}, u32[]{:S(2)}, u32[]{:S(2)}) async-start(f32[16,32,128]{2,1,0:T(8,128)} %param.13), calls=%async_computation.2 | async-start | bytes 524288 | tf_op jit(solution)/shard_map/all_to_all | solution.py:163
  11.0 0.8 copy-start.4
  11.9 19.2 %collective-permute-start.1 = (f32[40,128]{1,0:T(8,128)S(1)}, f32[40,128]{1,0:T(8,128)S(1)}, u32[]{:S(2)}, u32[]{:S(2)}) collective-permute-start(f32[40,128]{1,0:T(8,128)S(1)} %bitcast.91), channel_id=1, source_target_pairs={{0,32},{32,64},{64,96},{96,128},{128,160},{160,192},{192,224},{224... | collective-permute-start | bytes 61448 | tf_op jit(solution)/shard_map/ppermute | solution.py:200
  15.4 15.7 %collective-permute-start = (f32[40,128]{1,0:T(8,128)S(1)}, f32[40,128]{1,0:T(8,128)S(1)}, u32[]{:S(2)}, u32[]{:S(2)}) collective-permute-start(f32[40,128]{1,0:T(8,128)S(1)} %bitcast.90), channel_id=1, source_target_pairs={{32,0},{64,32},{96,64},{128,96},{160,128},{192,160},{224,192},{256... | collective-permute-start | bytes 61448 | tf_op jit(solution)/shard_map/ppermute | solution.py:201
  17.7 12.8 %collective-permute-start.3 = (f32[10,128]{1,0:T(8,128)S(1)}, f32[10,128]{1,0:T(8,128)S(1)}, u32[]{:S(2)}, u32[]{:S(2)}) collective-permute-start(f32[10,128]{1,0:T(8,128)S(1)} %reshape.127), channel_id=1, source_target_pairs={{0,1},{1,2},{2,3},{3,4},{4,5},{5,6},{6,7},{7,8},{8,9},{9,10},{10,1... | collective-permute-start | bytes 15368 | tf_op jit(solution)/shard_map/ppermute | solution.py:200
  19.8 10.9 %collective-permute-start.2 = (f32[10,128]{1,0:T(8,128)S(1)}, f32[10,128]{1,0:T(8,128)S(1)}, u32[]{:S(2)}, u32[]{:S(2)}) collective-permute-start(f32[10,128]{1,0:T(8,128)S(1)} %reshape.125), channel_id=1, source_target_pairs={{1,0},{2,1},{3,2},{4,3},{5,4},{6,5},{7,6},{8,7},{9,8},{10,9},{11,1... | collective-permute-start | bytes 15368 | tf_op jit(solution)/shard_map/ppermute | solution.py:201
  31.1 15.7 %copy-start.1 = (f32[512,512]{1,0:T(8,128)S(1)}, f32[512,512]{1,0:T(8,128)}, u32[]{:S(2)}) copy-start(f32[512,512]{1,0:T(8,128)} %constant.39.clone) | copy-start | bytes 3145732
  35.1 25.2 %all-to-all-start = ((f32[32,1,3]{2,1,0:T(1,128)}), f32[32,1,3]{2,1,0:T(1,128)S(1)}, u32[]{:S(2)}, u32[]{:S(2)}) async-start(f32[32,1,3]{2,1,0:T(1,128)} %broadcast_in_dim.4), calls=%async_computation | async-start | bytes 32768 | tf_op jit(solution)/shard_map/all_to_all | solution.py:185
  60.3 4.0 %copy-start.6 = (f32[16,4096]{1,0:T(8,128)S(1)}, f32[16,4096]{1,0:T(8,128)}, u32[]{:S(2)}) copy-start(f32[16,4096]{1,0:T(8,128)} %param.17) | copy-start | bytes 786436
  60.3 20.9 %all-to-all-start.3 = ((f32[1,32,16,128]{3,2,0,1:T(8,128)}), f32[1,32,16,128]{3,2,0,1:T(8,128)S(1)}, u32[]{:S(2)}, u32[]{:S(2)}) async-start(f32[1,32,16,128]{3,2,0,1:T(8,128)} %bitcast.13), calls=%async_computation.3 | async-start | bytes 524288 | tf_op jit(solution)/shard_map/all_to_all | solution.py:169
  65.1 27.6 %copy-start.12 = (f32[32,32,1]{1,0,2:T(8,128)S(1)}, f32[32,32,1]{1,0,2:T(8,128)}, u32[]{:S(2)}) copy-start(f32[32,32,1]{1,0,2:T(8,128)} %constant.50) | copy-start | bytes 12292
  81.8 16.5 %all-to-all-start.1 = ((f32[16,1,3]{2,1,0:T(1,128)}), f32[16,1,3]{2,1,0:T(1,128)}, u32[]{:S(2)}, u32[]{:S(2)}) async-start(f32[16,1,3]{2,1,0:T(1,128)} %broadcast_in_dim.5), calls=%async_computation.1 | async-start | bytes 16384 | tf_op jit(solution)/shard_map/all_to_all | solution.py:185
  92.7 0.7 copy-start.9
  92.7 0.7 copy-start.10
  92.8 0.7 copy-start.11
  93.5 0.8 copy-start.3
  94.3 0.8 copy-start.2
  98.2 5.1 %copy-start.13 = (f32[2]{0:T(128)S(1)}, f32[2]{0:T(128)}, u32[]{:S(2)}) copy-start(f32[2]{0:T(128)} %param.18) | copy-start | bytes 28
  98.3 26.0 %all-to-all-start.4 = ((f32[1,32,16,128]{3,2,0,1:T(8,128)}), f32[1,32,16,128]{3,2,0,1:T(8,128)S(1)}, u32[]{:S(2)}, u32[]{:S(2)}) async-start(f32[1,32,16,128]{3,2,0,1:T(8,128)} %copy.85), calls=%async_computation.4 | async-start | bytes 524288 | tf_op jit(solution)/shard_map/all_to_all | solution.py:174
  126.0 13.8 %all-to-all-start.5 = ((f32[1,16,32,128]{3,2,0,1:T(8,128)}), f32[1,16,32,128]{3,2,0,1:T(8,128)S(1)}, u32[]{:S(2)}, u32[]{:S(2)}) async-start(f32[1,16,32,128]{3,2,0,1:T(8,128)} %bitcast.36), calls=%async_computation.5 | async-start | bytes 524288 | tf_op jit(solution)/shard_map/all_to_all | solution.py:178
  139.7 0.9 copy-start.7
  139.7 1.0 copy-start.8
  142.2 0.8 copy-start.5

commit v3 on v2

--- a/solution.py
+++ b/solution.py
@@ -157,37 +157,38 @@
     )
 
 
-def convolve(source, interaction, primitive_tile_total):
+def with_sums(data, sums, dim):
+    shape = list(data.shape)
+    shape[dim] = 8
+    tile = jnp.zeros((8, data.shape[-1]), jnp.float32).at[0, 0 : sums.shape[0]].set(sums)
+    return jnp.concatenate([data, jnp.broadcast_to(tile.reshape([1] * (data.ndim - 2) + [8, -1]), shape)], axis=dim)
+
+
+def convolve_and_sum(source, interaction, local_sums, primitive_tile_total):
     kx_devices = lax.axis_size("kx")
     ky_devices = lax.axis_size("ky")
+    sum_count = local_sums.shape[0]
     along_kx = lax.all_to_all(source, "kx", split_axis=0, concat_axis=1, tiled=True)
     components, x_length, column_count = along_kx.shape
     row_count = x_length // ky_devices
     tables = hartley_tables(x_length, ky_devices, column_count)
     rows_x = contract("px,cxy->cpy", tables["cas_x"], along_kx)
-    split = rows_x.reshape(components, ky_devices, row_count, column_count)
+    split = with_sums(rows_x.reshape(components, ky_devices, row_count, column_count), local_sums, 2)
     along_ky = lax.all_to_all(split, "ky", split_axis=1, concat_axis=1, tiled=True)
-    spectrum = hartley_y(along_ky, tables)
+    ky_sums = jnp.sum(along_ky[0, :, row_count, 0:sum_count], axis=0)
+    spectrum = hartley_y(along_ky[:, :, 0:row_count], tables)
     weight = interaction.reshape(row_count, column_count, ky_devices).transpose(2, 0, 1)
     weighted = spectrum * (weight * (1.0 / primitive_tile_total))[None]
     back_y = hartley_y_transposed(weighted, tables)
     returned = lax.all_to_all(back_y, "ky", split_axis=1, concat_axis=1, tiled=True)
     returned = returned.reshape(components, x_length, column_count)
     final = contract("px,cpy->cxy", tables["cas_x"], returned)
-    final = final.reshape(components, kx_devices, x_length // kx_devices, column_count)
+    rows_local = x_length // kx_devices
+    final = with_sums(final.reshape(components, kx_devices, rows_local, column_count), ky_sums, 2)
     back = lax.all_to_all(final, "kx", split_axis=1, concat_axis=0, tiled=True)
-    return back.reshape(components * kx_devices, x_length // kx_devices, column_count)
-
-
-def group_sum(values, axis):
-    devices = lax.axis_size(axis)
-    spread = jnp.broadcast_to(values[None], (devices,) + values.shape)
-    gathered = lax.all_to_all(spread, axis, split_axis=0, concat_axis=0, tiled=True)
-    return jnp.sum(gathered, axis=0)
-
-
-def collect_moments(local_sums, primitive_tile_total):
-    return group_sum(group_sum(local_sums, "ky"), "kx") / primitive_tile_total
+    totals = jnp.sum(back[::components, 0, rows_local, 0:sum_count], axis=0) / primitive_tile_total
+    convolved = back[:, 0, 0:rows_local].reshape(components * kx_devices, rows_local, column_count)
+    return convolved, totals
 
 
 def neighbours(array, axis, dim, width):
@@ -225,9 +226,10 @@
             jnp.sum(gradient_y[16:20] * populations),
         ]
     )
-    totals = collect_moments(local_sums, primitive_tile_total)
+    convolved, totals = convolve_and_sum(
+        packed_state_matrix, interaction, local_sums, primitive_tile_total
+    )
     shielding_multiplier = 1.0 / (1.0 + SHIELDING_LEVEL * totals[0])
-    convolved = convolve(packed_state_matrix, interaction, primitive_tile_total)
     self_energy = -shielding_multiplier * convolved
     section_slope = slope_terms(
         packed_state_matrix,

time: 147 us -> 129 us (0.88)
  waiting for transfers between devices: 54.3 us -> 44.7 us
  starting transfers between devices: 65.9 us -> 57.6 us
  other arithmetic: 9.33 us -> 10.9 us
    all_to_all x6 -> x4, waiting for transfers between devices: 54.3 us -> 44.7 us  [the longest x1 19.6 us: convolve_and_sum(): lax.all_to_all(split, 'ky', split_axis=1, concat_axis=1, tiled=True)]
    all_to_all x6 -> x4, starting transfers between devices: 48.5 us -> 40.2 us  [the longest x1 11.7 us: convolve_and_sum(): lax.all_to_all(split, 'ky', split_axis=1, concat_axis=1, tiled=True)]
    reshape x0 -> x1, other arithmetic: none -> 2.05 us  [with_sums(): tile.reshape([1] * (data.ndim - 2) + [8, -1])]
    another operation x1 -> x0, other arithmetic: 1.99 us -> none  [body(): jnp.stack([jnp.sum(packed_state_matrix[2] + packed_state_matrix[3]), jnp....]
    mul x2, local copies, waits for them, and re-layouts: 0.67 us -> 2.31 us  [convolve_and_sum(): weighted = spectrum * (weight * (1.0 / primitive_tile_total))[None]]
    concatenate x0 -> x2, other arithmetic: none -> 1.53 us  [with_sums(): jnp.concatenate([data, jnp.broadcast_to(tile.reshape([1] * (data.ndim - 2...]
  transfers between devices with their start and end apart: 10 -> 8, of which waited for: 5 -> 3; matrix products, arithmetic and copies ran while one was open for 10% -> 7% of each run, Pallas kernels for 0% -> 0%
where the time goes in v3:
time: 129 us; the launch traced here: 128 us
  starting transfers between devices  57.6 us (45%)
  waiting for transfers between devices  44.7 us (35%)
  other arithmetic  10.9 us (8%)
  local copies, waits for them, and re-layouts  7.96 us (6%)
  matrix products  5.28 us (4%)
    all_to_all x1, waiting for transfers between devices, convolve_and_sum(): lax.all_to_all(split, 'ky', split_axis=1, concat_axis=1, tiled=True)  19.6 us
    all_to_all x1, waiting for transfers between devices, convolve_and_sum(): lax.all_to_all(back_y, 'ky', split_axis=1, concat_axis=1, tiled=True)  18 us
    ppermute x2, starting transfers between devices, neighbours(): lax.ppermute(initial.reshape(dense), axis, down).reshape(initial.shape)  11.9 us
    all_to_all x1, starting transfers between devices, convolve_and_sum(): lax.all_to_all(split, 'ky', split_axis=1, concat_axis=1, tiled=True)  11.7 us
    all_to_all x1, starting transfers between devices, convolve_and_sum(): lax.all_to_all(source, 'kx', split_axis=0, concat_axis=1, tiled=True)  10.3 us
    all_to_all x1, starting transfers between devices, convolve_and_sum(): back = lax.all_to_all(final, 'kx', split_axis=1, concat_axis=0, tiled=True)  10.3 us
    all_to_all x1, starting transfers between devices, convolve_and_sum(): lax.all_to_all(back_y, 'ky', split_axis=1, concat_axis=1, tiled=True)  7.8 us
    all_to_all x1, waiting for transfers between devices, convolve_and_sum(): back = lax.all_to_all(final, 'kx', split_axis=1, concat_axis=0, tiled=True)  7.11 us
  transfers between devices with their start and end apart: 8, of which 3 were waited for; matrix products, arithmetic and copies ran while one was open for 7% of the time, Pallas kernels for 0%

profile of v3, /device:TPU:1, one launch (start us, length us, event | category | flops | bytes accessed | tf_op | source)
XLA Modules:
  0.0 127.6 jit_solution(115464982620760456)
XLA Ops:
  0.6 10.3 %all-to-all-start = ((f32[16,32,128]{2,1,0:T(8,128)}), f32[16,32,128]{2,1,0:T(8,128)S(1)}, u32[]{:S(2)}, u32[]{:S(2)}) async-start(f32[16,32,128]{2,1,0:T(8,128)} %param.17), calls=%async_computation | async-start | bytes 524288 | tf_op jit(solution)/shard_map/all_to_all | solution.py:171
  11.0 0.8 copy-done.5
  11.9 3.5 %collective-permute-start.1 = (f32[40,128]{1,0:T(8,128)S(1)}, f32[40,128]{1,0:T(8,128)S(1)}, u32[]{:S(2)}, u32[]{:S(2)}) collective-permute-start(f32[40,128]{1,0:T(8,128)S(1)} %bitcast.100), channel_id=1, source_target_pairs={{0,32},{32,64},{64,96},{96,128},{128,160},{160,192},{192,224},{224... | collective-permute-start | bytes 61448 | tf_op jit(solution)/shard_map/ppermute | solution.py:201
  15.4 1.9 %collective-permute-start = (f32[40,128]{1,0:T(8,128)S(1)}, f32[40,128]{1,0:T(8,128)S(1)}, u32[]{:S(2)}, u32[]{:S(2)}) collective-permute-start(f32[40,128]{1,0:T(8,128)S(1)} %bitcast.99), channel_id=1, source_target_pairs={{32,0},{64,32},{96,64},{128,96},{160,128},{192,160},{224,192},{256... | collective-permute-start | bytes 61448 | tf_op jit(solution)/shard_map/ppermute | solution.py:202
  17.7 1.9 %collective-permute-start.3 = (f32[10,128]{1,0:T(8,128)S(1)}, f32[10,128]{1,0:T(8,128)S(1)}, u32[]{:S(2)}, u32[]{:S(2)}) collective-permute-start(f32[10,128]{1,0:T(8,128)S(1)} %reshape.183), channel_id=1, source_target_pairs={{0,1},{1,2},{2,3},{3,4},{4,5},{5,6},{6,7},{7,8},{8,9},{9,10},{10,1... | collective-permute-start | bytes 15368 | tf_op jit(solution)/shard_map/ppermute | solution.py:201
  19.8 10.0 %collective-permute-start.2 = (f32[10,128]{1,0:T(8,128)S(1)}, f32[10,128]{1,0:T(8,128)S(1)}, u32[]{:S(2)}, u32[]{:S(2)}) collective-permute-start(f32[10,128]{1,0:T(8,128)S(1)} %reshape.181), channel_id=1, source_target_pairs={{1,0},{2,1},{3,2},{4,3},{5,4},{6,5},{7,6},{8,7},{9,8},{10,9},{11,1... | collective-permute-start | bytes 15368 | tf_op jit(solution)/shard_map/ppermute | solution.py:202
  31.1 0.8 fusion.7
  32.5 2.1 %maximum_bitcast_fusion.1 = f32[1,1,1,3]{3,2,1,0:T(1,128)S(1)} fusion(f32[1]{0:T(128)} %bitcast.12, f32[1]{0:T(128)} %bitcast.11, f32[1]{0:T(128)} %bitcast.6), kind=kLoop, calls=%fused_computation.92 | loop fusion | flops 6 | bytes 24 | tf_op jit(solution)/shard_map/reshape | solution.py:164
  34.6 1.0 fusion.33
  35.6 0.8 pad_maximum_fusion
  36.4 11.7 %all-to-all-start.1 = ((f32[1,32,24,128]{3,2,0,1:T(8,128)}), f32[1,32,24,128]{3,2,0,1:T(8,128)S(1)}, u32[]{:S(2)}, u32[]{:S(2)}) async-start(f32[1,32,24,128]{3,2,0,1:T(8,128)} %pad_maximum_fusion), calls=%async_computation.1 | async-start | bytes 786432 | tf_op jit(solution)/shard_map/all_to_all | solution.py:177
  48.9 1.3 %mul.1164 = f32[16,128,32]{2,1,0:T(8,128)S(1)} reshape(f32[16,4096]{1,0:T(8,128)} %broadcast_multiply_fusion) | data formatting | bytes 524288 | tf_op jit(solution)/shard_map/mul | solution.py:181
  50.2 1.0 copy.37
  51.2 19.6 %all-to-all-done.1 = f32[1,32,24,128]{3,2,0,1:T(8,128)S(1)} async-done(((f32[1,32,24,128]{3,2,0,1:T(8,128)}), f32[1,32,24,128]{3,2,0,1:T(8,128)S(1)}, u32[]{:S(2)}, u32[]{:S(2)}) %all-to-all-start.1) | async-done | bytes 393248 | tf_op jit(solution)/shard_map/all_to_all | solution.py:177
  75.5 0.9 copy.42
  76.4 7.8 %all-to-all-start.2 = ((f32[1,32,16,128]{3,2,0,1:T(8,128)}), f32[1,32,16,128]{3,2,0,1:T(8,128)S(1)}, u32[]{:S(2)}, u32[]{:S(2)}) async-start(f32[1,32,16,128]{3,2,0,1:T(8,128)} %copy.42), calls=%async_computation.2 | async-start | bytes 524288 | tf_op jit(solution)/shard_map/all_to_all | solution.py:183
  84.2 18.0 %all-to-all-done.2 = f32[1,32,16,128]{3,2,0,1:T(8,128)S(1)} async-done(((f32[1,32,16,128]{3,2,0,1:T(8,128)}), f32[1,32,16,128]{3,2,0,1:T(8,128)S(1)}, u32[]{:S(2)}, u32[]{:S(2)}) %all-to-all-start.2) | async-done | bytes 262176 | tf_op jit(solution)/shard_map/all_to_all | solution.py:183
  102.3 0.8 convolution_bitcast_fusion
  103.2 0.7 maximum_bitcast_fusion
  103.9 10.3 %all-to-all-start.3 = ((f32[1,16,40,128]{3,2,0,1:T(8,128)}), f32[1,16,40,128]{3,2,0,1:T(8,128)S(1)}, u32[]{:S(2)}, u32[]{:S(2)}) async-start(f32[1,16,40,128]{3,2,0,1:T(8,128)} %maximum_bitcast_fusion), calls=%async_computation.3 | async-start | bytes 655360 | tf_op jit(solution)/shard_map/all_to_all | solution.py:188
  114.8 7.1 %all-to-all-done.3 = f32[1,16,40,128]{3,2,0,1:T(8,128)S(1)} async-done(((f32[1,16,40,128]{3,2,0,1:T(8,128)}), f32[1,16,40,128]{3,2,0,1:T(8,128)S(1)}, u32[]{:S(2)}, u32[]{:S(2)}) %all-to-all-start.3) | async-done | bytes 327712 | tf_op jit(solution)/shard_map/all_to_all | solution.py:188
  122.1 0.9 copy-done.8
  123.1 1.3 fusion.26
  124.9 1.3 %fusion.17 = f32[16,32,128]{2,1,0:T(8,128)S(1)} fusion(f32[20,32,128]{2,1,0:T(8,128)S(1)} %get-tuple-element.33, f32[16,32,128]{2,1,0:T(8,128)S(1)} %constant_dynamic-update-slice_fusion.2, f32[20,32,128]{2,1,0:T(8,128)S(1)} %get-tuple-element.32, f32[]{:T(128)} %bitcast.44, f32[]{:T(128)} %bitcast.43), kind=kLoop, calls=%fused_computation.38 | loop fusion | flops 262144 | bytes 1048584 | tf_op jit(solution)/shard_map/add | solution.py:104
  (82 shorter events, 10.7 us)
Async XLA Ops:
  0.6 10.4 %copy-start = (f32[16,32,128]{2,1,0:T(8,128)S(1)}, f32[16,32,128]{2,1,0:T(8,128)}, u32[]{:S(2)}) copy-start(f32[16,32,128]{2,1,0:T(8,128)} %param.17) | copy-start | bytes 786436
  0.6 34.0 %all-to-all-start = ((f32[16,32,128]{2,1,0:T(8,128)}), f32[16,32,128]{2,1,0:T(8,128)S(1)}, u32[]{:S(2)}, u32[]{:S(2)}) async-start(f32[16,32,128]{2,1,0:T(8,128)} %param.17), calls=%async_computation | async-start | bytes 524288 | tf_op jit(solution)/shard_map/all_to_all | solution.py:171
  11.0 0.8 copy-start.5
  11.9 19.3 %collective-permute-start.1 = (f32[40,128]{1,0:T(8,128)S(1)}, f32[40,128]{1,0:T(8,128)S(1)}, u32[]{:S(2)}, u32[]{:S(2)}) collective-permute-start(f32[40,128]{1,0:T(8,128)S(1)} %bitcast.100), channel_id=1, source_target_pairs={{0,32},{32,64},{64,96},{96,128},{128,160},{160,192},{192,224},{224... | collective-permute-start | bytes 61448 | tf_op jit(solution)/shard_map/ppermute | solution.py:201
  15.4 15.7 %collective-permute-start = (f32[40,128]{1,0:T(8,128)S(1)}, f32[40,128]{1,0:T(8,128)S(1)}, u32[]{:S(2)}, u32[]{:S(2)}) collective-permute-start(f32[40,128]{1,0:T(8,128)S(1)} %bitcast.99), channel_id=1, source_target_pairs={{32,0},{64,32},{96,64},{128,96},{160,128},{192,160},{224,192},{256... | collective-permute-start | bytes 61448 | tf_op jit(solution)/shard_map/ppermute | solution.py:202
  17.7 12.8 %collective-permute-start.3 = (f32[10,128]{1,0:T(8,128)S(1)}, f32[10,128]{1,0:T(8,128)S(1)}, u32[]{:S(2)}, u32[]{:S(2)}) collective-permute-start(f32[10,128]{1,0:T(8,128)S(1)} %reshape.183), channel_id=1, source_target_pairs={{0,1},{1,2},{2,3},{3,4},{4,5},{5,6},{6,7},{7,8},{8,9},{9,10},{10,1... | collective-permute-start | bytes 15368 | tf_op jit(solution)/shard_map/ppermute | solution.py:201
  19.8 11.0 %collective-permute-start.2 = (f32[10,128]{1,0:T(8,128)S(1)}, f32[10,128]{1,0:T(8,128)S(1)}, u32[]{:S(2)}, u32[]{:S(2)}) collective-permute-start(f32[10,128]{1,0:T(8,128)S(1)} %reshape.181), channel_id=1, source_target_pairs={{1,0},{2,1},{3,2},{4,3},{5,4},{6,5},{7,6},{8,7},{9,8},{10,9},{11,1... | collective-permute-start | bytes 15368 | tf_op jit(solution)/shard_map/ppermute | solution.py:202
  30.8 3.8 %copy-start.1 = (f32[512,512]{1,0:T(8,128)S(1)}, f32[512,512]{1,0:T(8,128)}, u32[]{:S(2)}) copy-start(f32[512,512]{1,0:T(8,128)} %constant.85.clone) | copy-start | bytes 3145732
  36.4 11.7 %copy-start.6 = (f32[16,4096]{1,0:T(8,128)S(1)}, f32[16,4096]{1,0:T(8,128)}, u32[]{:S(2)}) copy-start(f32[16,4096]{1,0:T(8,128)} %param.21) | copy-start | bytes 786436
  36.4 34.4 %all-to-all-start.1 = ((f32[1,32,24,128]{3,2,0,1:T(8,128)}), f32[1,32,24,128]{3,2,0,1:T(8,128)S(1)}, u32[]{:S(2)}, u32[]{:S(2)}) async-start(f32[1,32,24,128]{3,2,0,1:T(8,128)} %pad_maximum_fusion), calls=%async_computation.1 | async-start | bytes 786432 | tf_op jit(solution)/shard_map/all_to_all | solution.py:177
  51.2 19.6 %copy-start.12 = (f32[32,32,1]{1,0,2:T(8,128)S(1)}, f32[32,32,1]{1,0,2:T(8,128)}, u32[]{:S(2)}) copy-start(f32[32,32,1]{1,0,2:T(8,128)} %constant.100) | copy-start | bytes 12292
  70.8 0.7 copy-start.9
  70.8 0.7 copy-start.10
  70.8 0.7 copy-start.11
  71.6 0.8 copy-start.4
  72.4 0.9 copy-start.2
  72.4 1.0 copy-start.3
  76.4 25.9 %all-to-all-start.2 = ((f32[1,32,16,128]{3,2,0,1:T(8,128)}), f32[1,32,16,128]{3,2,0,1:T(8,128)S(1)}, u32[]{:S(2)}, u32[]{:S(2)}) async-start(f32[1,32,16,128]{3,2,0,1:T(8,128)} %copy.42), calls=%async_computation.2 | async-start | bytes 524288 | tf_op jit(solution)/shard_map/all_to_all | solution.py:183
  103.9 10.3 %copy-start.13 = (f32[2]{0:T(128)S(1)}, f32[2]{0:T(128)}, u32[]{:S(2)}) copy-start(f32[2]{0:T(128)} %param.22) | copy-start | bytes 28
  103.9 18.0 %all-to-all-start.3 = ((f32[1,16,40,128]{3,2,0,1:T(8,128)}), f32[1,16,40,128]{3,2,0,1:T(8,128)S(1)}, u32[]{:S(2)}, u32[]{:S(2)}) async-start(f32[1,16,40,128]{3,2,0,1:T(8,128)} %maximum_bitcast_fusion), calls=%async_computation.3 | async-start | bytes 655360 | tf_op jit(solution)/shard_map/all_to_all | solution.py:188
  122.0 0.9 copy-start.8
  122.1 1.0 copy-start.7

commit v4 on v3

--- a/solution.py
+++ b/solution.py
@@ -164,24 +164,25 @@
     return jnp.concatenate([data, jnp.broadcast_to(tile.reshape([1] * (data.ndim - 2) + [8, -1]), shape)], axis=dim)
 
 
-def convolve_and_sum(source, interaction, local_sums, primitive_tile_total):
+def convolve_and_sum(source, interaction, local_sums, after_transform, primitive_tile_total):
     kx_devices = lax.axis_size("kx")
     ky_devices = lax.axis_size("ky")
-    sum_count = local_sums.shape[0]
+    sum_count = 3
     along_kx = lax.all_to_all(source, "kx", split_axis=0, concat_axis=1, tiled=True)
     components, x_length, column_count = along_kx.shape
     row_count = x_length // ky_devices
     tables = hartley_tables(x_length, ky_devices, column_count)
     rows_x = contract("px,cxy->cpy", tables["cas_x"], along_kx)
-    split = with_sums(rows_x.reshape(components, ky_devices, row_count, column_count), local_sums, 2)
+    rows_x = after_transform(rows_x)
+    split = rows_x.reshape(components, ky_devices, row_count, column_count)
     along_ky = lax.all_to_all(split, "ky", split_axis=1, concat_axis=1, tiled=True)
-    ky_sums = jnp.sum(along_ky[0, :, row_count, 0:sum_count], axis=0)
-    spectrum = hartley_y(along_ky[:, :, 0:row_count], tables)
+    spectrum = hartley_y(along_ky, tables)
     weight = interaction.reshape(row_count, column_count, ky_devices).transpose(2, 0, 1)
     weighted = spectrum * (weight * (1.0 / primitive_tile_total))[None]
-    back_y = hartley_y_transposed(weighted, tables)
+    back_y = with_sums(hartley_y_transposed(weighted, tables), local_sums(), 2)
     returned = lax.all_to_all(back_y, "ky", split_axis=1, concat_axis=1, tiled=True)
-    returned = returned.reshape(components, x_length, column_count)
+    ky_sums = jnp.sum(returned[0, :, row_count, 0:sum_count], axis=0)
+    returned = returned[:, :, 0:row_count].reshape(components, x_length, column_count)
     final = contract("px,cpy->cxy", tables["cas_x"], returned)
     rows_local = x_length // kx_devices
     final = with_sums(final.reshape(components, kx_devices, rows_local, column_count), ky_sums, 2)
@@ -207,28 +208,40 @@
     rows_local = packed_state_matrix.shape[1]
     columns_local = packed_state_matrix.shape[2]
     primitive_tile_total = rows_local * columns_local * lax.axis_size("kx") * lax.axis_size("ky")
-    stacked = jnp.concatenate([packed_state_matrix, energies])
-    column_core = neighbours(stacked, "kx", 1, 2)
-    row_core = neighbours(stacked, "ky", 2, 2)
-    gradient_x = (
-        8.0 * (column_core[:, 3:-1] - column_core[:, 1:-3])
-        - (column_core[:, 4:] - column_core[:, :-4])
-    ) / 12.0
-    gradient_y = (
-        8.0 * (row_core[:, :, 3:-1] - row_core[:, :, 1:-3])
-        - (row_core[:, :, 4:] - row_core[:, :, :-4])
-    ) / 12.0
     populations = packed_state_matrix[0:4]
-    local_sums = jnp.stack(
-        [
-            jnp.sum(packed_state_matrix[2] + packed_state_matrix[3]),
-            jnp.sum(gradient_x[16:20] * populations),
-            jnp.sum(gradient_y[16:20] * populations),
-        ]
-    )
+    halo_source = []
+    gradients = []
+
+    def after_transform(rows_x):
+        rows_x, late = lax.optimization_barrier((rows_x, jnp.concatenate([packed_state_matrix, energies])))
+        halo_source.append(late)
+        return rows_x
+
+    def local_sums():
+        stacked = halo_source[0]
+        column_core = neighbours(stacked, "kx", 1, 2)
+        row_core = neighbours(stacked, "ky", 2, 2)
+        gradient_x = (
+            8.0 * (column_core[:, 3:-1] - column_core[:, 1:-3])
+            - (column_core[:, 4:] - column_core[:, :-4])
+        ) / 12.0
+        gradient_y = (
+            8.0 * (row_core[:, :, 3:-1] - row_core[:, :, 1:-3])
+            - (row_core[:, :, 4:] - row_core[:, :, :-4])
+        ) / 12.0
+        gradients.extend([gradient_x, gradient_y])
+        return jnp.stack(
+            [
+                jnp.sum(packed_state_matrix[2] + packed_state_matrix[3]),
+                jnp.sum(gradient_x[16:20] * populations),
+                jnp.sum(gradient_y[16:20] * populations),
+            ]
+        )
+
     convolved, totals = convolve_and_sum(
-        packed_state_matrix, interaction, local_sums, primitive_tile_total
-    )
+        packed_state_matrix, interaction, local_sums, after_transform, primitive_tile_total
+    )
+    gradient_x, gradient_y = gradients
     shielding_multiplier = 1.0 / (1.0 + SHIELDING_LEVEL * totals[0])
     self_energy = -shielding_multiplier * convolved
     section_slope = slope_terms(

time: 129 us -> 123 us (0.953)
  blocking collectives: 0 us -> 34.2 us
  waiting for transfers between devices: 44.7 us -> 14 us
  starting transfers between devices: 57.6 us -> 50.7 us
  local copies, waits for them, and re-layouts: 7.96 us -> 5.71 us
  matrix products: 5.28 us -> 7.2 us
  other arithmetic: 10.9 us -> 9.26 us
    all_to_all x0 -> x1, blocking collectives: none -> 34.2 us  [convolve_and_sum(): lax.all_to_all(back_y, 'ky', split_axis=1, concat_axis=1, tiled=True)]
    all_to_all x1, waiting for transfers between devices: 19.6 us -> 0.01 us  [convolve_and_sum(): lax.all_to_all(split, 'ky', split_axis=1, concat_axis=1, tiled=True)]
    all_to_all x1 -> x0, waiting for transfers between devices: 18 us -> none  [convolve_and_sum(): lax.all_to_all(back_y, 'ky', split_axis=1, concat_axis=1, tiled=True)]
    all_to_all x1 -> x0, starting transfers between devices: 7.8 us -> none  [convolve_and_sum(): lax.all_to_all(back_y, 'ky', split_axis=1, concat_axis=1, tiled=True)]
    all_to_all x1, waiting for transfers between devices: 0.01 us -> 6.23 us  [convolve_and_sum(): lax.all_to_all(source, 'kx', split_axis=0, concat_axis=1, tiled=True)]
    ppermute x2, starting transfers between devices: 11.9 us -> 6.96 us  [neighbours(): lax.ppermute(initial.reshape(dense), axis, down).reshape(initial.shape)]
    all_to_all x1, starting transfers between devices: 11.7 us -> 14 us  [convolve_and_sum(): lax.all_to_all(split, 'ky', split_axis=1, concat_axis=1, tiled=True)]
    dot_general x10, matrix products: 5.28 us -> 7.2 us  [contract(): jnp.einsum(einsum_form, left, right, precision=lax.Precision.HIGHEST, pre...]
  transfers between devices with their start and end apart: 8 -> 7, of which waited for: 3 -> 3; matrix products, arithmetic and copies ran while one was open for 7% -> 5% of each run, Pallas kernels for 0% -> 0%
where the time goes in v4:
time: 123 us; the launch traced here: 122 us
  starting transfers between devices  50.7 us (41%)
  blocking collectives  34.2 us (28%)
  waiting for transfers between devices  14 us (11%)
  other arithmetic  9.26 us (8%)
  matrix products  7.2 us (6%)
  local copies, waits for them, and re-layouts  5.71 us (5%)
    all_to_all x1, blocking collectives, convolve_and_sum(): lax.all_to_all(back_y, 'ky', split_axis=1, concat_axis=1, tiled=True)  34.2 us
    all_to_all x1, starting transfers between devices, convolve_and_sum(): lax.all_to_all(split, 'ky', split_axis=1, concat_axis=1, tiled=True)  14 us
    all_to_all x1, starting transfers between devices, convolve_and_sum(): back = lax.all_to_all(final, 'kx', split_axis=1, concat_axis=0, tiled=True)  12.1 us
    all_to_all x1, starting transfers between devices, convolve_and_sum(): lax.all_to_all(source, 'kx', split_axis=0, concat_axis=1, tiled=True)  10.3 us
    ppermute x2, starting transfers between devices, neighbours(): before = lax.ppermute(last.reshape(dense), axis, up).reshape(last.shape)  7.3 us
    dot_general x10, matrix products, contract(): jnp.einsum(einsum_form, left, right, precision=lax.Precision.HIGHEST, pre...  7.2 us
    all_to_all x1, waiting for transfers between devices, convolve_and_sum(): back = lax.all_to_all(final, 'kx', split_axis=1, concat_axis=0, tiled=True)  7.1 us
    ppermute x2, starting transfers between devices, neighbours(): lax.ppermute(initial.reshape(dense), axis, down).reshape(initial.shape)  6.96 us
  transfers between devices with their start and end apart: 7, of which 3 were waited for; matrix products, arithmetic and copies ran while one was open for 5% of the time, Pallas kernels for 0%

profile of v4, /device:TPU:1, one launch (start us, length us, event | category | flops | bytes accessed | tf_op | source)
XLA Modules:
  0.0 122.2 jit_solution(11633970067301399161)
XLA Ops:
  0.6 10.3 %all-to-all-start = ((f32[16,32,128]{2,1,0:T(8,128)}), f32[16,32,128]{2,1,0:T(8,128)S(1)}, u32[]{:S(2)}, u32[]{:S(2)}) async-start(f32[16,32,128]{2,1,0:T(8,128)} %param.17), calls=%async_computation | async-start | bytes 524288 | tf_op jit(solution)/shard_map/all_to_all | solution.py:171
  11.0 0.9 copy-done
  12.0 6.2 %all-to-all-done = f32[16,32,128]{2,1,0:T(8,128)S(1)} async-done(((f32[16,32,128]{2,1,0:T(8,128)}), f32[16,32,128]{2,1,0:T(8,128)S(1)}, u32[]{:S(2)}, u32[]{:S(2)}) %all-to-all-start) | async-done | bytes 262176 | tf_op jit(solution)/shard_map/all_to_all | solution.py:171
  18.2 2.9 %convolution_bitcast_fusion.2 = f32[1,512,128]{2,1,0:T(8,128)} fusion(f32[512,512]{1,0:T(8,128)} %constant.85.clone, f32[512,128]{1,0:T(8,128)S(1)} %bitcast.99), kind=kOutput, calls=%fused_computation.9 | convolution fusion | flops 402653184 | bytes 1572864 | tf_op jit(solution)/shard_map/px,cxy->cpy/dot_general | solution.py:109
  21.3 14.0 %all-to-all-start.1 = ((f32[1,32,16,128]{3,2,0,1:T(8,128)}), f32[1,32,16,128]{3,2,0,1:T(8,128)S(1)}, u32[]{:S(2)}, u32[]{:S(2)}) async-start(f32[1,32,16,128]{3,2,0,1:T(8,128)} %bitcast.5), calls=%async_computation.1 | async-start | bytes 524288 | tf_op jit(solution)/shard_map/all_to_all | solution.py:178
  35.6 4.6 %collective-permute-start.3 = (f32[10,128]{1,0:T(8,128)S(1)}, f32[10,128]{1,0:T(8,128)S(1)}, u32[]{:S(2)}, u32[]{:S(2)}) collective-permute-start(f32[10,128]{1,0:T(8,128)S(1)} %reshape.186), channel_id=1, source_target_pairs={{0,1},{1,2},{2,3},{3,4},{4,5},{5,6},{6,7},{7,8},{8,9},{9,10},{10,1... | collective-permute-start | bytes 15368 | tf_op jit(solution)/shard_map/ppermute | solution.py:202
  40.2 2.7 %collective-permute-start.1 = (f32[40,128]{1,0:T(8,128)S(1)}, f32[40,128]{1,0:T(8,128)S(1)}, u32[]{:S(2)}, u32[]{:S(2)}) collective-permute-start(f32[40,128]{1,0:T(8,128)S(1)} %bitcast.102), channel_id=1, source_target_pairs={{0,32},{32,64},{64,96},{96,128},{128,160},{160,192},{192,224},{224... | collective-permute-start | bytes 61448 | tf_op jit(solution)/shard_map/ppermute | solution.py:202
  42.9 3.0 %collective-permute-start = (f32[40,128]{1,0:T(8,128)S(1)}, f32[40,128]{1,0:T(8,128)S(1)}, u32[]{:S(2)}, u32[]{:S(2)}) collective-permute-start(f32[40,128]{1,0:T(8,128)S(1)} %bitcast.101), channel_id=1, source_target_pairs={{32,0},{64,32},{96,64},{128,96},{160,128},{192,160},{224,192},{256... | collective-permute-start | bytes 61448 | tf_op jit(solution)/shard_map/ppermute | solution.py:203
  46.1 4.0 %collective-permute-start.2 = (f32[10,128]{1,0:T(8,128)S(1)}, f32[10,128]{1,0:T(8,128)S(1)}, u32[]{:S(2)}, u32[]{:S(2)}) collective-permute-start(f32[10,128]{1,0:T(8,128)S(1)} %reshape.184), channel_id=1, source_target_pairs={{1,0},{2,1},{3,2},{4,3},{5,4},{6,5},{7,6},{8,7},{9,8},{10,9},{11,1... | collective-permute-start | bytes 15368 | tf_op jit(solution)/shard_map/ppermute | solution.py:203
  50.1 0.6 add_reduce_fusion
  51.7 0.6 collective-permute-done.2
  53.3 0.7 fusion.32
  54.0 2.0 %maximum_bitcast_fusion.1 = f32[1,1,1,3]{3,2,1,0:T(1,128)S(1)} fusion(f32[1]{0:T(128)} %bitcast.30, f32[1]{0:T(128)} %bitcast.29, f32[1]{0:T(128)} %bitcast.24), kind=kLoop, calls=%fused_computation.93 | loop fusion | flops 6 | bytes 24 | tf_op jit(solution)/shard_map/reshape | solution.py:164
  60.9 34.2 %all_to_all.31 = f32[1,32,24,128]{3,2,0,1:T(8,128)S(1)} all-to-all(f32[1,32,24,128]{3,2,0,1:T(8,128)S(1)} %copy.42), channel_id=1, replica_groups=mesh['kx'=16,'ky'=32] {'ky'}, dimensions={1} | all-to-all | bytes 786432 | tf_op jit(solution)/shard_map/all_to_all | solution.py:183
  95.2 0.8 convolution_bitcast_fusion
  96.1 0.7 maximum_bitcast_fusion
  96.8 12.1 %all-to-all-start.3 = ((f32[1,16,40,128]{3,2,0,1:T(8,128)}), f32[1,16,40,128]{3,2,0,1:T(8,128)S(1)}, u32[]{:S(2)}, u32[]{:S(2)}) async-start(f32[1,16,40,128]{3,2,0,1:T(8,128)} %maximum_bitcast_fusion), calls=%async_computation.3 | async-start | bytes 655360 | tf_op jit(solution)/shard_map/all_to_all | solution.py:189
  108.9 0.6 fusion.35
  109.5 7.1 %all-to-all-done.3 = f32[1,16,40,128]{3,2,0,1:T(8,128)S(1)} async-done(((f32[1,16,40,128]{3,2,0,1:T(8,128)}), f32[1,16,40,128]{3,2,0,1:T(8,128)S(1)}, u32[]{:S(2)}, u32[]{:S(2)}) %all-to-all-start.3) | async-done | bytes 327712 | tf_op jit(solution)/shard_map/all_to_all | solution.py:189
  116.8 0.9 copy-done.7
  117.8 1.2 %fusion.29 = f32[12,32,128]{2,1,0:T(8,128)S(1)} fusion(f32[16,1,32,128]{3,2,0,1:T(8,128)S(1)} %slice_multiply_fusion.2, f32[12,32,128]{2,1,0:T(8,128)S(1)} %copy-done.6, f32[12,32,128]{2,1,0:T(8,128)S(1)} %copy-done.7, f32[]{:T(128)} %bitcast.45, f32[]{:T(128)} %bitcast.44), kind=kLoop, calls=%fused_computation.58 | loop fusion | flops 196608 | bytes 786440 | tf_op jit(solution)/shard_map/add | solution.py:101
  119.6 1.3 %fusion.16 = f32[16,32,128]{2,1,0:T(8,128)S(1)} fusion(f32[20,32,128]{2,1,0:T(8,128)S(1)} %fusion.13, f32[16,32,128]{2,1,0:T(8,128)S(1)} %constant_dynamic-update-slice_fusion.2, f32[20,32,128]{2,1,0:T(8,128)S(1)} %get-tuple-element.36, f32[]{:T(128)} %bitcast.45, f32[]{:T(128)} %bitcast.44), kind=kLoop, calls=%fused_computation.36 | loop fusion | flops 262144 | bytes 1048584 | tf_op jit(solution)/shard_map/add | solution.py:104
  120.9 0.6 multiply_subtract_fusion.1
  121.5 0.7 pad_maximum_fusion.5
  (80 shorter events, 8.3 us)
Async XLA Ops:
  0.6 10.4 %copy-start.5 = (f32[16,4096]{1,0:T(8,128)S(1)}, f32[16,4096]{1,0:T(8,128)}, u32[]{:S(2)}) copy-start(f32[16,4096]{1,0:T(8,128)} %param.21) | copy-start | bytes 786436
  0.6 17.6 %all-to-all-start = ((f32[16,32,128]{2,1,0:T(8,128)}), f32[16,32,128]{2,1,0:T(8,128)S(1)}, u32[]{:S(2)}, u32[]{:S(2)}) async-start(f32[16,32,128]{2,1,0:T(8,128)} %param.17), calls=%async_computation | async-start | bytes 524288 | tf_op jit(solution)/shard_map/all_to_all | solution.py:171
  11.0 1.0 copy-start
  11.0 1.0 copy-start.2
  21.3 34.7 %all-to-all-start.1 = ((f32[1,32,16,128]{3,2,0,1:T(8,128)}), f32[1,32,16,128]{3,2,0,1:T(8,128)S(1)}, u32[]{:S(2)}, u32[]{:S(2)}) async-start(f32[1,32,16,128]{3,2,0,1:T(8,128)} %bitcast.5), calls=%async_computation.1 | async-start | bytes 524288 | tf_op jit(solution)/shard_map/all_to_all | solution.py:178
  35.6 15.8 %collective-permute-start.3 = (f32[10,128]{1,0:T(8,128)S(1)}, f32[10,128]{1,0:T(8,128)S(1)}, u32[]{:S(2)}, u32[]{:S(2)}) collective-permute-start(f32[10,128]{1,0:T(8,128)S(1)} %reshape.186), channel_id=1, source_target_pairs={{0,1},{1,2},{2,3},{3,4},{4,5},{5,6},{6,7},{7,8},{8,9},{9,10},{10,1... | collective-permute-start | bytes 15368 | tf_op jit(solution)/shard_map/ppermute | solution.py:202
  40.2 12.3 %collective-permute-start.1 = (f32[40,128]{1,0:T(8,128)S(1)}, f32[40,128]{1,0:T(8,128)S(1)}, u32[]{:S(2)}, u32[]{:S(2)}) collective-permute-start(f32[40,128]{1,0:T(8,128)S(1)} %bitcast.102), channel_id=1, source_target_pairs={{0,32},{32,64},{64,96},{96,128},{128,160},{160,192},{192,224},{224... | collective-permute-start | bytes 61448 | tf_op jit(solution)/shard_map/ppermute | solution.py:202
  42.9 9.7 %collective-permute-start = (f32[40,128]{1,0:T(8,128)S(1)}, f32[40,128]{1,0:T(8,128)S(1)}, u32[]{:S(2)}, u32[]{:S(2)}) collective-permute-start(f32[40,128]{1,0:T(8,128)S(1)} %bitcast.101), channel_id=1, source_target_pairs={{32,0},{64,32},{96,64},{128,96},{160,128},{192,160},{224,192},{256... | collective-permute-start | bytes 61448 | tf_op jit(solution)/shard_map/ppermute | solution.py:203
  46.1 6.2 %collective-permute-start.2 = (f32[10,128]{1,0:T(8,128)S(1)}, f32[10,128]{1,0:T(8,128)S(1)}, u32[]{:S(2)}, u32[]{:S(2)}) collective-permute-start(f32[10,128]{1,0:T(8,128)S(1)} %reshape.184), channel_id=1, source_target_pairs={{1,0},{2,1},{3,2},{4,3},{5,4},{6,5},{7,6},{8,7},{9,8},{10,9},{11,1... | collective-permute-start | bytes 15368 | tf_op jit(solution)/shard_map/ppermute | solution.py:203
  53.3 2.7 %copy-start.11 = (f32[32,32,1]{1,0,2:T(8,128)S(1)}, f32[32,32,1]{1,0,2:T(8,128)}, u32[]{:S(2)}) copy-start(f32[32,32,1]{1,0,2:T(8,128)} %constant.100) | copy-start | bytes 12292
  56.0 0.7 copy-start.8
  56.0 0.7 copy-start.9
  56.0 0.7 copy-start.10
  56.7 0.8 copy-start.4
  57.6 0.8 copy-start.3
  60.6 34.6 %copy-start.1 = (f32[512,512]{1,0:T(8,128)S(1)}, f32[512,512]{1,0:T(8,128)}, u32[]{:S(2)}) copy-start(f32[512,512]{1,0:T(8,128)} %constant.85.clone) | copy-start | bytes 3145732
  96.8 12.1 %copy-start.12 = (f32[2]{0:T(128)S(1)}, f32[2]{0:T(128)}, u32[]{:S(2)}) copy-start(f32[2]{0:T(128)} %param.22) | copy-start | bytes 28
  96.8 19.8 %all-to-all-start.3 = ((f32[1,16,40,128]{3,2,0,1:T(8,128)}), f32[1,16,40,128]{3,2,0,1:T(8,128)S(1)}, u32[]{:S(2)}, u32[]{:S(2)}) async-start(f32[1,16,40,128]{3,2,0,1:T(8,128)} %maximum_bitcast_fusion), calls=%async_computation.3 | async-start | bytes 655360 | tf_op jit(solution)/shard_map/all_to_all | solution.py:189
  116.7 0.9 copy-start.7
  116.8 1.0 copy-start.6

commit v5 on v4

--- a/solution.py
+++ b/solution.py
@@ -179,10 +179,10 @@
     spectrum = hartley_y(along_ky, tables)
     weight = interaction.reshape(row_count, column_count, ky_devices).transpose(2, 0, 1)
     weighted = spectrum * (weight * (1.0 / primitive_tile_total))[None]
-    back_y = with_sums(hartley_y_transposed(weighted, tables), local_sums(), 2)
+    ky_sums = lax.psum(local_sums(), "ky")
+    back_y = hartley_y_transposed(weighted, tables)
     returned = lax.all_to_all(back_y, "ky", split_axis=1, concat_axis=1, tiled=True)
-    ky_sums = jnp.sum(returned[0, :, row_count, 0:sum_count], axis=0)
-    returned = returned[:, :, 0:row_count].reshape(components, x_length, column_count)
+    returned = returned.reshape(components, x_length, column_count)
     final = contract("px,cpy->cxy", tables["cas_x"], returned)
     rows_local = x_length // kx_devices
     final = with_sums(final.reshape(components, kx_devices, rows_local, column_count), ky_sums, 2)

time: 123 us -> 186 us (1.51)
  blocking collectives: 34.2 us -> 63.5 us
  starting transfers between devices: 50.7 us -> 70.4 us
  waiting for transfers between devices: 14 us -> 28.2 us
    psum x0 -> x1, blocking collectives: none -> 63.5 us  [convolve_and_sum(): ky_sums = lax.psum(local_sums(), 'ky')]
    all_to_all x1 -> x0, blocking collectives: 34.2 us -> none  [convolve_and_sum(): lax.all_to_all(back_y, 'ky', split_axis=1, concat_axis=1, tiled=True)]
    all_to_all x1, waiting for transfers between devices: 0.01 us -> 13.9 us  [convolve_and_sum(): lax.all_to_all(split, 'ky', split_axis=1, concat_axis=1, tiled=True)]
    all_to_all x1, starting transfers between devices: 12.1 us -> 22.2 us  [convolve_and_sum(): back = lax.all_to_all(final, 'kx', split_axis=1, concat_axis=0, tiled=True)]
    all_to_all x0 -> x1, starting transfers between devices: none -> 6.15 us  [convolve_and_sum(): lax.all_to_all(back_y, 'ky', split_axis=1, concat_axis=1, tiled=True)]
    ppermute x2, starting transfers between devices: 6.96 us -> 9.05 us  [neighbours(): lax.ppermute(initial.reshape(dense), axis, down).reshape(initial.shape)]
    reshape x1 -> x0, other arithmetic: 1.97 us -> none  [with_sums(): tile.reshape([1] * (data.ndim - 2) + [8, -1])]
    broadcast_in_dim x0 -> x1, other arithmetic: none -> 1.95 us  [with_sums(): jnp.broadcast_to(tile.reshape([1] * (data.ndim - 2) + [8, -1]), shape)]
  transfers between devices with their start and end apart: 7 -> 8, of which waited for: 3 -> 3; matrix products, arithmetic and copies ran while one was open for 5% -> 6% of each run, Pallas kernels for 0% -> 0%
where the time goes in v5:
time: 186 us; the launch traced here: 185 us
  starting transfers between devices  70.4 us (38%)
  blocking collectives  63.5 us (34%)
  waiting for transfers between devices  28.2 us (15%)
  other arithmetic  9.39 us (5%)
  matrix products  7.21 us (4%)
  local copies, waits for them, and re-layouts  5.2 us (3%)
    psum x1, blocking collectives, convolve_and_sum(): ky_sums = lax.psum(local_sums(), 'ky')  63.5 us
    all_to_all x1, starting transfers between devices, convolve_and_sum(): back = lax.all_to_all(final, 'kx', split_axis=1, concat_axis=0, tiled=True)  22.2 us
    all_to_all x1, starting transfers between devices, convolve_and_sum(): lax.all_to_all(split, 'ky', split_axis=1, concat_axis=1, tiled=True)  14.1 us
    all_to_all x1, waiting for transfers between devices, convolve_and_sum(): lax.all_to_all(split, 'ky', split_axis=1, concat_axis=1, tiled=True)  13.9 us
    all_to_all x1, starting transfers between devices, convolve_and_sum(): lax.all_to_all(source, 'kx', split_axis=0, concat_axis=1, tiled=True)  10.3 us
    ppermute x2, starting transfers between devices, neighbours(): lax.ppermute(initial.reshape(dense), axis, down).reshape(initial.shape)  9.05 us
    ppermute x2, starting transfers between devices, neighbours(): before = lax.ppermute(last.reshape(dense), axis, up).reshape(last.shape)  8.53 us
    dot_general x10, matrix products, contract(): jnp.einsum(einsum_form, left, right, precision=lax.Precision.HIGHEST, pre...  7.21 us
  transfers between devices with their start and end apart: 8, of which 3 were waited for; matrix products, arithmetic and copies ran while one was open for 6% of the time, Pallas kernels for 0%

profile of v5, /device:TPU:1, one launch (start us, length us, event | category | flops | bytes accessed | tf_op | source)
XLA Modules:
  0.0 185.0 jit_solution(18380948689115364729)
XLA Ops:
  0.6 10.3 %all-to-all-start = ((f32[16,32,128]{2,1,0:T(8,128)}), f32[16,32,128]{2,1,0:T(8,128)S(1)}, u32[]{:S(2)}, u32[]{:S(2)}) async-start(f32[16,32,128]{2,1,0:T(8,128)} %param.15), calls=%async_computation | async-start | bytes 524288 | tf_op jit(solution)/shard_map/all_to_all | solution.py:171
  11.0 7.2 %all-to-all-done = f32[16,32,128]{2,1,0:T(8,128)S(1)} async-done(((f32[16,32,128]{2,1,0:T(8,128)}), f32[16,32,128]{2,1,0:T(8,128)S(1)}, u32[]{:S(2)}, u32[]{:S(2)}) %all-to-all-start) | async-done | bytes 262176 | tf_op jit(solution)/shard_map/all_to_all | solution.py:171
  18.2 2.9 %convolution_bitcast_fusion.2 = f32[1,512,128]{2,1,0:T(8,128)} fusion(f32[512,512]{1,0:T(8,128)} %constant.68.clone, f32[512,128]{1,0:T(8,128)S(1)} %bitcast.93), kind=kOutput, calls=%fused_computation.9 | convolution fusion | flops 402653184 | bytes 1572864 | tf_op jit(solution)/shard_map/px,cxy->cpy/dot_general | solution.py:109
  21.1 14.1 %all-to-all-start.1 = ((f32[1,32,16,128]{3,2,0,1:T(8,128)}), f32[1,32,16,128]{3,2,0,1:T(8,128)S(1)}, u32[]{:S(2)}, u32[]{:S(2)}) async-start(f32[1,32,16,128]{3,2,0,1:T(8,128)} %bitcast.5), calls=%async_computation.1 | async-start | bytes 524288 | tf_op jit(solution)/shard_map/all_to_all | solution.py:178
  36.4 4.8 %collective-permute-start.3 = (f32[10,128]{1,0:T(8,128)S(1)}, f32[10,128]{1,0:T(8,128)S(1)}, u32[]{:S(2)}, u32[]{:S(2)}) collective-permute-start(f32[10,128]{1,0:T(8,128)S(1)} %reshape.159), channel_id=1, source_target_pairs={{0,1},{1,2},{2,3},{3,4},{4,5},{5,6},{6,7},{7,8},{8,9},{9,10},{10,1... | collective-permute-start | bytes 15368 | tf_op jit(solution)/shard_map/ppermute | solution.py:202
  41.2 13.9 %all-to-all-done.1 = f32[1,32,16,128]{3,2,0,1:T(8,128)S(1)} async-done(((f32[1,32,16,128]{3,2,0,1:T(8,128)}), f32[1,32,16,128]{3,2,0,1:T(8,128)S(1)}, u32[]{:S(2)}, u32[]{:S(2)}) %all-to-all-start.1) | async-done | bytes 262176 | tf_op jit(solution)/shard_map/all_to_all | solution.py:178
  59.5 0.9 copy.42
  60.3 6.2 %all-to-all-start.2 = ((f32[1,32,16,128]{3,2,0,1:T(8,128)}), f32[1,32,16,128]{3,2,0,1:T(8,128)S(1)}, u32[]{:S(2)}, u32[]{:S(2)}) async-start(f32[1,32,16,128]{3,2,0,1:T(8,128)} %copy.42), calls=%async_computation.2 | async-start | bytes 524288 | tf_op jit(solution)/shard_map/all_to_all | solution.py:184
  66.5 3.8 %collective-permute-start.1 = (f32[40,128]{1,0:T(8,128)S(1)}, f32[40,128]{1,0:T(8,128)S(1)}, u32[]{:S(2)}, u32[]{:S(2)}) collective-permute-start(f32[40,128]{1,0:T(8,128)S(1)} %bitcast.95), channel_id=1, source_target_pairs={{0,32},{32,64},{64,96},{96,128},{128,160},{160,192},{192,224},{224... | collective-permute-start | bytes 61448 | tf_op jit(solution)/shard_map/ppermute | solution.py:202
  70.3 1.9 %collective-permute-start = (f32[40,128]{1,0:T(8,128)S(1)}, f32[40,128]{1,0:T(8,128)S(1)}, u32[]{:S(2)}, u32[]{:S(2)}) collective-permute-start(f32[40,128]{1,0:T(8,128)S(1)} %bitcast.94), channel_id=1, source_target_pairs={{32,0},{64,32},{96,64},{128,96},{160,128},{192,160},{224,192},{256... | collective-permute-start | bytes 61448 | tf_op jit(solution)/shard_map/ppermute | solution.py:203
  72.4 7.1 %collective-permute-start.2 = (f32[10,128]{1,0:T(8,128)S(1)}, f32[10,128]{1,0:T(8,128)S(1)}, u32[]{:S(2)}, u32[]{:S(2)}) collective-permute-start(f32[10,128]{1,0:T(8,128)S(1)} %reshape.157), channel_id=1, source_target_pairs={{1,0},{2,1},{3,2},{4,3},{5,4},{6,5},{7,6},{8,7},{9,8},{10,9},{11,1... | collective-permute-start | bytes 15368 | tf_op jit(solution)/shard_map/ppermute | solution.py:203
  79.5 0.7 add_reduce_fusion
  81.5 0.6 fusion.32
  82.2 2.0 %maximum_bitcast_fusion.1 = f32[1,3]{1,0:T(1,128)S(1)} fusion(f32[1]{0:T(128)} %bitcast.34, f32[1]{0:T(128)} %bitcast.33, f32[1]{0:T(128)} %bitcast.28), kind=kLoop, calls=%fused_computation.89 | loop fusion | flops 6 | bytes 24 | tf_op jit(solution)/shard_map/broadcast_in_dim | solution.py:164
  84.1 63.5 %psum.7 = f32[1,3]{1,0:T(1,128)S(1)} all-reduce(f32[1,3]{1,0:T(1,128)S(1)} %maximum_bitcast_fusion.1), channel_id=1, replica_groups=mesh['kx'=16,'ky'=32] {'ky'}, use_global_device_ids=true, to_apply=%region_3.0 | all-reduce | flops 3 | bytes 24 | tf_op jit(solution)/shard_map/psum | solution.py:182
  147.6 0.8 convolution_bitcast_fusion
  148.5 0.7 maximum_bitcast_fusion
  149.2 22.2 %all-to-all-start.3 = ((f32[1,16,40,128]{3,2,0,1:T(8,128)}), f32[1,16,40,128]{3,2,0,1:T(8,128)S(1)}, u32[]{:S(2)}, u32[]{:S(2)}) async-start(f32[1,16,40,128]{3,2,0,1:T(8,128)} %maximum_bitcast_fusion), calls=%async_computation.3 | async-start | bytes 655360 | tf_op jit(solution)/shard_map/all_to_all | solution.py:189
  171.4 0.6 fusion.35
  172.1 7.1 %all-to-all-done.3 = f32[1,16,40,128]{3,2,0,1:T(8,128)S(1)} async-done(((f32[1,16,40,128]{3,2,0,1:T(8,128)}), f32[1,16,40,128]{3,2,0,1:T(8,128)S(1)}, u32[]{:S(2)}, u32[]{:S(2)}) %all-to-all-start.3) | async-done | bytes 327712 | tf_op jit(solution)/shard_map/all_to_all | solution.py:189
  179.4 0.9 copy-done.7
  180.4 1.4 fusion.29
  182.3 1.4 fusion.16
  184.3 0.7 pad_maximum_fusion.4
  (77 shorter events, 8.3 us)
Async XLA Ops:
  0.6 10.4 %copy-start = (f32[16,32,128]{2,1,0:T(8,128)S(1)}, f32[16,32,128]{2,1,0:T(8,128)}, u32[]{:S(2)}) copy-start(f32[16,32,128]{2,1,0:T(8,128)} %param.15) | copy-start | bytes 786436
  0.6 10.4 %copy-start.2 = (f32[4,32,128]{2,1,0:T(8,128)S(1)}, f32[4,32,128]{2,1,0:T(8,128)}, u32[]{:S(2)}) copy-start(f32[4,32,128]{2,1,0:T(8,128)} %param.16) | copy-start | bytes 196612
  0.6 17.6 %all-to-all-start = ((f32[16,32,128]{2,1,0:T(8,128)}), f32[16,32,128]{2,1,0:T(8,128)S(1)}, u32[]{:S(2)}, u32[]{:S(2)}) async-start(f32[16,32,128]{2,1,0:T(8,128)} %param.15), calls=%async_computation | async-start | bytes 524288 | tf_op jit(solution)/shard_map/all_to_all | solution.py:171
  21.1 14.2 %copy-start.5 = (f32[16,4096]{1,0:T(8,128)S(1)}, f32[16,4096]{1,0:T(8,128)}, u32[]{:S(2)}) copy-start(f32[16,4096]{1,0:T(8,128)} %param.19) | copy-start | bytes 786436
  21.1 34.0 %all-to-all-start.1 = ((f32[1,32,16,128]{3,2,0,1:T(8,128)}), f32[1,32,16,128]{3,2,0,1:T(8,128)S(1)}, u32[]{:S(2)}, u32[]{:S(2)}) async-start(f32[1,32,16,128]{3,2,0,1:T(8,128)} %bitcast.5), calls=%async_computation.1 | async-start | bytes 524288 | tf_op jit(solution)/shard_map/all_to_all | solution.py:178
  36.2 18.9 %copy-start.11 = (f32[32,32,1]{1,0,2:T(8,128)S(1)}, f32[32,32,1]{1,0,2:T(8,128)}, u32[]{:S(2)}) copy-start(f32[32,32,1]{1,0,2:T(8,128)} %constant.81) | copy-start | bytes 12292
  36.4 19.2 %copy-start.8 = (f32[32,128]{1,0:T(8,128)S(1)}, f32[32,128]{1,0:T(8,128)}, u32[]{:S(2)}) copy-start(f32[32,128]{1,0:T(8,128)} %constant.79) | copy-start | bytes 49156
  36.4 19.2 %copy-start.9 = (f32[32,128]{1,0:T(8,128)S(1)}, f32[32,128]{1,0:T(8,128)}, u32[]{:S(2)}) copy-start(f32[32,128]{1,0:T(8,128)} %constant.78) | copy-start | bytes 49156
  36.4 19.2 %copy-start.10 = (f32[32,32,1]{1,0,2:T(8,128)S(1)}, f32[32,32,1]{1,0,2:T(8,128)}, u32[]{:S(2)}) copy-start(f32[32,32,1]{1,0,2:T(8,128)} %constant.80) | copy-start | bytes 12292
  36.4 43.8 %collective-permute-start.3 = (f32[10,128]{1,0:T(8,128)S(1)}, f32[10,128]{1,0:T(8,128)S(1)}, u32[]{:S(2)}, u32[]{:S(2)}) collective-permute-start(f32[10,128]{1,0:T(8,128)S(1)} %reshape.159), channel_id=1, source_target_pairs={{0,1},{1,2},{2,3},{3,4},{4,5},{5,6},{6,7},{7,8},{8,9},{9,10},{10,1... | collective-permute-start | bytes 15368 | tf_op jit(solution)/shard_map/ppermute | solution.py:202
  55.6 0.8 copy-start.4
  56.4 0.8 copy-start.3
  60.3 87.3 %all-to-all-start.2 = ((f32[1,32,16,128]{3,2,0,1:T(8,128)}), f32[1,32,16,128]{3,2,0,1:T(8,128)S(1)}, u32[]{:S(2)}, u32[]{:S(2)}) async-start(f32[1,32,16,128]{3,2,0,1:T(8,128)} %copy.42), calls=%async_computation.2 | async-start | bytes 524288 | tf_op jit(solution)/shard_map/all_to_all | solution.py:184
  66.5 14.3 %collective-permute-start.1 = (f32[40,128]{1,0:T(8,128)S(1)}, f32[40,128]{1,0:T(8,128)S(1)}, u32[]{:S(2)}, u32[]{:S(2)}) collective-permute-start(f32[40,128]{1,0:T(8,128)S(1)} %bitcast.95), channel_id=1, source_target_pairs={{0,32},{32,64},{64,96},{96,128},{128,160},{160,192},{192,224},{224... | collective-permute-start | bytes 61448 | tf_op jit(solution)/shard_map/ppermute | solution.py:202
  70.3 10.5 %collective-permute-start = (f32[40,128]{1,0:T(8,128)S(1)}, f32[40,128]{1,0:T(8,128)S(1)}, u32[]{:S(2)}, u32[]{:S(2)}) collective-permute-start(f32[40,128]{1,0:T(8,128)S(1)} %bitcast.94), channel_id=1, source_target_pairs={{32,0},{64,32},{96,64},{128,96},{160,128},{192,160},{224,192},{256... | collective-permute-start | bytes 61448 | tf_op jit(solution)/shard_map/ppermute | solution.py:203
  72.4 8.1 %collective-permute-start.2 = (f32[10,128]{1,0:T(8,128)S(1)}, f32[10,128]{1,0:T(8,128)S(1)}, u32[]{:S(2)}, u32[]{:S(2)}) collective-permute-start(f32[10,128]{1,0:T(8,128)S(1)} %reshape.157), channel_id=1, source_target_pairs={{1,0},{2,1},{3,2},{4,3},{5,4},{6,5},{7,6},{8,7},{9,8},{10,9},{11,1... | collective-permute-start | bytes 15368 | tf_op jit(solution)/shard_map/ppermute | solution.py:203
  81.0 66.5 %copy-start.1 = (f32[512,512]{1,0:T(8,128)S(1)}, f32[512,512]{1,0:T(8,128)}, u32[]{:S(2)}) copy-start(f32[512,512]{1,0:T(8,128)} %constant.68.clone) | copy-start | bytes 3145732
  149.2 22.2 %copy-start.12 = (f32[2]{0:T(128)S(1)}, f32[2]{0:T(128)}, u32[]{:S(2)}) copy-start(f32[2]{0:T(128)} %param.20) | copy-start | bytes 28
  149.2 30.0 %all-to-all-start.3 = ((f32[1,16,40,128]{3,2,0,1:T(8,128)}), f32[1,16,40,128]{3,2,0,1:T(8,128)S(1)}, u32[]{:S(2)}, u32[]{:S(2)}) async-start(f32[1,16,40,128]{3,2,0,1:T(8,128)} %maximum_bitcast_fusion), calls=%async_computation.3 | async-start | bytes 655360 | tf_op jit(solution)/shard_map/all_to_all | solution.py:189
  179.3 0.9 copy-start.7
  179.4 1.0 copy-start.6

commit v6 on v4

--- a/solution.py
+++ b/solution.py
@@ -159,9 +159,9 @@
 
 def with_sums(data, sums, dim):
     shape = list(data.shape)
-    shape[dim] = 8
-    tile = jnp.zeros((8, data.shape[-1]), jnp.float32).at[0, 0 : sums.shape[0]].set(sums)
-    return jnp.concatenate([data, jnp.broadcast_to(tile.reshape([1] * (data.ndim - 2) + [8, -1]), shape)], axis=dim)
+    shape[dim] = 1
+    row = jnp.zeros((1, data.shape[-1]), jnp.float32).at[0, 0 : sums.shape[0]].set(sums)
+    return jnp.concatenate([data, jnp.broadcast_to(row.reshape([1] * (data.ndim - 2) + [1, -1]), shape)], axis=dim)
 
 
 def convolve_and_sum(source, interaction, local_sums, after_transform, primitive_tile_total):

time: 123 us -> 119 us (0.967)
  blocking collectives: 34.2 us -> 30.2 us
  other arithmetic: 9.26 us -> 10.7 us
    all_to_all x1, blocking collectives: 34.2 us -> 30.2 us  [convolve_and_sum(): lax.all_to_all(back_y, 'ky', split_axis=1, concat_axis=1, tiled=True)]
    reshape x1 -> x2, other arithmetic: 1.97 us -> 3.19 us  [with_sums(): row.reshape([1] * (data.ndim - 2) + [1, -1])]
  transfers between devices with their start and end apart: 7 -> 7, of which waited for: 3 -> 2; matrix products, arithmetic and copies ran while one was open for 5% -> 6% of each run, Pallas kernels for 0% -> 0%
where the time goes in v6:
time: 119 us; the launch traced here: 118 us
  starting transfers between devices  49.7 us (42%)
  blocking collectives  30.2 us (25%)
  waiting for transfers between devices  12.9 us (11%)
  other arithmetic  10.7 us (9%)
  matrix products  7.18 us (6%)
  local copies, waits for them, and re-layouts  6.54 us (5%)
  between operations  1.2 us (1%)
    all_to_all x1, blocking collectives, convolve_and_sum(): lax.all_to_all(back_y, 'ky', split_axis=1, concat_axis=1, tiled=True)  30.2 us
    all_to_all x1, starting transfers between devices, convolve_and_sum(): lax.all_to_all(split, 'ky', split_axis=1, concat_axis=1, tiled=True)  14 us
    all_to_all x1, starting transfers between devices, convolve_and_sum(): back = lax.all_to_all(final, 'kx', split_axis=1, concat_axis=0, tiled=True)  11 us
    all_to_all x1, starting transfers between devices, convolve_and_sum(): lax.all_to_all(source, 'kx', split_axis=0, concat_axis=1, tiled=True)  10.3 us
    ppermute x2, starting transfers between devices, neighbours(): before = lax.ppermute(last.reshape(dense), axis, up).reshape(last.shape)  7.3 us
    dot_general x10, matrix products, contract(): jnp.einsum(einsum_form, left, right, precision=lax.Precision.HIGHEST, pre...  7.18 us
    ppermute x2, starting transfers between devices, neighbours(): lax.ppermute(initial.reshape(dense), axis, down).reshape(initial.shape)  6.96 us
    all_to_all x1, waiting for transfers between devices, convolve_and_sum(): back = lax.all_to_all(final, 'kx', split_axis=1, concat_axis=0, tiled=True)  6.62 us
  transfers between devices with their start and end apart: 7, of which 2 were waited for; matrix products, arithmetic and copies ran while one was open for 6% of the time, Pallas kernels for 0%

profile of v6, /device:TPU:1, one launch (start us, length us, event | category | flops | bytes accessed | tf_op | source)
XLA Modules:
  0.0 118.4 jit_solution(2294306501772013355)
XLA Ops:
  0.6 10.3 %all-to-all-start = ((f32[16,32,128]{2,1,0:T(8,128)}), f32[16,32,128]{2,1,0:T(8,128)S(1)}, u32[]{:S(2)}, u32[]{:S(2)}) async-start(f32[16,32,128]{2,1,0:T(8,128)} %param.17), calls=%async_computation | async-start | bytes 524288 | tf_op jit(solution)/shard_map/all_to_all | solution.py:171
  11.0 0.9 copy-done
  12.0 6.2 %all-to-all-done = f32[16,32,128]{2,1,0:T(8,128)S(1)} async-done(((f32[16,32,128]{2,1,0:T(8,128)}), f32[16,32,128]{2,1,0:T(8,128)S(1)}, u32[]{:S(2)}, u32[]{:S(2)}) %all-to-all-start) | async-done | bytes 262176 | tf_op jit(solution)/shard_map/all_to_all | solution.py:171
  18.2 2.9 %convolution_bitcast_fusion.2 = f32[1,512,128]{2,1,0:T(8,128)} fusion(f32[512,512]{1,0:T(8,128)} %constant.89.clone, f32[512,128]{1,0:T(8,128)S(1)} %bitcast.95), kind=kOutput, calls=%fused_computation.9 | convolution fusion | flops 402653184 | bytes 1572864 | tf_op jit(solution)/shard_map/px,cxy->cpy/dot_general | solution.py:109
  21.3 14.0 %all-to-all-start.1 = ((f32[1,32,16,128]{3,2,0,1:T(8,128)}), f32[1,32,16,128]{3,2,0,1:T(8,128)S(1)}, u32[]{:S(2)}, u32[]{:S(2)}) async-start(f32[1,32,16,128]{3,2,0,1:T(8,128)} %bitcast.5), calls=%async_computation.1 | async-start | bytes 524288 | tf_op jit(solution)/shard_map/all_to_all | solution.py:178
  35.6 4.6 %collective-permute-start.3 = (f32[10,128]{1,0:T(8,128)S(1)}, f32[10,128]{1,0:T(8,128)S(1)}, u32[]{:S(2)}, u32[]{:S(2)}) collective-permute-start(f32[10,128]{1,0:T(8,128)S(1)} %reshape.228), channel_id=1, source_target_pairs={{0,1},{1,2},{2,3},{3,4},{4,5},{5,6},{6,7},{7,8},{8,9},{9,10},{10,1... | collective-permute-start | bytes 15368 | tf_op jit(solution)/shard_map/ppermute | solution.py:202
  40.2 2.7 %collective-permute-start.1 = (f32[40,128]{1,0:T(8,128)S(1)}, f32[40,128]{1,0:T(8,128)S(1)}, u32[]{:S(2)}, u32[]{:S(2)}) collective-permute-start(f32[40,128]{1,0:T(8,128)S(1)} %bitcast.99), channel_id=1, source_target_pairs={{0,32},{32,64},{64,96},{96,128},{128,160},{160,192},{192,224},{224... | collective-permute-start | bytes 61448 | tf_op jit(solution)/shard_map/ppermute | solution.py:202
  42.9 3.0 %collective-permute-start = (f32[40,128]{1,0:T(8,128)S(1)}, f32[40,128]{1,0:T(8,128)S(1)}, u32[]{:S(2)}, u32[]{:S(2)}) collective-permute-start(f32[40,128]{1,0:T(8,128)S(1)} %bitcast.98), channel_id=1, source_target_pairs={{32,0},{64,32},{96,64},{128,96},{160,128},{192,160},{224,192},{256... | collective-permute-start | bytes 61448 | tf_op jit(solution)/shard_map/ppermute | solution.py:203
  46.1 4.0 %collective-permute-start.2 = (f32[10,128]{1,0:T(8,128)S(1)}, f32[10,128]{1,0:T(8,128)S(1)}, u32[]{:S(2)}, u32[]{:S(2)}) collective-permute-start(f32[10,128]{1,0:T(8,128)S(1)} %reshape.226), channel_id=1, source_target_pairs={{1,0},{2,1},{3,2},{4,3},{5,4},{6,5},{7,6},{8,7},{9,8},{10,9},{11,1... | collective-permute-start | bytes 15368 | tf_op jit(solution)/shard_map/ppermute | solution.py:203
  50.1 0.6 add_reduce_fusion
  51.4 0.6 compare_reduce_fusion
  53.3 0.6 fusion.31
  54.0 2.5 %broadcast_select_fusion.1 = f32[1,1,1,3]{3,2,1,0:T(1,128)S(1)} fusion(pred[]{:T(512)} %compare_reduce_fusion, f32[1,1,1,1]{3,2,1,0:T(1,128)} %bitcast.30, f32[1,1,1,1]{3,2,1,0:T(1,128)} %bitcast.29, f32[1,1,1,1]{3,2,1,0:T(1,128)} %bitcast.24), kind=kLoop, calls=%fused_computation.91 | loop fusion | flops 9 | bytes 25 | tf_op jit(solution)/shard_map/reshape | solution.py:164
  61.5 30.2 %all_to_all.31 = f32[1,32,17,128]{3,0,2,1:T(1,128)S(1)} all-to-all(f32[1,32,17,128]{3,0,2,1:T(1,128)S(1)} %copy.56), channel_id=1, replica_groups=mesh['kx'=16,'ky'=32] {'ky'}, dimensions={1} | all-to-all | bytes 557056 | tf_op jit(solution)/shard_map/all_to_all | solution.py:183
  91.7 0.6 fusion.32
  92.4 0.8 convolution_bitcast_fusion
  93.4 1.0 copy.59
  94.3 11.0 %all-to-all-start.3 = ((f32[1,16,33,128]{3,0,2,1:T(1,128)}), f32[1,16,33,128]{3,0,2,1:T(1,128)S(1)}, u32[]{:S(2)}, u32[]{:S(2)}) async-start(f32[1,16,33,128]{3,0,2,1:T(1,128)} %copy.59), calls=%async_computation.3 | async-start | bytes 540672 | tf_op jit(solution)/shard_map/all_to_all | solution.py:189
  105.4 0.6 fusion.35
  106.0 6.6 %all-to-all-done.3 = f32[1,16,33,128]{3,0,2,1:T(1,128)S(1)} async-done(((f32[1,16,33,128]{3,0,2,1:T(1,128)}), f32[1,16,33,128]{3,0,2,1:T(1,128)S(1)}, u32[]{:S(2)}, u32[]{:S(2)}) %all-to-all-start.3) | async-done | bytes 270368 | tf_op jit(solution)/shard_map/all_to_all | solution.py:189
  113.1 0.6 copy-done.6
  113.8 1.3 %fusion.29 = f32[12,32,128]{2,1,0:T(8,128)S(1)} fusion(f32[16,1,32,128]{3,2,0,1:T(8,128)S(1)} %bitcast.94, f32[12,32,128]{2,1,0:T(8,128)S(1)} %copy-done.6, f32[12,32,128]{2,1,0:T(8,128)S(1)} %copy-done.7, f32[]{:T(128)} %bitcast.43, f32[]{:T(128)} %bitcast.42), kind=kLoop, calls=%fused_computation.58 | loop fusion | flops 196608 | bytes 786440 | tf_op jit(solution)/shard_map/add | solution.py:101
  115.7 1.3 %fusion.16 = f32[16,32,128]{2,1,0:T(8,128)S(1)} fusion(f32[20,32,128]{2,1,0:T(8,128)S(1)} %fusion.13, f32[16,32,128]{2,1,0:T(8,128)S(1)} %constant_dynamic-update-slice_fusion.2, f32[20,32,128]{2,1,0:T(8,128)S(1)} %get-tuple-element.36, f32[]{:T(128)} %bitcast.43, f32[]{:T(128)} %bitcast.42), kind=kLoop, calls=%fused_computation.36 | loop fusion | flops 262144 | bytes 1048584 | tf_op jit(solution)/shard_map/add | solution.py:104
  117.7 0.7 pad_maximum_fusion.6
  (84 shorter events, 9.2 us)
Async XLA Ops:
  0.6 10.4 %copy-start.5 = (f32[16,4096]{1,0:T(8,128)S(1)}, f32[16,4096]{1,0:T(8,128)}, u32[]{:S(2)}) copy-start(f32[16,4096]{1,0:T(8,128)} %param.21) | copy-start | bytes 786436
  0.6 17.6 %all-to-all-start = ((f32[16,32,128]{2,1,0:T(8,128)}), f32[16,32,128]{2,1,0:T(8,128)S(1)}, u32[]{:S(2)}, u32[]{:S(2)}) async-start(f32[16,32,128]{2,1,0:T(8,128)} %param.17), calls=%async_computation | async-start | bytes 524288 | tf_op jit(solution)/shard_map/all_to_all | solution.py:171
  11.0 1.0 copy-start
  11.0 1.0 copy-start.2
  21.3 35.3 %all-to-all-start.1 = ((f32[1,32,16,128]{3,2,0,1:T(8,128)}), f32[1,32,16,128]{3,2,0,1:T(8,128)S(1)}, u32[]{:S(2)}, u32[]{:S(2)}) async-start(f32[1,32,16,128]{3,2,0,1:T(8,128)} %bitcast.5), calls=%async_computation.1 | async-start | bytes 524288 | tf_op jit(solution)/shard_map/all_to_all | solution.py:178
  35.6 16.5 %collective-permute-start.3 = (f32[10,128]{1,0:T(8,128)S(1)}, f32[10,128]{1,0:T(8,128)S(1)}, u32[]{:S(2)}, u32[]{:S(2)}) collective-permute-start(f32[10,128]{1,0:T(8,128)S(1)} %reshape.228), channel_id=1, source_target_pairs={{0,1},{1,2},{2,3},{3,4},{4,5},{5,6},{6,7},{7,8},{8,9},{9,10},{10,1... | collective-permute-start | bytes 15368 | tf_op jit(solution)/shard_map/ppermute | solution.py:202
  40.2 12.4 %collective-permute-start.1 = (f32[40,128]{1,0:T(8,128)S(1)}, f32[40,128]{1,0:T(8,128)S(1)}, u32[]{:S(2)}, u32[]{:S(2)}) collective-permute-start(f32[40,128]{1,0:T(8,128)S(1)} %bitcast.99), channel_id=1, source_target_pairs={{0,32},{32,64},{64,96},{96,128},{128,160},{160,192},{192,224},{224... | collective-permute-start | bytes 61448 | tf_op jit(solution)/shard_map/ppermute | solution.py:202
  42.9 9.7 %collective-permute-start = (f32[40,128]{1,0:T(8,128)S(1)}, f32[40,128]{1,0:T(8,128)S(1)}, u32[]{:S(2)}, u32[]{:S(2)}) collective-permute-start(f32[40,128]{1,0:T(8,128)S(1)} %bitcast.98), channel_id=1, source_target_pairs={{32,0},{64,32},{96,64},{128,96},{160,128},{192,160},{224,192},{256... | collective-permute-start | bytes 61448 | tf_op jit(solution)/shard_map/ppermute | solution.py:203
  46.1 6.2 %collective-permute-start.2 = (f32[10,128]{1,0:T(8,128)S(1)}, f32[10,128]{1,0:T(8,128)S(1)}, u32[]{:S(2)}, u32[]{:S(2)}) collective-permute-start(f32[10,128]{1,0:T(8,128)S(1)} %reshape.226), channel_id=1, source_target_pairs={{1,0},{2,1},{3,2},{4,3},{5,4},{6,5},{7,6},{8,7},{9,8},{10,9},{11,1... | collective-permute-start | bytes 15368 | tf_op jit(solution)/shard_map/ppermute | solution.py:203
  53.3 3.2 %copy-start.11 = (f32[32,32,1]{1,0,2:T(8,128)S(1)}, f32[32,32,1]{1,0,2:T(8,128)}, u32[]{:S(2)}) copy-start(f32[32,32,1]{1,0,2:T(8,128)} %constant.104) | copy-start | bytes 12292
  56.5 0.7 copy-start.8
  56.5 0.7 copy-start.9
  56.5 0.7 copy-start.10
  57.3 0.8 copy-start.4
  58.1 0.8 copy-start.3
  61.1 31.3 %copy-start.1 = (f32[512,512]{1,0:T(8,128)S(1)}, f32[512,512]{1,0:T(8,128)}, u32[]{:S(2)}) copy-start(f32[512,512]{1,0:T(8,128)} %constant.89.clone) | copy-start | bytes 3145732
  94.3 11.1 %copy-start.12 = (f32[2]{0:T(128)S(1)}, f32[2]{0:T(128)}, u32[]{:S(2)}) copy-start(f32[2]{0:T(128)} %param.22) | copy-start | bytes 28
  94.3 18.3 %all-to-all-start.3 = ((f32[1,16,33,128]{3,0,2,1:T(1,128)}), f32[1,16,33,128]{3,0,2,1:T(1,128)S(1)}, u32[]{:S(2)}, u32[]{:S(2)}) async-start(f32[1,16,33,128]{3,0,2,1:T(1,128)} %copy.59), calls=%async_computation.3 | async-start | bytes 540672 | tf_op jit(solution)/shard_map/all_to_all | solution.py:189
  112.7 0.9 copy-start.6
  112.8 1.0 copy-start.7

commit v7 on v6

--- a/solution.py
+++ b/solution.py
@@ -218,9 +218,8 @@
         return rows_x
 
     def local_sums():
-        stacked = halo_source[0]
-        column_core = neighbours(stacked, "kx", 1, 2)
-        row_core = neighbours(stacked, "ky", 2, 2)
+        column_core = neighbours(jnp.concatenate([packed_state_matrix, energies]), "kx", 1, 2)
+        row_core = neighbours(halo_source[0], "ky", 2, 2)
         gradient_x = (
             8.0 * (column_core[:, 3:-1] - column_core[:, 1:-3])
             - (column_core[:, 4:] - column_core[:, :-4])

time: 119 us -> 119 us (level)
  local copies, waits for them, and re-layouts: 6.54 us -> 8.9 us
  blocking collectives: 30.2 us -> 28.3 us
  matrix products: 7.18 us -> 5.97 us
    ppermute x2, waiting for transfers between devices: 0.01 us -> 6.65 us  [neighbours(): before = lax.ppermute(last.reshape(dense), axis, up).reshape(last.shape)]
    all_to_all x1, waiting for transfers between devices: 6.23 us -> 0.01 us  [convolve_and_sum(): lax.all_to_all(source, 'kx', split_axis=0, concat_axis=1, tiled=True)]
    ppermute x2, starting transfers between devices: 6.96 us -> 8.98 us  [neighbours(): lax.ppermute(initial.reshape(dense), axis, down).reshape(initial.shape)]
    ppermute x2, starting transfers between devices: 7.3 us -> 5.35 us  [neighbours(): before = lax.ppermute(last.reshape(dense), axis, up).reshape(last.shape)]
    all_to_all x1, blocking collectives: 30.2 us -> 28.3 us  [convolve_and_sum(): lax.all_to_all(back_y, 'ky', split_axis=1, concat_axis=1, tiled=True)]
    dot_general x10, matrix products: 7.18 us -> 5.97 us  [contract(): jnp.einsum(einsum_form, left, right, precision=lax.Precision.HIGHEST, pre...]
    unnamed x26 -> x32, local copies, waits for them, and re-layouts: 2.67 us -> 3.61 us
  transfers between devices with their start and end apart: 7 -> 7, of which waited for: 2 -> 3; matrix products, arithmetic and copies ran while one was open for 6% -> 8% of each run, Pallas kernels for 0% -> 0%
where the time goes in v7:
time: 119 us; the launch traced here: 118 us
  starting transfers between devices  49.5 us (42%)
  blocking collectives  28.3 us (24%)
  waiting for transfers between devices  13.3 us (11%)
  other arithmetic  10.7 us (9%)
  local copies, waits for them, and re-layouts  8.9 us (7%)
  matrix products  5.97 us (5%)
  between operations  1.19 us (1%)
    all_to_all x1, blocking collectives, convolve_and_sum(): lax.all_to_all(back_y, 'ky', split_axis=1, concat_axis=1, tiled=True)  28.3 us
    all_to_all x1, starting transfers between devices, convolve_and_sum(): lax.all_to_all(split, 'ky', split_axis=1, concat_axis=1, tiled=True)  14 us
    all_to_all x1, starting transfers between devices, convolve_and_sum(): back = lax.all_to_all(final, 'kx', split_axis=1, concat_axis=0, tiled=True)  10.9 us
    all_to_all x1, starting transfers between devices, convolve_and_sum(): lax.all_to_all(source, 'kx', split_axis=0, concat_axis=1, tiled=True)  10.3 us
    ppermute x2, starting transfers between devices, neighbours(): lax.ppermute(initial.reshape(dense), axis, down).reshape(initial.shape)  8.98 us
    ppermute x2, waiting for transfers between devices, neighbours(): before = lax.ppermute(last.reshape(dense), axis, up).reshape(last.shape)  6.65 us
    all_to_all x1, waiting for transfers between devices, convolve_and_sum(): back = lax.all_to_all(final, 'kx', split_axis=1, concat_axis=0, tiled=True)  6.61 us
    dot_general x10, matrix products, contract(): jnp.einsum(einsum_form, left, right, precision=lax.Precision.HIGHEST, pre...  5.97 us
  transfers between devices with their start and end apart: 7, of which 3 were waited for; matrix products, arithmetic and copies ran while one was open for 8% of the time, Pallas kernels for 0%

profile of v7, /device:TPU:1, one launch (start us, length us, event | category | flops | bytes accessed | tf_op | source)
XLA Modules:
  0.0 117.9 jit_solution(17498953330710789125)
XLA Ops:
  0.6 10.3 %all-to-all-start = ((f32[16,32,128]{2,1,0:T(8,128)}), f32[16,32,128]{2,1,0:T(8,128)S(1)}, u32[]{:S(2)}, u32[]{:S(2)}) async-start(f32[16,32,128]{2,1,0:T(8,128)} %param.17), calls=%async_computation | async-start | bytes 524288 | tf_op jit(solution)/shard_map/all_to_all | solution.py:171
  11.0 0.8 copy-done.6
  11.9 2.1 %collective-permute-start = (f32[40,128]{1,0:T(8,128)S(1)}, f32[40,128]{1,0:T(8,128)S(1)}, u32[]{:S(2)}, u32[]{:S(2)}) collective-permute-start(f32[40,128]{1,0:T(8,128)S(1)} %bitcast.101), channel_id=1, source_target_pairs={{32,0},{64,32},{96,64},{128,96},{160,128},{192,160},{224,192},{256... | collective-permute-start | bytes 61448 | tf_op jit(solution)/shard_map/ppermute | solution.py:203
  14.0 3.4 %collective-permute-start.1 = (f32[40,128]{1,0:T(8,128)S(1)}, f32[40,128]{1,0:T(8,128)S(1)}, u32[]{:S(2)}, u32[]{:S(2)}) collective-permute-start(f32[40,128]{1,0:T(8,128)S(1)} %bitcast.100), channel_id=1, source_target_pairs={{0,32},{32,64},{64,96},{96,128},{128,160},{160,192},{192,224},{224... | collective-permute-start | bytes 61448 | tf_op jit(solution)/shard_map/ppermute | solution.py:202
  18.5 1.0 copy.51
  19.5 0.6 compare_reduce_fusion
  20.5 1.7 %convolution_bitcast_fusion.2 = f32[1,512,128]{2,1,0:T(8,128)} fusion(f32[512,512]{1,0:T(8,128)S(1)} %copy-done.1, f32[512,128]{1,0:T(8,128)S(1)} %bitcast.95), kind=kOutput, calls=%fused_computation.9 | convolution fusion | flops 402653184 | bytes 1572864 | tf_op jit(solution)/shard_map/px,cxy->cpy/dot_general | solution.py:109
  22.2 14.0 %all-to-all-start.1 = ((f32[1,32,16,128]{3,2,0,1:T(8,128)}), f32[1,32,16,128]{3,2,0,1:T(8,128)S(1)}, u32[]{:S(2)}, u32[]{:S(2)}) async-start(f32[1,32,16,128]{3,2,0,1:T(8,128)} %bitcast.5), calls=%async_computation.1 | async-start | bytes 524288 | tf_op jit(solution)/shard_map/all_to_all | solution.py:178
  36.6 6.8 %collective-permute-start.2 = (f32[10,128]{1,0:T(8,128)S(1)}, f32[10,128]{1,0:T(8,128)S(1)}, u32[]{:S(2)}, u32[]{:S(2)}) collective-permute-start(f32[10,128]{1,0:T(8,128)S(1)} %reshape.226), channel_id=1, source_target_pairs={{1,0},{2,1},{3,2},{4,3},{5,4},{6,5},{7,6},{8,7},{9,8},{10,9},{11,1... | collective-permute-start | bytes 15368 | tf_op jit(solution)/shard_map/ppermute | solution.py:203
  43.7 1.9 %collective-permute-start.3 = (f32[10,128]{1,0:T(8,128)S(1)}, f32[10,128]{1,0:T(8,128)S(1)}, u32[]{:S(2)}, u32[]{:S(2)}) collective-permute-start(f32[10,128]{1,0:T(8,128)S(1)} %reshape.228), channel_id=1, source_target_pairs={{0,1},{1,2},{2,3},{3,4},{4,5},{5,6},{6,7},{7,8},{8,9},{9,10},{10,1... | collective-permute-start | bytes 15368 | tf_op jit(solution)/shard_map/ppermute | solution.py:202
  45.9 6.4 %collective-permute-done.3 = f32[10,128]{1,0:T(8,128)S(1)} collective-permute-done((f32[10,128]{1,0:T(8,128)S(1)}, f32[10,128]{1,0:T(8,128)S(1)}, u32[]{:S(2)}, u32[]{:S(2)}) %collective-permute-start.3) | collective-permute-done | bytes 5152 | tf_op jit(solution)/shard_map/ppermute | solution.py:202
  52.3 1.0 reshape.229
  53.4 0.9 copy-done.2
  54.8 0.7 fusion.31
  55.5 2.5 %broadcast_select_fusion.1 = f32[1,1,1,3]{3,2,1,0:T(1,128)S(1)} fusion(pred[]{:T(512)} %compare_reduce_fusion, f32[1,1,1,1]{3,2,1,0:T(1,128)} %bitcast.30, f32[1,1,1,1]{3,2,1,0:T(1,128)} %bitcast.29, f32[1,1,1,1]{3,2,1,0:T(1,128)} %bitcast.24), kind=kLoop, calls=%fused_computation.92 | loop fusion | flops 9 | bytes 25 | tf_op jit(solution)/shard_map/reshape | solution.py:164
  63.0 28.3 %all_to_all.31 = f32[1,32,17,128]{3,0,2,1:T(1,128)S(1)} all-to-all(f32[1,32,17,128]{3,0,2,1:T(1,128)S(1)} %copy.56), channel_id=1, replica_groups=mesh['kx'=16,'ky'=32] {'ky'}, dimensions={1} | all-to-all | bytes 557056 | tf_op jit(solution)/shard_map/all_to_all | solution.py:183
  91.4 0.8 convolution_bitcast_fusion
  92.4 0.7 fusion.32
  93.1 1.0 copy.59
  94.1 10.9 %all-to-all-start.3 = ((f32[1,16,33,128]{3,0,2,1:T(1,128)}), f32[1,16,33,128]{3,0,2,1:T(1,128)S(1)}, u32[]{:S(2)}, u32[]{:S(2)}) async-start(f32[1,16,33,128]{3,0,2,1:T(1,128)} %copy.59), calls=%async_computation.3 | async-start | bytes 540672 | tf_op jit(solution)/shard_map/all_to_all | solution.py:189
  105.6 6.6 %all-to-all-done.3 = f32[1,16,33,128]{3,0,2,1:T(1,128)S(1)} async-done(((f32[1,16,33,128]{3,0,2,1:T(1,128)}), f32[1,16,33,128]{3,0,2,1:T(1,128)S(1)}, u32[]{:S(2)}, u32[]{:S(2)}) %all-to-all-start.3) | async-done | bytes 270368 | tf_op jit(solution)/shard_map/all_to_all | solution.py:189
  113.3 1.3 %fusion.29 = f32[12,32,128]{2,1,0:T(8,128)S(1)} fusion(f32[16,1,32,128]{3,2,0,1:T(8,128)S(1)} %bitcast.94, f32[12,32,128]{2,1,0:T(8,128)S(1)} %copy-done.8, f32[12,32,128]{2,1,0:T(8,128)S(1)} %copy-done.9, f32[]{:T(128)} %bitcast.43, f32[]{:T(128)} %bitcast.42), kind=kLoop, calls=%fused_computation.57 | loop fusion | flops 196608 | bytes 786440 | tf_op jit(solution)/shard_map/add | solution.py:101
  115.2 1.3 %fusion.16 = f32[16,32,128]{2,1,0:T(8,128)S(1)} fusion(f32[20,32,128]{2,1,0:T(8,128)S(1)} %fusion.13, f32[16,32,128]{2,1,0:T(8,128)S(1)} %constant_dynamic-update-slice_fusion.4, f32[20,32,128]{2,1,0:T(8,128)S(1)} %fusion.7, f32[]{:T(128)} %bitcast.43, f32[]{:T(128)} %bitcast.42), kind=kLoop, calls=%fused_computation.35 | loop fusion | flops 262144 | bytes 1048584 | tf_op jit(solution)/shard_map/add | solution.py:104
  117.2 0.7 pad_maximum_fusion.5
  (90 shorter events, 10.8 us)
Async XLA Ops:
  0.6 10.4 %copy-start = (f32[16,32,128]{2,1,0:T(8,128)S(1)}, f32[16,32,128]{2,1,0:T(8,128)}, u32[]{:S(2)}) copy-start(f32[16,32,128]{2,1,0:T(8,128)} %param.17) | copy-start | bytes 786436
  0.6 19.9 %all-to-all-start = ((f32[16,32,128]{2,1,0:T(8,128)}), f32[16,32,128]{2,1,0:T(8,128)S(1)}, u32[]{:S(2)}, u32[]{:S(2)}) async-start(f32[16,32,128]{2,1,0:T(8,128)} %param.17), calls=%async_computation | async-start | bytes 524288 | tf_op jit(solution)/shard_map/all_to_all | solution.py:171
  11.0 0.8 copy-start.6
  11.0 6.4 %copy-start.7 = (f32[16,4096]{1,0:T(8,128)S(1)}, f32[16,4096]{1,0:T(8,128)}, u32[]{:S(2)}) copy-start(f32[16,4096]{1,0:T(8,128)} %param.21) | copy-start | bytes 786436
  11.9 8.2 %collective-permute-start = (f32[40,128]{1,0:T(8,128)S(1)}, f32[40,128]{1,0:T(8,128)S(1)}, u32[]{:S(2)}, u32[]{:S(2)}) collective-permute-start(f32[40,128]{1,0:T(8,128)S(1)} %bitcast.101), channel_id=1, source_target_pairs={{32,0},{64,32},{96,64},{128,96},{160,128},{192,160},{224,192},{256... | collective-permute-start | bytes 61448 | tf_op jit(solution)/shard_map/ppermute | solution.py:203
  14.0 6.3 %collective-permute-start.1 = (f32[40,128]{1,0:T(8,128)S(1)}, f32[40,128]{1,0:T(8,128)S(1)}, u32[]{:S(2)}, u32[]{:S(2)}) collective-permute-start(f32[40,128]{1,0:T(8,128)S(1)} %bitcast.100), channel_id=1, source_target_pairs={{0,32},{32,64},{64,96},{96,128},{128,160},{160,192},{192,224},{224... | collective-permute-start | bytes 61448 | tf_op jit(solution)/shard_map/ppermute | solution.py:202
  18.4 2.1 %copy-start.1 = (f32[512,512]{1,0:T(8,128)S(1)}, f32[512,512]{1,0:T(8,128)}, u32[]{:S(2)}) copy-start(f32[512,512]{1,0:T(8,128)} %constant.89.clone) | copy-start | bytes 3145732
  22.2 35.8 %all-to-all-start.1 = ((f32[1,32,16,128]{3,2,0,1:T(8,128)}), f32[1,32,16,128]{3,2,0,1:T(8,128)S(1)}, u32[]{:S(2)}, u32[]{:S(2)}) async-start(f32[1,32,16,128]{3,2,0,1:T(8,128)} %bitcast.5), calls=%async_computation.1 | async-start | bytes 524288 | tf_op jit(solution)/shard_map/all_to_all | solution.py:178
  36.6 9.0 %collective-permute-start.2 = (f32[10,128]{1,0:T(8,128)S(1)}, f32[10,128]{1,0:T(8,128)S(1)}, u32[]{:S(2)}, u32[]{:S(2)}) collective-permute-start(f32[10,128]{1,0:T(8,128)S(1)} %reshape.226), channel_id=1, source_target_pairs={{1,0},{2,1},{3,2},{4,3},{5,4},{6,5},{7,6},{8,7},{9,8},{10,9},{11,1... | collective-permute-start | bytes 15368 | tf_op jit(solution)/shard_map/ppermute | solution.py:203
  43.7 8.7 %collective-permute-start.3 = (f32[10,128]{1,0:T(8,128)S(1)}, f32[10,128]{1,0:T(8,128)S(1)}, u32[]{:S(2)}, u32[]{:S(2)}) collective-permute-start(f32[10,128]{1,0:T(8,128)S(1)} %reshape.228), channel_id=1, source_target_pairs={{0,1},{1,2},{2,3},{3,4},{4,5},{5,6},{6,7},{7,8},{8,9},{9,10},{10,1... | collective-permute-start | bytes 15368 | tf_op jit(solution)/shard_map/ppermute | solution.py:202
  53.3 1.0 copy-start.2
  54.8 3.3 %copy-start.13 = (f32[32,32,1]{1,0,2:T(8,128)S(1)}, f32[32,32,1]{1,0,2:T(8,128)}, u32[]{:S(2)}) copy-start(f32[32,32,1]{1,0,2:T(8,128)} %constant.104) | copy-start | bytes 12292
  58.0 0.7 copy-start.10
  58.0 0.7 copy-start.11
  58.0 0.7 copy-start.12
  58.8 0.8 copy-start.5
  59.6 0.9 copy-start.3
  59.6 1.0 copy-start.4
  94.1 10.9 %copy-start.14 = (f32[2]{0:T(128)S(1)}, f32[2]{0:T(128)}, u32[]{:S(2)}) copy-start(f32[2]{0:T(128)} %param.22) | copy-start | bytes 28
  94.1 18.1 %all-to-all-start.3 = ((f32[1,16,33,128]{3,0,2,1:T(1,128)}), f32[1,16,33,128]{3,0,2,1:T(1,128)S(1)}, u32[]{:S(2)}, u32[]{:S(2)}) async-start(f32[1,16,33,128]{3,0,2,1:T(1,128)} %copy.59), calls=%async_computation.3 | async-start | bytes 540672 | tf_op jit(solution)/shard_map/all_to_all | solution.py:189
  112.3 0.9 copy-start.8
  112.3 1.0 copy-start.9

commit v8 on v7

--- a/solution.py
+++ b/solution.py
@@ -10,6 +10,7 @@
 DEPHASING = 0.5
 SHIELDING_LEVEL = 2.0
 COUPLING = 40.0
+KY = ("kz", "kh")
 
 
 def unpack(packed):
@@ -164,9 +165,18 @@
     return jnp.concatenate([data, jnp.broadcast_to(row.reshape([1] * (data.ndim - 2) + [1, -1]), shape)], axis=dim)
 
 
+def ky_exchange(data, order):
+    shape = data.shape
+    split = data.reshape(shape[0], lax.axis_size("kz"), lax.axis_size("kh"), *shape[2:])
+    for axis in order:
+        dim = 1 if axis == "kz" else 2
+        split = lax.all_to_all(split, axis, split_axis=dim, concat_axis=dim, tiled=True)
+    return split.reshape(shape)
+
+
 def convolve_and_sum(source, interaction, local_sums, after_transform, primitive_tile_total):
     kx_devices = lax.axis_size("kx")
-    ky_devices = lax.axis_size("ky")
+    ky_devices = lax.axis_size(KY)
     sum_count = 3
     along_kx = lax.all_to_all(source, "kx", split_axis=0, concat_axis=1, tiled=True)
     components, x_length, column_count = along_kx.shape
@@ -175,12 +185,12 @@
     rows_x = contract("px,cxy->cpy", tables["cas_x"], along_kx)
     rows_x = after_transform(rows_x)
     split = rows_x.reshape(components, ky_devices, row_count, column_count)
-    along_ky = lax.all_to_all(split, "ky", split_axis=1, concat_axis=1, tiled=True)
+    along_ky = ky_exchange(split, ("kh", "kz"))
     spectrum = hartley_y(along_ky, tables)
     weight = interaction.reshape(row_count, column_count, ky_devices).transpose(2, 0, 1)
     weighted = spectrum * (weight * (1.0 / primitive_tile_total))[None]
     back_y = with_sums(hartley_y_transposed(weighted, tables), local_sums(), 2)
-    returned = lax.all_to_all(back_y, "ky", split_axis=1, concat_axis=1, tiled=True)
+    returned = ky_exchange(back_y, ("kz", "kh"))
     ky_sums = jnp.sum(returned[0, :, row_count, 0:sum_count], axis=0)
     returned = returned[:, :, 0:row_count].reshape(components, x_length, column_count)
     final = contract("px,cpy->cxy", tables["cas_x"], returned)
@@ -207,7 +217,7 @@
 def body(packed_state_matrix, energies, dipole_x, dipole_y, interaction, driving_field):
     rows_local = packed_state_matrix.shape[1]
     columns_local = packed_state_matrix.shape[2]
-    primitive_tile_total = rows_local * columns_local * lax.axis_size("kx") * lax.axis_size("ky")
+    primitive_tile_total = rows_local * columns_local * lax.axis_size("kx") * lax.axis_size(KY)
     populations = packed_state_matrix[0:4]
     halo_source = []
     gradients = []
@@ -219,7 +229,7 @@
 
     def local_sums():
         column_core = neighbours(jnp.concatenate([packed_state_matrix, energies]), "kx", 1, 2)
-        row_core = neighbours(halo_source[0], "ky", 2, 2)
+        row_core = neighbours(halo_source[0], KY, 2, 2)
         gradient_x = (
             8.0 * (column_core[:, 3:-1] - column_core[:, 1:-3])
             - (column_core[:, 4:] - column_core[:, :-4])
@@ -258,13 +268,17 @@
 
 
 def solution(mesh):
+    kx_size, ky_size = mesh.devices.shape
+    split_mesh = jax.sharding.Mesh(
+        mesh.devices.reshape(kx_size, ky_size // 2, 2), ("kx", "kz", "kh")
+    )
     in_specs = (
-        P(None, "kx", "ky"),
-        P(None, "kx", "ky"),
-        P(None, "kx", "ky"),
-        P(None, "kx", "ky"),
-        P("ky", None),
+        P(None, "kx", KY),
+        P(None, "kx", KY),
+        P(None, "kx", KY),
+        P(None, "kx", KY),
+        P(KY, None),
         P(),
     )
-    out_specs = (P(None, "kx", "ky"), P())
-    return jax.shard_map(body, mesh=mesh, in_specs=in_specs, out_specs=out_specs, check_vma=False)
+    out_specs = (P(None, "kx", KY), P())
+    return jax.shard_map(body, mesh=split_mesh, in_specs=in_specs, out_specs=out_specs, check_vma=False)

time: 119 us -> 131 us (1.10)
  starting transfers between devices: 49.5 us -> 55 us
  blocking collectives: 28.3 us -> 30.6 us
  waiting for transfers between devices: 13.3 us -> 15.3 us
  local copies, waits for them, and re-layouts: 8.9 us -> 10.8 us
    all_to_all x1, starting transfers between devices: 10.9 us -> 16.9 us  [convolve_and_sum(): back = lax.all_to_all(final, 'kx', split_axis=1, concat_axis=0, tiled=True)]
    all_to_all x1 -> x2, waiting for transfers between devices: 0.01 us -> 2.66 us  [ky_exchange(): lax.all_to_all(split, axis, split_axis=dim, concat_axis=dim, tiled=True)]
    ppermute x2, starting transfers between devices: 8.98 us -> 6.59 us  [neighbours(): lax.ppermute(initial.reshape(dense), axis, down).reshape(initial.shape)]
    all_to_all x1 -> x2, blocking collectives: 28.3 us -> 30.6 us  [ky_exchange(): lax.all_to_all(split, axis, split_axis=dim, concat_axis=dim, tiled=True)]
    all_to_all x0 -> x4, local copies, waits for them, and re-layouts: none -> 1.95 us  [ky_exchange(): lax.all_to_all(split, axis, split_axis=dim, concat_axis=dim, tiled=True)]
    all_to_all x1 -> x2, starting transfers between devices: 14 us -> 15.4 us  [ky_exchange(): lax.all_to_all(split, axis, split_axis=dim, concat_axis=dim, tiled=True)]
    unnamed x32 -> x28, local copies, waits for them, and re-layouts: 3.61 us -> 2.89 us
  transfers between devices with their start and end apart: 7 -> 8, of which waited for: 3 -> 3; matrix products, arithmetic and copies ran while one was open for 8% -> 9% of each run, Pallas kernels for 0% -> 0%
where the time goes in v8:
time: 131 us; the launch traced here: 130 us
  starting transfers between devices  55 us (42%)
  blocking collectives  30.6 us (23%)
  waiting for transfers between devices  15.3 us (12%)
  other arithmetic  11.7 us (9%)
  local copies, waits for them, and re-layouts  10.8 us (8%)
  matrix products  5.06 us (4%)
    all_to_all x2, blocking collectives, ky_exchange(): lax.all_to_all(split, axis, split_axis=dim, concat_axis=dim, tiled=True)  30.6 us
    all_to_all x1, starting transfers between devices, convolve_and_sum(): back = lax.all_to_all(final, 'kx', split_axis=1, concat_axis=0, tiled=True)  16.9 us
    all_to_all x2, starting transfers between devices, ky_exchange(): lax.all_to_all(split, axis, split_axis=dim, concat_axis=dim, tiled=True)  15.4 us
    all_to_all x1, starting transfers between devices, convolve_and_sum(): lax.all_to_all(source, 'kx', split_axis=0, concat_axis=1, tiled=True)  10.3 us
    all_to_all x1, waiting for transfers between devices, convolve_and_sum(): back = lax.all_to_all(final, 'kx', split_axis=1, concat_axis=0, tiled=True)  6.61 us
    ppermute x2, starting transfers between devices, neighbours(): lax.ppermute(initial.reshape(dense), axis, down).reshape(initial.shape)  6.59 us
    ppermute x2, waiting for transfers between devices, neighbours(): before = lax.ppermute(last.reshape(dense), axis, up).reshape(last.shape)  6.01 us
    ppermute x2, starting transfers between devices, neighbours(): before = lax.ppermute(last.reshape(dense), axis, up).reshape(last.shape)  5.76 us
  transfers between devices with their start and end apart: 8, of which 3 were waited for; matrix products, arithmetic and copies ran while one was open for 9% of the time, Pallas kernels for 0%

profile of v8, /device:TPU:1, one launch (start us, length us, event | category | flops | bytes accessed | tf_op | source)
XLA Modules:
  0.0 129.7 jit_solution(11335212706363914911)
XLA Ops:
  0.7 10.3 %all-to-all-start = ((f32[16,32,128]{2,1,0:T(8,128)}), f32[16,32,128]{2,1,0:T(8,128)S(1)}, u32[]{:S(2)}, u32[]{:S(2)}) async-start(f32[16,32,128]{2,1,0:T(8,128)} %param.17), calls=%async_computation | async-start | bytes 524288 | tf_op jit(solution)/shard_map/all_to_all | solution.py:181
  11.0 0.8 constant_dynamic-update-slice_fusion
  11.9 2.1 %collective-permute-start = (f32[40,128]{1,0:T(8,128)S(1)}, f32[40,128]{1,0:T(8,128)S(1)}, u32[]{:S(2)}, u32[]{:S(2)}) collective-permute-start(f32[40,128]{1,0:T(8,128)S(1)} %bitcast.101), channel_id=1, source_target_pairs={{32,0},{64,32},{96,64},{128,96},{160,128},{192,160},{224,192},{256... | collective-permute-start | bytes 61448 | tf_op jit(solution)/shard_map/ppermute | solution.py:213
  14.0 3.4 %collective-permute-start.1 = (f32[40,128]{1,0:T(8,128)S(1)}, f32[40,128]{1,0:T(8,128)S(1)}, u32[]{:S(2)}, u32[]{:S(2)}) collective-permute-start(f32[40,128]{1,0:T(8,128)S(1)} %bitcast.100), channel_id=1, source_target_pairs={{0,32},{32,64},{64,96},{96,128},{128,160},{160,192},{192,224},{224... | collective-permute-start | bytes 61448 | tf_op jit(solution)/shard_map/ppermute | solution.py:212
  17.5 1.0 broadcast_multiply_fusion
  18.5 1.0 convolution_bitcast_fusion.2
  20.2 3.4 %all-to-all-start.1 = ((f32[1,16,2,16,128]{4,3,1,0,2:T(8,128)}), f32[1,16,2,16,128]{4,3,1,0,2:T(8,128)S(1)}, u32[]{:S(2)}, u32[]{:S(2)}) async-start(f32[1,16,2,16,128]{4,3,1,0,2:T(8,128)} %copy.33), calls=%async_computation.1 | async-start | bytes 524288 | tf_op jit(solution)/shard_map/all_to_all | solution.py:173
  24.6 1.0 copy.38
  26.5 2.7 %all-to-all-done.1 = f32[1,16,2,16,128]{4,3,1,0,2:T(8,128)S(1)} async-done(((f32[1,16,2,16,128]{4,3,1,0,2:T(8,128)}), f32[1,16,2,16,128]{4,3,1,0,2:T(8,128)S(1)}, u32[]{:S(2)}, u32[]{:S(2)}) %all-to-all-start.1) | async-done | bytes 262176 | tf_op jit(solution)/shard_map/all_to_all | solution.py:173
  29.9 12.0 %all-to-all-start.2 = ((f32[1,16,2,16,128]{4,3,2,0,1:T(8,128)}), f32[1,16,2,16,128]{4,3,2,0,1:T(8,128)}, u32[]{:S(2)}, u32[]{:S(2)}) async-start(f32[1,16,2,16,128]{4,3,2,0,1:T(8,128)} %copy.34), calls=%async_computation.2 | async-start | bytes 524288 | tf_op jit(solution)/shard_map/all_to_all | solution.py:173
  42.2 4.5 %collective-permute-start.2 = (f32[10,128]{1,0:T(8,128)S(1)}, f32[10,128]{1,0:T(8,128)S(1)}, u32[]{:S(2)}, u32[]{:S(2)}) collective-permute-start(f32[10,128]{1,0:T(8,128)S(1)} %reshape.231), channel_id=1, source_target_pairs={{1,0},{2,1},{3,2},{4,3},{5,4},{6,5},{7,6},{8,7},{9,8},{10,9},{11,1... | collective-permute-start | bytes 15368 | tf_op jit(solution)/shard_map/ppermute | solution.py:213
  46.9 2.3 %collective-permute-start.3 = (f32[10,128]{1,0:T(8,128)S(1)}, f32[10,128]{1,0:T(8,128)S(1)}, u32[]{:S(2)}, u32[]{:S(2)}) collective-permute-start(f32[10,128]{1,0:T(8,128)S(1)} %reshape.233), channel_id=1, source_target_pairs={{0,1},{1,2},{2,3},{3,4},{4,5},{5,6},{6,7},{7,8},{8,9},{9,10},{10,1... | collective-permute-start | bytes 15368 | tf_op jit(solution)/shard_map/ppermute | solution.py:212
  49.5 6.0 %collective-permute-done.3 = f32[10,128]{1,0:T(8,128)S(1)} collective-permute-done((f32[10,128]{1,0:T(8,128)S(1)}, f32[10,128]{1,0:T(8,128)S(1)}, u32[]{:S(2)}, u32[]{:S(2)}) %collective-permute-start.3) | collective-permute-done | bytes 5152 | tf_op jit(solution)/shard_map/ppermute | solution.py:212
  57.0 2.6 %broadcast_select_fusion.1 = f32[1,1,1,3]{3,2,1,0:T(1,128)S(1)} fusion(pred[]{:T(512)} %compare_reduce_fusion, f32[1,1,1,1]{3,2,1,0:T(1,128)} %bitcast.29, f32[1,1,1,1]{3,2,1,0:T(1,128)} %bitcast.28, f32[1,1,1,1]{3,2,1,0:T(1,128)} %bitcast.23), kind=kLoop, calls=%fused_computation.88 | loop fusion | flops 9 | bytes 25 | tf_op jit(solution)/shard_map/reshape | solution.py:165
  59.6 1.1 copy.35
  65.6 22.1 %all_to_all.41 = f32[1,16,2,17,128]{4,2,3,0,1:T(2,128)S(1)} all-to-all(f32[1,16,2,17,128]{4,2,3,0,1:T(2,128)S(1)} %copy.43), channel_id=1, replica_groups=mesh['kx'=16,'kz'=16,'kh'=2] {'kz'}, dimensions={1} | all-to-all | bytes 557056 | tf_op jit(solution)/shard_map/all_to_all | solution.py:173
  87.7 8.5 %all_to_all.42 = f32[1,16,2,17,128]{4,1,3,0,2:T(8,128)S(1)} all-to-all(f32[1,16,2,17,128]{4,1,3,0,2:T(8,128)S(1)} %copy.44), channel_id=1, replica_groups=mesh['kx'=16,'kz'=16,'kh'=2] {'kh'}, dimensions={2} | all-to-all | bytes 557056 | tf_op jit(solution)/shard_map/all_to_all | solution.py:173
  97.1 0.8 convolution_bitcast_fusion
  98.0 1.0 copy.47
  99.0 16.9 %all-to-all-start.5 = ((f32[1,16,33,128]{3,0,2,1:T(1,128)}), f32[1,16,33,128]{3,0,2,1:T(1,128)S(1)}, u32[]{:S(2)}, u32[]{:S(2)}) async-start(f32[1,16,33,128]{3,0,2,1:T(1,128)} %copy.47), calls=%async_computation.5 | async-start | bytes 540672 | tf_op jit(solution)/shard_map/all_to_all | solution.py:199
  116.5 6.6 %all-to-all-done.5 = f32[1,16,33,128]{3,0,2,1:T(1,128)S(1)} async-done(((f32[1,16,33,128]{3,0,2,1:T(1,128)}), f32[1,16,33,128]{3,0,2,1:T(1,128)S(1)}, u32[]{:S(2)}, u32[]{:S(2)}) %all-to-all-start.5) | async-done | bytes 270368 | tf_op jit(solution)/shard_map/all_to_all | solution.py:199
  124.3 1.3 %fusion.25 = f32[12,32,128]{2,1,0:T(8,128)S(1)} fusion(f32[16,1,32,128]{3,2,0,1:T(8,128)S(1)} %bitcast.93, f32[12,32,128]{2,1,0:T(8,128)S(1)} %copy-done.6, f32[12,32,128]{2,1,0:T(8,128)S(1)} %copy-done.7, f32[]{:T(128)} %bitcast.44, f32[]{:T(128)} %bitcast.43), kind=kLoop, calls=%fused_computation.53 | loop fusion | flops 196608 | bytes 786440 | tf_op jit(solution)/shard_map/add | solution.py:102
  125.7 0.8 copy-done.5
  127.0 1.3 %fusion.16 = f32[16,32,128]{2,1,0:T(8,128)S(1)} fusion(f32[20,32,128]{2,1,0:T(8,128)S(1)} %fusion.13, f32[16,32,128]{2,1,0:T(8,128)S(1)} %constant_dynamic-update-slice_fusion.4, f32[20,32,128]{2,1,0:T(8,128)S(1)} %fusion.7, f32[]{:T(128)} %bitcast.44, f32[]{:T(128)} %bitcast.43), kind=kLoop, calls=%fused_computation.35 | loop fusion | flops 262144 | bytes 1048584 | tf_op jit(solution)/shard_map/add | solution.py:105
  (94 shorter events, 14.9 us)
Async XLA Ops:
  0.6 10.4 %copy-start = (f32[16,32,128]{2,1,0:T(8,128)S(1)}, f32[16,32,128]{2,1,0:T(8,128)}, u32[]{:S(2)}) copy-start(f32[16,32,128]{2,1,0:T(8,128)} %param.17) | copy-start | bytes 786436
  0.6 17.8 %copy-start.1 = (f32[512,512]{1,0:T(8,128)S(1)}, f32[512,512]{1,0:T(8,128)}, u32[]{:S(2)}) copy-start(f32[512,512]{1,0:T(8,128)} %constant.89.clone) | copy-start | bytes 3145732
  0.7 17.8 %all-to-all-start = ((f32[16,32,128]{2,1,0:T(8,128)}), f32[16,32,128]{2,1,0:T(8,128)S(1)}, u32[]{:S(2)}, u32[]{:S(2)}) async-start(f32[16,32,128]{2,1,0:T(8,128)} %param.17), calls=%async_computation | async-start | bytes 524288 | tf_op jit(solution)/shard_map/all_to_all | solution.py:181
  11.9 14.4 %collective-permute-start = (f32[40,128]{1,0:T(8,128)S(1)}, f32[40,128]{1,0:T(8,128)S(1)}, u32[]{:S(2)}, u32[]{:S(2)}) collective-permute-start(f32[40,128]{1,0:T(8,128)S(1)} %bitcast.101), channel_id=1, source_target_pairs={{32,0},{64,32},{96,64},{128,96},{160,128},{192,160},{224,192},{256... | collective-permute-start | bytes 61448 | tf_op jit(solution)/shard_map/ppermute | solution.py:213
  14.0 12.3 %collective-permute-start.1 = (f32[40,128]{1,0:T(8,128)S(1)}, f32[40,128]{1,0:T(8,128)S(1)}, u32[]{:S(2)}, u32[]{:S(2)}) collective-permute-start(f32[40,128]{1,0:T(8,128)S(1)} %bitcast.100), channel_id=1, source_target_pairs={{0,32},{32,64},{64,96},{96,128},{128,160},{160,192},{192,224},{224... | collective-permute-start | bytes 61448 | tf_op jit(solution)/shard_map/ppermute | solution.py:212
  20.2 9.0 %all-to-all-start.1 = ((f32[1,16,2,16,128]{4,3,1,0,2:T(8,128)}), f32[1,16,2,16,128]{4,3,1,0,2:T(8,128)S(1)}, u32[]{:S(2)}, u32[]{:S(2)}) async-start(f32[1,16,2,16,128]{4,3,1,0,2:T(8,128)} %copy.33), calls=%async_computation.1 | async-start | bytes 524288 | tf_op jit(solution)/shard_map/all_to_all | solution.py:173
  29.9 29.7 %all-to-all-start.2 = ((f32[1,16,2,16,128]{4,3,2,0,1:T(8,128)}), f32[1,16,2,16,128]{4,3,2,0,1:T(8,128)}, u32[]{:S(2)}, u32[]{:S(2)}) async-start(f32[1,16,2,16,128]{4,3,2,0,1:T(8,128)} %copy.34), calls=%async_computation.2 | async-start | bytes 524288 | tf_op jit(solution)/shard_map/all_to_all | solution.py:173
  42.2 7.0 %collective-permute-start.2 = (f32[10,128]{1,0:T(8,128)S(1)}, f32[10,128]{1,0:T(8,128)S(1)}, u32[]{:S(2)}, u32[]{:S(2)}) collective-permute-start(f32[10,128]{1,0:T(8,128)S(1)} %reshape.231), channel_id=1, source_target_pairs={{1,0},{2,1},{3,2},{4,3},{5,4},{6,5},{7,6},{8,7},{9,8},{10,9},{11,1... | collective-permute-start | bytes 15368 | tf_op jit(solution)/shard_map/ppermute | solution.py:213
  46.9 8.7 %collective-permute-start.3 = (f32[10,128]{1,0:T(8,128)S(1)}, f32[10,128]{1,0:T(8,128)S(1)}, u32[]{:S(2)}, u32[]{:S(2)}) collective-permute-start(f32[10,128]{1,0:T(8,128)S(1)} %reshape.233), channel_id=1, source_target_pairs={{0,1},{1,2},{2,3},{3,4},{4,5},{5,6},{6,7},{7,8},{8,9},{9,10},{10,1... | collective-permute-start | bytes 15368 | tf_op jit(solution)/shard_map/ppermute | solution.py:212
  59.6 1.1 copy-start.11
  60.7 0.7 copy-start.8
  60.7 0.7 copy-start.9
  60.8 0.7 copy-start.10
  61.5 0.8 copy-start.4
  62.3 0.9 copy-start.2
  62.3 1.0 copy-start.3
  99.0 16.9 %copy-start.12 = (f32[2]{0:T(128)S(1)}, f32[2]{0:T(128)}, u32[]{:S(2)}) copy-start(f32[2]{0:T(128)} %param.22) | copy-start | bytes 28
  99.0 24.1 %all-to-all-start.5 = ((f32[1,16,33,128]{3,0,2,1:T(1,128)}), f32[1,16,33,128]{3,0,2,1:T(1,128)S(1)}, u32[]{:S(2)}, u32[]{:S(2)}) async-start(f32[1,16,33,128]{3,0,2,1:T(1,128)} %copy.47), calls=%async_computation.5 | async-start | bytes 540672 | tf_op jit(solution)/shard_map/all_to_all | solution.py:199
  123.3 0.9 copy-start.6
  123.3 1.0 copy-start.7
  125.7 0.8 copy-start.5

commit v9 on v7

--- a/solution.py
+++ b/solution.py
@@ -128,33 +128,31 @@
     inner_angle = angles(group_length, group_length, group_length)
     return dict(
         cas_x=table(np.cos(x_angle) + np.sin(x_angle)),
-        group_cos=table(np.cos(group_angle)),
-        group_sin=table(np.sin(group_angle)),
+        group=table(np.stack([np.cos(group_angle), -np.sin(group_angle)])),
         twist_cos=table(np.cos(twist_angle)[None, :, None, :]),
         twist_sin=table(np.sin(twist_angle)[None, :, None, :]),
-        inner_plus=table(np.cos(inner_angle) + np.sin(inner_angle)),
-        inner_minus=table(np.cos(inner_angle) - np.sin(inner_angle)),
+        inner=table(
+            np.stack(
+                [np.cos(inner_angle) + np.sin(inner_angle), np.sin(inner_angle) - np.cos(inner_angle)]
+            )
+        ),
     )
 
 
 def hartley_y(data, tables):
-    first_real = contract("ka,capb->ckpb", tables["group_cos"], data)
-    first_imaginary = -contract("ka,capb->ckpb", tables["group_sin"], data)
+    first_real, first_imaginary = contract("ska,capb->sckpb", tables["group"], data)
     turned_real = first_real * tables["twist_cos"] + first_imaginary * tables["twist_sin"]
     turned_imaginary = first_imaginary * tables["twist_cos"] - first_real * tables["twist_sin"]
-    return contract("ckpb,bq->ckpq", turned_real, tables["inner_plus"]) - contract(
-        "ckpb,bq->ckpq", turned_imaginary, tables["inner_minus"]
-    )
+    turned = jnp.stack([turned_real, turned_imaginary])
+    return contract("sckpb,sbq->ckpq", turned, tables["inner"])
 
 
 def hartley_y_transposed(data, tables):
-    turned_real = contract("ckpq,bq->ckpb", data, tables["inner_plus"])
-    turned_imaginary = -contract("ckpq,bq->ckpb", data, tables["inner_minus"])
+    turned_real, turned_imaginary = contract("ckpq,sbq->sckpb", data, tables["inner"])
     first_real = turned_real * tables["twist_cos"] - turned_imaginary * tables["twist_sin"]
     first_imaginary = turned_real * tables["twist_sin"] + turned_imaginary * tables["twist_cos"]
-    return contract("ka,ckpb->capb", tables["group_cos"], first_real) - contract(
-        "ka,ckpb->capb", tables["group_sin"], first_imaginary
-    )
+    first = jnp.stack([first_real, first_imaginary])
+    return contract("ska,sckpb->capb", tables["group"], first)
 
 
 def with_sums(data, sums, dim):

time: 119 us -> 117 us (0.983)
  local copies, waits for them, and re-layouts: 8.9 us -> 7.1 us
  waiting for transfers between devices: 13.3 us -> 12.1 us
    ppermute x2, waiting for transfers between devices: 6.65 us -> 0.81 us  [neighbours(): before = lax.ppermute(last.reshape(dense), axis, up).reshape(last.shape)]
    all_to_all x1, waiting for transfers between devices: 0.01 us -> 3.32 us  [convolve_and_sum(): lax.all_to_all(split, 'ky', split_axis=1, concat_axis=1, tiled=True)]
    ppermute x2, starting transfers between devices: 5.35 us -> 8.11 us  [neighbours(): before = lax.ppermute(last.reshape(dense), axis, up).reshape(last.shape)]
    ppermute x2, starting transfers between devices: 8.98 us -> 6.25 us  [neighbours(): lax.ppermute(initial.reshape(dense), axis, down).reshape(initial.shape)]
    ppermute x2, waiting for transfers between devices: 0.01 us -> 1.36 us  [neighbours(): lax.ppermute(initial.reshape(dense), axis, down).reshape(initial.shape)]
    unnamed x32 -> x26, local copies, waits for them, and re-layouts: 3.61 us -> 2.49 us
    dot_general x10 -> x6, matrix products: 5.97 us -> 5.6 us  [contract(): jnp.einsum(einsum_form, left, right, precision=lax.Precision.HIGHEST, pre...]
  transfers between devices with their start and end apart: 7 -> 7, of which waited for: 3 -> 5; matrix products, arithmetic and copies ran while one was open for 8% -> 7% of each run, Pallas kernels for 0% -> 0%
where the time goes in v9:
time: 117 us
  starting transfers between devices  50.5 us (43%)
  blocking collectives  29.3 us (25%)
  waiting for transfers between devices  12.1 us (10%)
  other arithmetic  10.9 us (9%)
  local copies, waits for them, and re-layouts  7.1 us (6%)
  matrix products  5.6 us (5%)
  between operations  1.18 us (1%)
    all_to_all x1, blocking collectives, convolve_and_sum(): lax.all_to_all(back_y, 'ky', split_axis=1, concat_axis=1, tiled=True)  29.3 us
    all_to_all x1, starting transfers between devices, convolve_and_sum(): lax.all_to_all(split, 'ky', split_axis=1, concat_axis=1, tiled=True)  14.2 us
    all_to_all x1, starting transfers between devices, convolve_and_sum(): back = lax.all_to_all(final, 'kx', split_axis=1, concat_axis=0, tiled=True)  11.6 us
    all_to_all x1, starting transfers between devices, convolve_and_sum(): lax.all_to_all(source, 'kx', split_axis=0, concat_axis=1, tiled=True)  10.3 us
    ppermute x2, starting transfers between devices, neighbours(): before = lax.ppermute(last.reshape(dense), axis, up).reshape(last.shape)  8.11 us
    all_to_all x1, waiting for transfers between devices, convolve_and_sum(): back = lax.all_to_all(final, 'kx', split_axis=1, concat_axis=0, tiled=True)  6.58 us
    ppermute x2, starting transfers between devices, neighbours(): lax.ppermute(initial.reshape(dense), axis, down).reshape(initial.shape)  6.25 us
    dot_general x6, matrix products, contract(): jnp.einsum(einsum_form, left, right, precision=lax.Precision.HIGHEST, pre...  5.6 us
  transfers between devices with their start and end apart: 7, of which 5 were waited for; matrix products, arithmetic and copies ran while one was open for 7% of the time, Pallas kernels for 0%

profile of v9, /device:TPU:1, one launch (start us, length us, event | category | flops | bytes accessed | tf_op | source)
XLA Modules:
  0.0 116.7 jit_solution(14702608499181948532)
XLA Ops:
  0.6 10.3 %all-to-all-start = ((f32[16,32,128]{2,1,0:T(8,128)}), f32[16,32,128]{2,1,0:T(8,128)S(1)}, u32[]{:S(2)}, u32[]{:S(2)}) async-start(f32[16,32,128]{2,1,0:T(8,128)} %param.15), calls=%async_computation | async-start | bytes 524288 | tf_op jit(solution)/shard_map/all_to_all | solution.py:169
  11.0 0.8 copy-done.4
  11.9 3.5 %collective-permute-start.1 = (f32[40,128]{1,0:T(8,128)S(1)}, f32[40,128]{1,0:T(8,128)S(1)}, u32[]{:S(2)}, u32[]{:S(2)}) collective-permute-start(f32[40,128]{1,0:T(8,128)S(1)} %bitcast.105), channel_id=1, source_target_pairs={{0,32},{32,64},{64,96},{96,128},{128,160},{160,192},{192,224},{224... | collective-permute-start | bytes 61448 | tf_op jit(solution)/shard_map/ppermute | solution.py:200
  15.4 1.9 %collective-permute-start = (f32[40,128]{1,0:T(8,128)S(1)}, f32[40,128]{1,0:T(8,128)S(1)}, u32[]{:S(2)}, u32[]{:S(2)}) collective-permute-start(f32[40,128]{1,0:T(8,128)S(1)} %bitcast.104), channel_id=1, source_target_pairs={{32,0},{64,32},{96,64},{128,96},{160,128},{192,160},{224,192},{256... | collective-permute-start | bytes 61448 | tf_op jit(solution)/shard_map/ppermute | solution.py:201
  18.3 1.0 copy.36
  20.7 1.7 %convolution_bitcast_fusion.5 = f32[1,512,128]{2,1,0:T(8,128)} fusion(f32[512,512]{1,0:T(8,128)S(1)} %copy-done.1, f32[512,128]{1,0:T(8,128)S(1)} %bitcast.99), kind=kOutput, calls=%fused_computation.7 | convolution fusion | flops 402653184 | bytes 1572864 | tf_op jit(solution)/shard_map/px,cxy->cpy/dot_general | solution.py:109
  22.4 14.2 %all-to-all-start.1 = ((f32[1,32,16,128]{3,2,0,1:T(8,128)}), f32[1,32,16,128]{3,2,0,1:T(8,128)}, u32[]{:S(2)}, u32[]{:S(2)}) async-start(f32[1,32,16,128]{3,2,0,1:T(8,128)} %bitcast.6), calls=%async_computation.1 | async-start | bytes 524288 | tf_op jit(solution)/shard_map/all_to_all | solution.py:176
  37.0 4.6 %collective-permute-start.3 = (f32[10,128]{1,0:T(8,128)S(1)}, f32[10,128]{1,0:T(8,128)S(1)}, u32[]{:S(2)}, u32[]{:S(2)}) collective-permute-start(f32[10,128]{1,0:T(8,128)S(1)} %reshape.235), channel_id=1, source_target_pairs={{0,1},{1,2},{2,3},{3,4},{4,5},{5,6},{6,7},{7,8},{8,9},{9,10},{10,1... | collective-permute-start | bytes 15368 | tf_op jit(solution)/shard_map/ppermute | solution.py:200
  41.8 4.3 %collective-permute-start.2 = (f32[10,128]{1,0:T(8,128)S(1)}, f32[10,128]{1,0:T(8,128)S(1)}, u32[]{:S(2)}, u32[]{:S(2)}) collective-permute-start(f32[10,128]{1,0:T(8,128)S(1)} %reshape.233), channel_id=1, source_target_pairs={{1,0},{2,1},{3,2},{4,3},{5,4},{6,5},{7,6},{8,7},{9,8},{10,9},{11,1... | collective-permute-start | bytes 15368 | tf_op jit(solution)/shard_map/ppermute | solution.py:201
  46.1 0.8 collective-permute-done.3
  47.2 0.9 collective-permute-done.2
  48.9 0.7 fusion.26
  49.5 2.5 %broadcast_select_fusion.1 = f32[1,1,1,3]{3,2,1,0:T(1,128)S(1)} fusion(pred[]{:T(512)} %compare_reduce_fusion, f32[1,1,1,1]{3,2,1,0:T(1,128)} %bitcast.35, f32[1,1,1,1]{3,2,1,0:T(1,128)} %bitcast.34, f32[1,1,1,1]{3,2,1,0:T(1,128)} %bitcast.29), kind=kLoop, calls=%fused_computation.88 | loop fusion | flops 9 | bytes 25 | tf_op jit(solution)/shard_map/reshape | solution.py:162
  52.1 3.3 %all-to-all-done.1 = f32[1,32,16,128]{3,2,0,1:T(8,128)} async-done(((f32[1,32,16,128]{3,2,0,1:T(8,128)}), f32[1,32,16,128]{3,2,0,1:T(8,128)}, u32[]{:S(2)}, u32[]{:S(2)}) %all-to-all-start.1) | async-done | bytes 262176 | tf_op jit(solution)/shard_map/all_to_all | solution.py:176
  55.4 1.6 %convolution_bitcast_fusion.1 = f32[2,1,32,16,128]{4,2,0,3,1:T(8,128)S(1)} fusion(f32[2,32,32,1]{2,1,0,3:T(8,128)S(1)} %copy-done.8, f32[1,32,16,128]{3,2,0,1:T(8,128)} %all-to-all-done.1), kind=kOutput, calls=%fused_computation.1 | convolution fusion | flops 50331648 | bytes 794624 | tf_op jit(solution)/shard_map/ska,capb->sckpb/dot_general | solution.py:109
  57.1 0.8 copy-done.2
  60.0 29.3 %all_to_all.31 = f32[1,32,17,128]{3,0,2,1:T(1,128)S(1)} all-to-all(f32[1,32,17,128]{3,0,2,1:T(1,128)S(1)} %copy.39), channel_id=1, replica_groups=mesh['kx'=16,'ky'=32] {'ky'}, dimensions={1} | all-to-all | bytes 557056 | tf_op jit(solution)/shard_map/all_to_all | solution.py:181
  90.0 0.8 convolution_bitcast_fusion.4
  91.0 1.0 copy.42
  92.0 11.6 %all-to-all-start.3 = ((f32[1,16,33,128]{3,0,2,1:T(1,128)}), f32[1,16,33,128]{3,0,2,1:T(1,128)S(1)}, u32[]{:S(2)}, u32[]{:S(2)}) async-start(f32[1,16,33,128]{3,0,2,1:T(1,128)} %copy.42), calls=%async_computation.3 | async-start | bytes 540672 | tf_op jit(solution)/shard_map/all_to_all | solution.py:187
  104.3 6.6 %all-to-all-done.3 = f32[1,16,33,128]{3,0,2,1:T(1,128)S(1)} async-done(((f32[1,16,33,128]{3,0,2,1:T(1,128)}), f32[1,16,33,128]{3,0,2,1:T(1,128)S(1)}, u32[]{:S(2)}, u32[]{:S(2)}) %all-to-all-start.3) | async-done | bytes 270368 | tf_op jit(solution)/shard_map/all_to_all | solution.py:187
  112.0 1.4 %fusion.24 = f32[12,32,128]{2,1,0:T(8,128)S(1)} fusion(f32[16,1,32,128]{3,2,0,1:T(8,128)S(1)} %bitcast.98, f32[12,32,128]{2,1,0:T(8,128)S(1)} %copy-done.6, f32[12,32,128]{2,1,0:T(8,128)S(1)} %copy-done.7, f32[]{:T(128)} %bitcast.48, f32[]{:T(128)} %bitcast.47), kind=kLoop, calls=%fused_computation.53 | loop fusion | flops 196608 | bytes 786440 | tf_op jit(solution)/shard_map/add | solution.py:101
  113.9 1.4 %fusion.19 = f32[16,32,128]{2,1,0:T(8,128)S(1)} fusion(f32[20,32,128]{2,1,0:T(8,128)S(1)} %fusion.16, f32[16,32,128]{2,1,0:T(8,128)S(1)} %constant_dynamic-update-slice_fusion.4, f32[20,32,128]{2,1,0:T(8,128)S(1)} %fusion.10, f32[]{:T(128)} %bitcast.48, f32[]{:T(128)} %bitcast.47), kind=kLoop, calls=%fused_computation.39 | loop fusion | flops 262144 | bytes 1048584 | tf_op jit(solution)/shard_map/add | solution.py:104
  116.0 0.7 pad_maximum_fusion.5
  (82 shorter events, 9.8 us)
Async XLA Ops:
  0.6 10.4 %copy-start = (f32[16,32,128]{2,1,0:T(8,128)S(1)}, f32[16,32,128]{2,1,0:T(8,128)}, u32[]{:S(2)}) copy-start(f32[16,32,128]{2,1,0:T(8,128)} %param.15) | copy-start | bytes 786436
  0.6 20.1 %all-to-all-start = ((f32[16,32,128]{2,1,0:T(8,128)}), f32[16,32,128]{2,1,0:T(8,128)S(1)}, u32[]{:S(2)}, u32[]{:S(2)}) async-start(f32[16,32,128]{2,1,0:T(8,128)} %param.15), calls=%async_computation | async-start | bytes 524288 | tf_op jit(solution)/shard_map/all_to_all | solution.py:169
  11.0 0.8 copy-start.4
  11.0 6.3 %copy-start.5 = (f32[16,4096]{1,0:T(8,128)S(1)}, f32[16,4096]{1,0:T(8,128)}, u32[]{:S(2)}) copy-start(f32[16,4096]{1,0:T(8,128)} %param.19) | copy-start | bytes 786436
  11.9 8.2 %collective-permute-start.1 = (f32[40,128]{1,0:T(8,128)S(1)}, f32[40,128]{1,0:T(8,128)S(1)}, u32[]{:S(2)}, u32[]{:S(2)}) collective-permute-start(f32[40,128]{1,0:T(8,128)S(1)} %bitcast.105), channel_id=1, source_target_pairs={{0,32},{32,64},{64,96},{96,128},{128,160},{160,192},{192,224},{224... | collective-permute-start | bytes 61448 | tf_op jit(solution)/shard_map/ppermute | solution.py:200
  15.4 5.1 %collective-permute-start = (f32[40,128]{1,0:T(8,128)S(1)}, f32[40,128]{1,0:T(8,128)S(1)}, u32[]{:S(2)}, u32[]{:S(2)}) collective-permute-start(f32[40,128]{1,0:T(8,128)S(1)} %bitcast.104), channel_id=1, source_target_pairs={{32,0},{64,32},{96,64},{128,96},{160,128},{192,160},{224,192},{256... | collective-permute-start | bytes 61448 | tf_op jit(solution)/shard_map/ppermute | solution.py:201
  18.3 2.4 %copy-start.1 = (f32[512,512]{1,0:T(8,128)S(1)}, f32[512,512]{1,0:T(8,128)}, u32[]{:S(2)}) copy-start(f32[512,512]{1,0:T(8,128)} %constant.85.clone) | copy-start | bytes 3145732
  22.4 33.0 %all-to-all-start.1 = ((f32[1,32,16,128]{3,2,0,1:T(8,128)}), f32[1,32,16,128]{3,2,0,1:T(8,128)}, u32[]{:S(2)}, u32[]{:S(2)}) async-start(f32[1,32,16,128]{3,2,0,1:T(8,128)} %bitcast.6), calls=%async_computation.1 | async-start | bytes 524288 | tf_op jit(solution)/shard_map/all_to_all | solution.py:176
  37.0 10.0 %collective-permute-start.3 = (f32[10,128]{1,0:T(8,128)S(1)}, f32[10,128]{1,0:T(8,128)S(1)}, u32[]{:S(2)}, u32[]{:S(2)}) collective-permute-start(f32[10,128]{1,0:T(8,128)S(1)} %reshape.235), channel_id=1, source_target_pairs={{0,1},{1,2},{2,3},{3,4},{4,5},{5,6},{6,7},{7,8},{8,9},{9,10},{10,1... | collective-permute-start | bytes 15368 | tf_op jit(solution)/shard_map/ppermute | solution.py:200
  41.8 6.3 %collective-permute-start.2 = (f32[10,128]{1,0:T(8,128)S(1)}, f32[10,128]{1,0:T(8,128)S(1)}, u32[]{:S(2)}, u32[]{:S(2)}) collective-permute-start(f32[10,128]{1,0:T(8,128)S(1)} %reshape.233), channel_id=1, source_target_pairs={{1,0},{2,1},{3,2},{4,3},{5,4},{6,5},{7,6},{8,7},{9,8},{10,9},{11,1... | collective-permute-start | bytes 15368 | tf_op jit(solution)/shard_map/ppermute | solution.py:201
  48.9 6.5 %copy-start.8 = (f32[2,32,32,1]{2,1,0,3:T(8,128)S(1)}, f32[2,32,32,1]{2,1,0,3:T(8,128)}, u32[]{:S(2)}) copy-start(f32[2,32,32,1]{2,1,0,3:T(8,128)} %constant.98) | copy-start | bytes 24580
  52.1 4.9 %copy-start.9 = (f32[32,128]{1,0:T(8,128)S(1)}, f32[32,128]{1,0:T(8,128)}, u32[]{:S(2)}) copy-start(f32[32,128]{1,0:T(8,128)} %constant.96) | copy-start | bytes 49156
  52.1 4.9 %copy-start.10 = (f32[32,128]{1,0:T(8,128)S(1)}, f32[32,128]{1,0:T(8,128)}, u32[]{:S(2)}) copy-start(f32[32,128]{1,0:T(8,128)} %constant.95) | copy-start | bytes 49156
  57.0 1.0 copy-start.2
  57.0 1.0 copy-start.3
  92.0 11.6 %copy-start.11 = (f32[2]{0:T(128)S(1)}, f32[2]{0:T(128)}, u32[]{:S(2)}) copy-start(f32[2]{0:T(128)} %param.20) | copy-start | bytes 28
  92.0 18.8 %all-to-all-start.3 = ((f32[1,16,33,128]{3,0,2,1:T(1,128)}), f32[1,16,33,128]{3,0,2,1:T(1,128)S(1)}, u32[]{:S(2)}, u32[]{:S(2)}) async-start(f32[1,16,33,128]{3,0,2,1:T(1,128)} %copy.42), calls=%async_computation.3 | async-start | bytes 540672 | tf_op jit(solution)/shard_map/all_to_all | solution.py:187
  111.0 0.9 copy-start.6
  111.0 1.0 copy-start.7

commit v10 on v9

--- a/solution.py
+++ b/solution.py
@@ -162,7 +162,7 @@
     return jnp.concatenate([data, jnp.broadcast_to(row.reshape([1] * (data.ndim - 2) + [1, -1]), shape)], axis=dim)
 
 
-def convolve_and_sum(source, interaction, local_sums, after_transform, primitive_tile_total):
+def convolve_and_sum(source, interaction, local_sums, primitive_tile_total):
     kx_devices = lax.axis_size("kx")
     ky_devices = lax.axis_size("ky")
     sum_count = 3
@@ -171,7 +171,6 @@
     row_count = x_length // ky_devices
     tables = hartley_tables(x_length, ky_devices, column_count)
     rows_x = contract("px,cxy->cpy", tables["cas_x"], along_kx)
-    rows_x = after_transform(rows_x)
     split = rows_x.reshape(components, ky_devices, row_count, column_count)
     along_ky = lax.all_to_all(split, "ky", split_axis=1, concat_axis=1, tiled=True)
     spectrum = hartley_y(along_ky, tables)
@@ -207,26 +206,20 @@
     columns_local = packed_state_matrix.shape[2]
     primitive_tile_total = rows_local * columns_local * lax.axis_size("kx") * lax.axis_size("ky")
     populations = packed_state_matrix[0:4]
-    halo_source = []
-    gradients = []
-
-    def after_transform(rows_x):
-        rows_x, late = lax.optimization_barrier((rows_x, jnp.concatenate([packed_state_matrix, energies])))
-        halo_source.append(late)
-        return rows_x
+    stacked = jnp.concatenate([packed_state_matrix, energies])
+    column_core = neighbours(stacked, "kx", 1, 2)
+    row_core = neighbours(stacked, "ky", 2, 2)
+    source, column_core, row_core = lax.optimization_barrier((packed_state_matrix, column_core, row_core))
+    gradient_x = (
+        8.0 * (column_core[:, 3:-1] - column_core[:, 1:-3])
+        - (column_core[:, 4:] - column_core[:, :-4])
+    ) / 12.0
+    gradient_y = (
+        8.0 * (row_core[:, :, 3:-1] - row_core[:, :, 1:-3])
+        - (row_core[:, :, 4:] - row_core[:, :, :-4])
+    ) / 12.0
 
     def local_sums():
-        column_core = neighbours(jnp.concatenate([packed_state_matrix, energies]), "kx", 1, 2)
-        row_core = neighbours(halo_source[0], "ky", 2, 2)
-        gradient_x = (
-            8.0 * (column_core[:, 3:-1] - column_core[:, 1:-3])
-            - (column_core[:, 4:] - column_core[:, :-4])
-        ) / 12.0
-        gradient_y = (
-            8.0 * (row_core[:, :, 3:-1] - row_core[:, :, 1:-3])
-            - (row_core[:, :, 4:] - row_core[:, :, :-4])
-        ) / 12.0
-        gradients.extend([gradient_x, gradient_y])
         return jnp.stack(
             [
                 jnp.sum(packed_state_matrix[2] + packed_state_matrix[3]),
@@ -235,10 +228,7 @@
             ]
         )
 
-    convolved, totals = convolve_and_sum(
-        packed_state_matrix, interaction, local_sums, after_transform, primitive_tile_total
-    )
-    gradient_x, gradient_y = gradients
+    convolved, totals = convolve_and_sum(source, interaction, local_sums, primitive_tile_total)
     shielding_multiplier = 1.0 / (1.0 + SHIELDING_LEVEL * totals[0])
     self_energy = -shielding_multiplier * convolved
     section_slope = slope_terms(

time: 117 us -> 126 us (1.077)
  starting transfers between devices: 50.5 us -> 38.5 us
  waiting for transfers between devices: 12.1 us -> 23 us
  blocking collectives: 29.3 us -> 39.3 us
  matrix products: 5.6 us -> 4.25 us
    all_to_all x0 -> x1, blocking collectives: none -> 13 us  [convolve_and_sum(): lax.all_to_all(source, 'kx', split_axis=0, concat_axis=1, tiled=True)]
    all_to_all x1, waiting for transfers between devices: 3.32 us -> 14.1 us  [convolve_and_sum(): lax.all_to_all(split, 'ky', split_axis=1, concat_axis=1, tiled=True)]
    all_to_all x1 -> x0, starting transfers between devices: 10.3 us -> none  [convolve_and_sum(): lax.all_to_all(source, 'kx', split_axis=0, concat_axis=1, tiled=True)]
    ppermute x2, starting transfers between devices: 6.25 us -> 12.8 us  [neighbours(): lax.ppermute(initial.reshape(dense), axis, down).reshape(initial.shape)]
    all_to_all x1, starting transfers between devices: 14.2 us -> 9.35 us  [convolve_and_sum(): lax.all_to_all(split, 'ky', split_axis=1, concat_axis=1, tiled=True)]
    all_to_all x1, starting transfers between devices: 11.6 us -> 6.82 us  [convolve_and_sum(): back = lax.all_to_all(final, 'kx', split_axis=1, concat_axis=0, tiled=True)]
    all_to_all x1, blocking collectives: 29.3 us -> 26.3 us  [convolve_and_sum(): lax.all_to_all(back_y, 'ky', split_axis=1, concat_axis=1, tiled=True)]
    ppermute x2, starting transfers between devices: 8.11 us -> 9.53 us  [neighbours(): before = lax.ppermute(last.reshape(dense), axis, up).reshape(last.shape)]
  transfers between devices with their start and end apart: 7 -> 6, of which waited for: 5 -> 3; matrix products, arithmetic and copies ran while one was open for 7% -> 6% of each run, Pallas kernels for 0% -> 0%
where the time goes in v10:
time: 126 us; the launch traced here: 125 us
  blocking collectives  39.3 us (31%)
  starting transfers between devices  38.5 us (31%)
  waiting for transfers between devices  23 us (18%)
  other arithmetic  10.9 us (9%)
  local copies, waits for them, and re-layouts  8.14 us (6%)
  matrix products  4.25 us (3%)
    all_to_all x1, blocking collectives, convolve_and_sum(): lax.all_to_all(back_y, 'ky', split_axis=1, concat_axis=1, tiled=True)  26.3 us
    all_to_all x1, waiting for transfers between devices, convolve_and_sum(): lax.all_to_all(split, 'ky', split_axis=1, concat_axis=1, tiled=True)  14.1 us
    all_to_all x1, blocking collectives, convolve_and_sum(): lax.all_to_all(source, 'kx', split_axis=0, concat_axis=1, tiled=True)  13 us
    ppermute x2, starting transfers between devices, neighbours(): lax.ppermute(initial.reshape(dense), axis, down).reshape(initial.shape)  12.8 us
    ppermute x2, starting transfers between devices, neighbours(): before = lax.ppermute(last.reshape(dense), axis, up).reshape(last.shape)  9.53 us
    all_to_all x1, starting transfers between devices, convolve_and_sum(): lax.all_to_all(split, 'ky', split_axis=1, concat_axis=1, tiled=True)  9.35 us
    all_to_all x1, starting transfers between devices, convolve_and_sum(): back = lax.all_to_all(final, 'kx', split_axis=1, concat_axis=0, tiled=True)  6.82 us
    all_to_all x1, waiting for transfers between devices, convolve_and_sum(): back = lax.all_to_all(final, 'kx', split_axis=1, concat_axis=0, tiled=True)  6.64 us
  transfers between devices with their start and end apart: 6, of which 3 were waited for; matrix products, arithmetic and copies ran while one was open for 6% of the time, Pallas kernels for 0%

profile of v10, /device:TPU:1, one launch (start us, length us, event | category | flops | bytes accessed | tf_op | source)
XLA Modules:
  0.0 125.4 jit_solution(12679586657750769007)
XLA Ops:
  0.6 1.0 constant_dynamic-update-slice_fusion.1
  2.0 5.5 %collective-permute-start.2 = (f32[10,128]{1,0:T(8,128)S(1)}, f32[10,128]{1,0:T(8,128)S(1)}, u32[]{:S(2)}, u32[]{:S(2)}) collective-permute-start(f32[10,128]{1,0:T(8,128)S(1)} %reshape.228), channel_id=1, source_target_pairs={{0,1},{1,2},{2,3},{3,4},{4,5},{5,6},{6,7},{7,8},{8,9},{9,10},{10,1... | collective-permute-start | bytes 15368 | tf_op jit(solution)/shard_map/ppermute | solution.py:199
  7.7 10.9 %collective-permute-start.3 = (f32[10,128]{1,0:T(8,128)S(1)}, f32[10,128]{1,0:T(8,128)S(1)}, u32[]{:S(2)}, u32[]{:S(2)}) collective-permute-start(f32[10,128]{1,0:T(8,128)S(1)} %reshape.230), channel_id=1, source_target_pairs={{1,0},{2,1},{3,2},{4,3},{5,4},{6,5},{7,6},{8,7},{9,8},{10,9},{11,1... | collective-permute-start | bytes 15368 | tf_op jit(solution)/shard_map/ppermute | solution.py:200
  18.6 4.0 %collective-permute-start = (f32[40,128]{1,0:T(8,128)S(1)}, f32[40,128]{1,0:T(8,128)S(1)}, u32[]{:S(2)}, u32[]{:S(2)}) collective-permute-start(f32[40,128]{1,0:T(8,128)S(1)} %bitcast.103), channel_id=1, source_target_pairs={{0,32},{32,64},{64,96},{96,128},{128,160},{160,192},{192,224},{224... | collective-permute-start | bytes 61448 | tf_op jit(solution)/shard_map/ppermute | solution.py:199
  22.7 1.9 %collective-permute-start.1 = (f32[40,128]{1,0:T(8,128)S(1)}, f32[40,128]{1,0:T(8,128)S(1)}, u32[]{:S(2)}, u32[]{:S(2)}) collective-permute-start(f32[40,128]{1,0:T(8,128)S(1)} %bitcast.102), channel_id=1, source_target_pairs={{32,0},{64,32},{96,64},{128,96},{160,128},{192,160},{224,192},{256... | collective-permute-start | bytes 61448 | tf_op jit(solution)/shard_map/ppermute | solution.py:200
  25.5 2.3 %collective-permute-done.1 = f32[40,128]{1,0:T(8,128)S(1)} collective-permute-done((f32[40,128]{1,0:T(8,128)S(1)}, f32[40,128]{1,0:T(8,128)S(1)}, u32[]{:S(2)}, u32[]{:S(2)}) %collective-permute-start.1) | collective-permute-done | bytes 20512 | tf_op jit(solution)/shard_map/ppermute | solution.py:200
  27.8 0.9 copy-done
  28.7 13.0 %all_to_all.31 = f32[16,32,128]{2,1,0:T(8,128)S(1)} all-to-all(f32[16,32,128]{2,1,0:T(8,128)S(1)} %copy-done), channel_id=1, replica_groups=mesh['kx'=16,'ky'=32] {'kx'}, dimensions={0} | all-to-all | bytes 524288 | tf_op jit(solution)/shard_map/all_to_all | solution.py:169
  41.8 1.3 %convolution_bitcast_fusion.5 = f32[1,512,128]{1,2,0:T(8,128)S(1)} fusion(f32[512,128]{1,0:T(8,128)S(1)} %bitcast.98, f32[512,512]{1,0:T(8,128)S(1)} %copy-done.1), kind=kOutput, calls=%fused_computation.7 | convolution fusion | flops 402653184 | bytes 1572864 | tf_op jit(solution)/shard_map/px,cxy->cpy/dot_general | solution.py:109
  43.0 0.8 copy.36
  43.9 9.4 %all-to-all-start.1 = ((f32[1,32,16,128]{3,2,0,1:T(8,128)}), f32[1,32,16,128]{3,2,0,1:T(8,128)S(1)}, u32[]{:S(2)}, u32[]{:S(2)}) async-start(f32[1,32,16,128]{3,2,0,1:T(8,128)} %bitcast.9), calls=%async_computation.1 | async-start | bytes 524288 | tf_op jit(solution)/shard_map/all_to_all | solution.py:175
  54.6 0.7 add_reduce_fusion
  55.6 0.7 fusion.13
  56.3 2.6 %broadcast_select_fusion.1 = f32[1,1,1,3]{3,2,1,0:T(1,128)S(1)} fusion(pred[]{:T(512)} %compare_reduce_fusion, f32[1,1,1,1]{3,2,1,0:T(1,128)} %bitcast.34, f32[1,1,1,1]{3,2,1,0:T(1,128)} %bitcast.33, f32[1,1,1,1]{3,2,1,0:T(1,128)} %bitcast.32), kind=kLoop, calls=%fused_computation.68 | loop fusion | flops 9 | bytes 25 | tf_op jit(solution)/shard_map/reshape | solution.py:162
  58.9 14.1 %all-to-all-done.1 = f32[1,32,16,128]{3,2,0,1:T(8,128)S(1)} async-done(((f32[1,32,16,128]{3,2,0,1:T(8,128)}), f32[1,32,16,128]{3,2,0,1:T(8,128)S(1)}, u32[]{:S(2)}, u32[]{:S(2)}) %all-to-all-start.1) | async-done | bytes 262176 | tf_op jit(solution)/shard_map/all_to_all | solution.py:175
  73.8 0.8 copy-done.3
  76.7 26.3 %all_to_all.32 = f32[1,32,17,128]{3,0,2,1:T(1,128)S(1)} all-to-all(f32[1,32,17,128]{3,0,2,1:T(1,128)S(1)} %copy.42), channel_id=1, replica_groups=mesh['kx'=16,'ky'=32] {'ky'}, dimensions={1} | all-to-all | bytes 557056 | tf_op jit(solution)/shard_map/all_to_all | solution.py:180
  103.0 0.8 convolution_bitcast_fusion.4
  104.7 1.0 copy.45
  105.7 6.8 %all-to-all-start.3 = ((f32[1,16,33,128]{3,0,2,1:T(1,128)}), f32[1,16,33,128]{3,0,2,1:T(1,128)S(1)}, u32[]{:S(2)}, u32[]{:S(2)}) async-start(f32[1,16,33,128]{3,0,2,1:T(1,128)} %copy.45), calls=%async_computation.3 | async-start | bytes 540672 | tf_op jit(solution)/shard_map/all_to_all | solution.py:186
  113.1 6.6 %all-to-all-done.3 = f32[1,16,33,128]{3,0,2,1:T(1,128)S(1)} async-done(((f32[1,16,33,128]{3,0,2,1:T(1,128)}), f32[1,16,33,128]{3,0,2,1:T(1,128)S(1)}, u32[]{:S(2)}, u32[]{:S(2)}) %all-to-all-start.3) | async-done | bytes 270368 | tf_op jit(solution)/shard_map/all_to_all | solution.py:186
  120.9 1.3 %fusion.11 = f32[12,32,128]{2,1,0:T(8,128)S(1)} fusion(f32[16,1,32,128]{3,2,0,1:T(8,128)S(1)} %bitcast.96, f32[12,32,128]{2,1,0:T(8,128)S(1)} %copy-done.6, f32[12,32,128]{2,1,0:T(8,128)S(1)} %copy-done.7, f32[]{:T(128)} %bitcast.47, f32[]{:T(128)} %bitcast.46), kind=kLoop, calls=%fused_computation.35 | loop fusion | flops 196608 | bytes 786440 | tf_op jit(solution)/shard_map/add | solution.py:101
  122.7 1.3 %fusion.6 = f32[16,32,128]{2,1,0:T(8,128)S(1)} fusion(f32[20,32,128]{2,1,0:T(8,128)S(1)} %get-tuple-element.44, f32[16,32,128]{2,1,0:T(8,128)S(1)} %constant_dynamic-update-slice_fusion.2, f32[20,32,128]{2,1,0:T(8,128)S(1)} %get-tuple-element.45, f32[]{:T(128)} %bitcast.47, f32[]{:T(128)} %bitcast.46), kind=kLoop, calls=%fused_computation.21 | loop fusion | flops 262144 | bytes 1048584 | tf_op jit(solution)/shard_map/add | solution.py:104
  124.6 0.7 pad_maximum_fusion.4
  (81 shorter events, 9.6 us)
Async XLA Ops:
  0.6 1.0 copy-start.4
  2.0 22.6 %collective-permute-start.2 = (f32[10,128]{1,0:T(8,128)S(1)}, f32[10,128]{1,0:T(8,128)S(1)}, u32[]{:S(2)}, u32[]{:S(2)}) collective-permute-start(f32[10,128]{1,0:T(8,128)S(1)} %reshape.228), channel_id=1, source_target_pairs={{0,1},{1,2},{2,3},{3,4},{4,5},{5,6},{6,7},{7,8},{8,9},{9,10},{10,1... | collective-permute-start | bytes 15368 | tf_op jit(solution)/shard_map/ppermute | solution.py:199
  7.7 17.2 %collective-permute-start.3 = (f32[10,128]{1,0:T(8,128)S(1)}, f32[10,128]{1,0:T(8,128)S(1)}, u32[]{:S(2)}, u32[]{:S(2)}) collective-permute-start(f32[10,128]{1,0:T(8,128)S(1)} %reshape.230), channel_id=1, source_target_pairs={{1,0},{2,1},{3,2},{4,3},{5,4},{6,5},{7,6},{8,7},{9,8},{10,9},{11,1... | collective-permute-start | bytes 15368 | tf_op jit(solution)/shard_map/ppermute | solution.py:200
  18.6 6.9 %collective-permute-start = (f32[40,128]{1,0:T(8,128)S(1)}, f32[40,128]{1,0:T(8,128)S(1)}, u32[]{:S(2)}, u32[]{:S(2)}) collective-permute-start(f32[40,128]{1,0:T(8,128)S(1)} %bitcast.103), channel_id=1, source_target_pairs={{0,32},{32,64},{64,96},{96,128},{128,160},{160,192},{192,224},{224... | collective-permute-start | bytes 61448 | tf_op jit(solution)/shard_map/ppermute | solution.py:199
  22.7 5.1 %collective-permute-start.1 = (f32[40,128]{1,0:T(8,128)S(1)}, f32[40,128]{1,0:T(8,128)S(1)}, u32[]{:S(2)}, u32[]{:S(2)}) collective-permute-start(f32[40,128]{1,0:T(8,128)S(1)} %bitcast.102), channel_id=1, source_target_pairs={{32,0},{64,32},{96,64},{128,96},{160,128},{192,160},{224,192},{256... | collective-permute-start | bytes 61448 | tf_op jit(solution)/shard_map/ppermute | solution.py:200
  25.2 16.6 %copy-start.1 = (f32[512,512]{1,0:T(8,128)S(1)}, f32[512,512]{1,0:T(8,128)}, u32[]{:S(2)}) copy-start(f32[512,512]{1,0:T(8,128)} %constant.85.clone) | copy-start | bytes 3145732
  27.8 1.0 copy-start
  43.9 9.4 %copy-start.5 = (f32[16,4096]{1,0:T(8,128)S(1)}, f32[16,4096]{1,0:T(8,128)}, u32[]{:S(2)}) copy-start(f32[16,4096]{1,0:T(8,128)} %param.19) | copy-start | bytes 786436
  43.9 29.2 %all-to-all-start.1 = ((f32[1,32,16,128]{3,2,0,1:T(8,128)}), f32[1,32,16,128]{3,2,0,1:T(8,128)S(1)}, u32[]{:S(2)}, u32[]{:S(2)}) async-start(f32[1,32,16,128]{3,2,0,1:T(8,128)} %bitcast.9), calls=%async_computation.1 | async-start | bytes 524288 | tf_op jit(solution)/shard_map/all_to_all | solution.py:175
  55.6 17.4 %copy-start.8 = (f32[2,32,32,1]{2,1,0,3:T(8,128)S(1)}, f32[2,32,32,1]{2,1,0,3:T(8,128)}, u32[]{:S(2)}) copy-start(f32[2,32,32,1]{2,1,0,3:T(8,128)} %constant.98) | copy-start | bytes 24580
  58.9 14.8 %copy-start.9 = (f32[32,128]{1,0:T(8,128)S(1)}, f32[32,128]{1,0:T(8,128)}, u32[]{:S(2)}) copy-start(f32[32,128]{1,0:T(8,128)} %constant.95) | copy-start | bytes 49156
  58.9 14.8 %copy-start.10 = (f32[32,128]{1,0:T(8,128)S(1)}, f32[32,128]{1,0:T(8,128)}, u32[]{:S(2)}) copy-start(f32[32,128]{1,0:T(8,128)} %constant.96) | copy-start | bytes 49156
  73.7 0.9 copy-start.3
  76.3 26.7 %copy-start.2 = (f32[512,512]{1,0:T(8,128)S(1)}, f32[512,512]{1,0:T(8,128)}, u32[]{:S(2)}) copy-start(f32[512,512]{1,0:T(8,128)} %constant.85.clone) | copy-start | bytes 3145732
  105.7 6.8 %copy-start.11 = (f32[2]{0:T(128)S(1)}, f32[2]{0:T(128)}, u32[]{:S(2)}) copy-start(f32[2]{0:T(128)} %param.20) | copy-start | bytes 28
  105.7 14.0 %all-to-all-start.3 = ((f32[1,16,33,128]{3,0,2,1:T(1,128)}), f32[1,16,33,128]{3,0,2,1:T(1,128)S(1)}, u32[]{:S(2)}, u32[]{:S(2)}) async-start(f32[1,16,33,128]{3,0,2,1:T(1,128)} %copy.45), calls=%async_computation.3 | async-start | bytes 540672 | tf_op jit(solution)/shard_map/all_to_all | solution.py:186
  119.8 0.9 copy-start.6
  119.8 1.0 copy-start.7

commit v11 on v9

--- a/solution.py
+++ b/solution.py
@@ -172,15 +172,15 @@
     tables = hartley_tables(x_length, ky_devices, column_count)
     rows_x = contract("px,cxy->cpy", tables["cas_x"], along_kx)
     rows_x = after_transform(rows_x)
-    split = rows_x.reshape(components, ky_devices, row_count, column_count)
+    split = with_sums(rows_x.reshape(components, ky_devices, row_count, column_count), local_sums(), 2)
     along_ky = lax.all_to_all(split, "ky", split_axis=1, concat_axis=1, tiled=True)
-    spectrum = hartley_y(along_ky, tables)
+    ky_sums = jnp.sum(along_ky[0, :, row_count, 0:sum_count], axis=0)
+    spectrum = hartley_y(along_ky[:, :, 0:row_count], tables)
     weight = interaction.reshape(row_count, column_count, ky_devices).transpose(2, 0, 1)
     weighted = spectrum * (weight * (1.0 / primitive_tile_total))[None]
-    back_y = with_sums(hartley_y_transposed(weighted, tables), local_sums(), 2)
+    back_y = hartley_y_transposed(weighted, tables)
     returned = lax.all_to_all(back_y, "ky", split_axis=1, concat_axis=1, tiled=True)
-    ky_sums = jnp.sum(returned[0, :, row_count, 0:sum_count], axis=0)
-    returned = returned[:, :, 0:row_count].reshape(components, x_length, column_count)
+    returned = returned.reshape(components, x_length, column_count)
     final = contract("px,cpy->cxy", tables["cas_x"], returned)
     rows_local = x_length // kx_devices
     final = with_sums(final.reshape(components, kx_devices, rows_local, column_count), ky_sums, 2)

time: 117 us -> 129 us (1.10)
  waiting for transfers between devices: 12.1 us -> 51.6 us
  blocking collectives: 29.3 us -> 0 us
  local copies, waits for them, and re-layouts: 7.1 us -> 8.48 us
    all_to_all x1 -> x0, blocking collectives: 29.3 us -> none  [convolve_and_sum(): lax.all_to_all(back_y, 'ky', split_axis=1, concat_axis=1, tiled=True)]
    all_to_all x0 -> x1, waiting for transfers between devices: none -> 18.3 us  [convolve_and_sum(): lax.all_to_all(back_y, 'ky', split_axis=1, concat_axis=1, tiled=True)]
    all_to_all x1, waiting for transfers between devices: 3.32 us -> 19 us  [convolve_and_sum(): lax.all_to_all(split, 'ky', split_axis=1, concat_axis=1, tiled=True)]
    all_to_all x1, starting transfers between devices: 14.2 us -> 5.95 us  [convolve_and_sum(): lax.all_to_all(split, 'ky', split_axis=1, concat_axis=1, tiled=True)]
    all_to_all x0 -> x1, starting transfers between devices: none -> 6.58 us  [convolve_and_sum(): lax.all_to_all(back_y, 'ky', split_axis=1, concat_axis=1, tiled=True)]
    ppermute x2, starting transfers between devices: 6.25 us -> 11.9 us  [neighbours(): lax.ppermute(initial.reshape(dense), axis, down).reshape(initial.shape)]
    ppermute x2, waiting for transfers between devices: 0.81 us -> 5.77 us  [neighbours(): before = lax.ppermute(last.reshape(dense), axis, up).reshape(last.shape)]
    ppermute x2, starting transfers between devices: 8.11 us -> 5.47 us  [neighbours(): before = lax.ppermute(last.reshape(dense), axis, up).reshape(last.shape)]
  transfers between devices with their start and end apart: 7 -> 8, of which waited for: 5 -> 5; matrix products, arithmetic and copies ran while one was open for 7% -> 4% of each run, Pallas kernels for 0% -> 0%
where the time goes in v11:
time: 129 us; the launch traced here: 128 us
  waiting for transfers between devices  51.6 us (40%)
  starting transfers between devices  50.4 us (39%)
  other arithmetic  11.8 us (9%)
  local copies, waits for them, and re-layouts  8.48 us (7%)
  matrix products  4.65 us (4%)
    all_to_all x1, waiting for transfers between devices, convolve_and_sum(): lax.all_to_all(split, 'ky', split_axis=1, concat_axis=1, tiled=True)  19 us
    all_to_all x1, waiting for transfers between devices, convolve_and_sum(): lax.all_to_all(back_y, 'ky', split_axis=1, concat_axis=1, tiled=True)  18.3 us
    ppermute x2, starting transfers between devices, neighbours(): lax.ppermute(initial.reshape(dense), axis, down).reshape(initial.shape)  11.9 us
    all_to_all x1, starting transfers between devices, convolve_and_sum(): lax.all_to_all(source, 'kx', split_axis=0, concat_axis=1, tiled=True)  10.3 us
    all_to_all x1, starting transfers between devices, convolve_and_sum(): back = lax.all_to_all(final, 'kx', split_axis=1, concat_axis=0, tiled=True)  10.2 us
    all_to_all x1, waiting for transfers between devices, convolve_and_sum(): back = lax.all_to_all(final, 'kx', split_axis=1, concat_axis=0, tiled=True)  6.61 us
    all_to_all x1, starting transfers between devices, convolve_and_sum(): lax.all_to_all(back_y, 'ky', split_axis=1, concat_axis=1, tiled=True)  6.58 us
    all_to_all x1, starting transfers between devices, convolve_and_sum(): lax.all_to_all(split, 'ky', split_axis=1, concat_axis=1, tiled=True)  5.95 us
  transfers between devices with their start and end apart: 8, of which 5 were waited for; matrix products, arithmetic and copies ran while one was open for 4% of the time, Pallas kernels for 0%

profile of v11, /device:TPU:1, one launch (start us, length us, event | category | flops | bytes accessed | tf_op | source)
XLA Modules:
  0.0 128.0 jit_solution(2713474497161294449)
XLA Ops:
  0.7 10.3 %all-to-all-start = ((f32[16,32,128]{2,1,0:T(8,128)}), f32[16,32,128]{2,1,0:T(8,128)S(1)}, u32[]{:S(2)}, u32[]{:S(2)}) async-start(f32[16,32,128]{2,1,0:T(8,128)} %param.15), calls=%async_computation | async-start | bytes 524288 | tf_op jit(solution)/shard_map/all_to_all | solution.py:169
  11.0 0.8 constant_dynamic-update-slice_fusion
  11.9 3.5 %collective-permute-start.1 = (f32[40,128]{1,0:T(8,128)S(1)}, f32[40,128]{1,0:T(8,128)S(1)}, u32[]{:S(2)}, u32[]{:S(2)}) collective-permute-start(f32[40,128]{1,0:T(8,128)S(1)} %bitcast.104), channel_id=1, source_target_pairs={{0,32},{32,64},{64,96},{96,128},{128,160},{160,192},{192,224},{224... | collective-permute-start | bytes 61448 | tf_op jit(solution)/shard_map/ppermute | solution.py:200
  15.4 1.9 %collective-permute-start = (f32[40,128]{1,0:T(8,128)S(1)}, f32[40,128]{1,0:T(8,128)S(1)}, u32[]{:S(2)}, u32[]{:S(2)}) collective-permute-start(f32[40,128]{1,0:T(8,128)S(1)} %bitcast.103), channel_id=1, source_target_pairs={{32,0},{64,32},{96,64},{128,96},{160,128},{192,160},{224,192},{256... | collective-permute-start | bytes 61448 | tf_op jit(solution)/shard_map/ppermute | solution.py:201
  18.7 1.9 %collective-permute-done = f32[40,128]{1,0:T(8,128)S(1)} collective-permute-done((f32[40,128]{1,0:T(8,128)S(1)}, f32[40,128]{1,0:T(8,128)S(1)}, u32[]{:S(2)}, u32[]{:S(2)}) %collective-permute-start) | collective-permute-done | bytes 20512 | tf_op jit(solution)/shard_map/ppermute | solution.py:201
  20.7 1.7 %convolution_bitcast_fusion.5 = f32[1,512,128]{2,1,0:T(8,128)} fusion(f32[512,512]{1,0:T(8,128)S(1)} %copy-done.1, f32[512,128]{1,0:T(8,128)S(1)} %bitcast.98), kind=kOutput, calls=%fused_computation.7 | convolution fusion | flops 402653184 | bytes 1572864 | tf_op jit(solution)/shard_map/px,cxy->cpy/dot_general | solution.py:109
  22.8 10.0 %collective-permute-start.2 = (f32[10,128]{1,0:T(8,128)S(1)}, f32[10,128]{1,0:T(8,128)S(1)}, u32[]{:S(2)}, u32[]{:S(2)}) collective-permute-start(f32[10,128]{1,0:T(8,128)S(1)} %reshape.230), channel_id=1, source_target_pairs={{1,0},{2,1},{3,2},{4,3},{5,4},{6,5},{7,6},{8,7},{9,8},{10,9},{11,1... | collective-permute-start | bytes 15368 | tf_op jit(solution)/shard_map/ppermute | solution.py:201
  33.1 1.9 %collective-permute-start.3 = (f32[10,128]{1,0:T(8,128)S(1)}, f32[10,128]{1,0:T(8,128)S(1)}, u32[]{:S(2)}, u32[]{:S(2)}) collective-permute-start(f32[10,128]{1,0:T(8,128)S(1)} %reshape.232), channel_id=1, source_target_pairs={{0,1},{1,2},{2,3},{3,4},{4,5},{5,6},{6,7},{7,8},{8,9},{9,10},{10,1... | collective-permute-start | bytes 15368 | tf_op jit(solution)/shard_map/ppermute | solution.py:200
  35.3 5.8 %collective-permute-done.3 = f32[10,128]{1,0:T(8,128)S(1)} collective-permute-done((f32[10,128]{1,0:T(8,128)S(1)}, f32[10,128]{1,0:T(8,128)S(1)}, u32[]{:S(2)}, u32[]{:S(2)}) %collective-permute-start.3) | collective-permute-done | bytes 5152 | tf_op jit(solution)/shard_map/ppermute | solution.py:200
  42.5 2.5 %broadcast_select_fusion.1 = f32[1,1,1,3]{3,2,1,0:T(1,128)S(1)} fusion(pred[]{:T(512)} %compare_reduce_fusion, f32[1,1,1,1]{3,2,1,0:T(1,128)} %bitcast.13, f32[1,1,1,1]{3,2,1,0:T(1,128)} %bitcast.12, f32[1,1,1,1]{3,2,1,0:T(1,128)} %bitcast.7), kind=kLoop, calls=%fused_computation.87 | loop fusion | flops 9 | bytes 25 | tf_op jit(solution)/shard_map/reshape | solution.py:162
  45.1 1.0 pad_maximum_fusion.4
  46.0 5.9 %all-to-all-start.1 = ((f32[1,32,17,128]{3,0,2,1:T(1,128)}), f32[1,32,17,128]{3,0,2,1:T(1,128)S(1)}, u32[]{:S(2)}, u32[]{:S(2)}) async-start(f32[1,32,17,128]{3,0,2,1:T(1,128)} %pad_maximum_fusion.4), calls=%async_computation.1 | async-start | bytes 557056 | tf_op jit(solution)/shard_map/all_to_all | solution.py:176
  52.7 19.0 %all-to-all-done.1 = f32[1,32,17,128]{3,0,2,1:T(1,128)S(1)} async-done(((f32[1,32,17,128]{3,0,2,1:T(1,128)}), f32[1,32,17,128]{3,0,2,1:T(1,128)S(1)}, u32[]{:S(2)}, u32[]{:S(2)}) %all-to-all-start.1) | async-done | bytes 278560 | tf_op jit(solution)/shard_map/all_to_all | solution.py:176
  72.5 0.8 copy-done.3
  75.7 0.9 copy.38
  76.6 6.6 %all-to-all-start.2 = ((f32[1,32,16,128]{3,2,0,1:T(8,128)}), f32[1,32,16,128]{3,2,0,1:T(8,128)S(1)}, u32[]{:S(2)}, u32[]{:S(2)}) async-start(f32[1,32,16,128]{3,2,0,1:T(8,128)} %copy.38), calls=%async_computation.2 | async-start | bytes 524288 | tf_op jit(solution)/shard_map/all_to_all | solution.py:182
  83.9 18.3 %all-to-all-done.2 = f32[1,32,16,128]{3,2,0,1:T(8,128)S(1)} async-done(((f32[1,32,16,128]{3,2,0,1:T(8,128)}), f32[1,32,16,128]{3,2,0,1:T(8,128)S(1)}, u32[]{:S(2)}, u32[]{:S(2)}) %all-to-all-start.2) | async-done | bytes 262176 | tf_op jit(solution)/shard_map/all_to_all | solution.py:182
  102.2 0.8 convolution_bitcast_fusion.4
  103.1 1.0 copy.40
  104.1 10.2 %all-to-all-start.3 = ((f32[1,16,33,128]{3,0,2,1:T(1,128)}), f32[1,16,33,128]{3,0,2,1:T(1,128)S(1)}, u32[]{:S(2)}, u32[]{:S(2)}) async-start(f32[1,16,33,128]{3,0,2,1:T(1,128)} %copy.40), calls=%async_computation.3 | async-start | bytes 540672 | tf_op jit(solution)/shard_map/all_to_all | solution.py:187
  114.9 6.6 %all-to-all-done.3 = f32[1,16,33,128]{3,0,2,1:T(1,128)S(1)} async-done(((f32[1,16,33,128]{3,0,2,1:T(1,128)}), f32[1,16,33,128]{3,0,2,1:T(1,128)S(1)}, u32[]{:S(2)}, u32[]{:S(2)}) %all-to-all-start.3) | async-done | bytes 270368 | tf_op jit(solution)/shard_map/all_to_all | solution.py:187
  122.7 1.3 %fusion.22 = f32[12,32,128]{2,1,0:T(8,128)S(1)} fusion(f32[16,1,32,128]{3,2,0,1:T(8,128)S(1)} %bitcast.96, f32[12,32,128]{2,1,0:T(8,128)S(1)} %copy-done.6, f32[12,32,128]{2,1,0:T(8,128)S(1)} %copy-done.7, f32[]{:T(128)} %bitcast.48, f32[]{:T(128)} %bitcast.47), kind=kLoop, calls=%fused_computation.52 | loop fusion | flops 196608 | bytes 786440 | tf_op jit(solution)/shard_map/add | solution.py:101
  124.1 0.8 copy-done.4
  125.4 1.3 %fusion.19 = f32[16,32,128]{2,1,0:T(8,128)S(1)} fusion(f32[20,32,128]{2,1,0:T(8,128)S(1)} %fusion.16, f32[16,32,128]{2,1,0:T(8,128)S(1)} %constant_dynamic-update-slice_fusion.4, f32[20,32,128]{2,1,0:T(8,128)S(1)} %fusion.10, f32[]{:T(128)} %bitcast.48, f32[]{:T(128)} %bitcast.47), kind=kLoop, calls=%fused_computation.39 | loop fusion | flops 262144 | bytes 1048584 | tf_op jit(solution)/shard_map/add | solution.py:104
  (85 shorter events, 12.0 us)
Async XLA Ops:
  0.6 10.4 %copy-start = (f32[16,32,128]{2,1,0:T(8,128)S(1)}, f32[16,32,128]{2,1,0:T(8,128)}, u32[]{:S(2)}) copy-start(f32[16,32,128]{2,1,0:T(8,128)} %param.15) | copy-start | bytes 786436
  0.6 20.1 %copy-start.1 = (f32[512,512]{1,0:T(8,128)S(1)}, f32[512,512]{1,0:T(8,128)}, u32[]{:S(2)}) copy-start(f32[512,512]{1,0:T(8,128)} %constant.85.clone) | copy-start | bytes 3145732
  0.7 20.1 %all-to-all-start = ((f32[16,32,128]{2,1,0:T(8,128)}), f32[16,32,128]{2,1,0:T(8,128)S(1)}, u32[]{:S(2)}, u32[]{:S(2)}) async-start(f32[16,32,128]{2,1,0:T(8,128)} %param.15), calls=%async_computation | async-start | bytes 524288 | tf_op jit(solution)/shard_map/all_to_all | solution.py:169
  11.9 6.8 %collective-permute-start.1 = (f32[40,128]{1,0:T(8,128)S(1)}, f32[40,128]{1,0:T(8,128)S(1)}, u32[]{:S(2)}, u32[]{:S(2)}) collective-permute-start(f32[40,128]{1,0:T(8,128)S(1)} %bitcast.104), channel_id=1, source_target_pairs={{0,32},{32,64},{64,96},{96,128},{128,160},{160,192},{192,224},{224... | collective-permute-start | bytes 61448 | tf_op jit(solution)/shard_map/ppermute | solution.py:200
  15.4 5.1 %collective-permute-start = (f32[40,128]{1,0:T(8,128)S(1)}, f32[40,128]{1,0:T(8,128)S(1)}, u32[]{:S(2)}, u32[]{:S(2)}) collective-permute-start(f32[40,128]{1,0:T(8,128)S(1)} %bitcast.103), channel_id=1, source_target_pairs={{32,0},{64,32},{96,64},{128,96},{160,128},{192,160},{224,192},{256... | collective-permute-start | bytes 61448 | tf_op jit(solution)/shard_map/ppermute | solution.py:201
  22.8 12.2 %collective-permute-start.2 = (f32[10,128]{1,0:T(8,128)S(1)}, f32[10,128]{1,0:T(8,128)S(1)}, u32[]{:S(2)}, u32[]{:S(2)}) collective-permute-start(f32[10,128]{1,0:T(8,128)S(1)} %reshape.230), channel_id=1, source_target_pairs={{1,0},{2,1},{3,2},{4,3},{5,4},{6,5},{7,6},{8,7},{9,8},{10,9},{11,1... | collective-permute-start | bytes 15368 | tf_op jit(solution)/shard_map/ppermute | solution.py:201
  33.1 8.0 %collective-permute-start.3 = (f32[10,128]{1,0:T(8,128)S(1)}, f32[10,128]{1,0:T(8,128)S(1)}, u32[]{:S(2)}, u32[]{:S(2)}) collective-permute-start(f32[10,128]{1,0:T(8,128)S(1)} %reshape.232), channel_id=1, source_target_pairs={{0,1},{1,2},{2,3},{3,4},{4,5},{5,6},{6,7},{7,8},{8,9},{9,10},{10,1... | collective-permute-start | bytes 15368 | tf_op jit(solution)/shard_map/ppermute | solution.py:200
  41.3 3.7 %copy-start.2 = (f32[1,512,128]{2,1,0:T(8,128)S(1)}, f32[1,512,128]{2,1,0:T(8,128)}, u32[]{:S(2)}) copy-start(f32[1,512,128]{2,1,0:T(8,128)} %convolution_bitcast_fusion.5) | copy-start | bytes 786436
  46.0 6.0 %copy-start.5 = (f32[16,4096]{1,0:T(8,128)S(1)}, f32[16,4096]{1,0:T(8,128)}, u32[]{:S(2)}) copy-start(f32[16,4096]{1,0:T(8,128)} %param.19) | copy-start | bytes 786436
  46.0 25.7 %all-to-all-start.1 = ((f32[1,32,17,128]{3,0,2,1:T(1,128)}), f32[1,32,17,128]{3,0,2,1:T(1,128)S(1)}, u32[]{:S(2)}, u32[]{:S(2)}) async-start(f32[1,32,17,128]{3,0,2,1:T(1,128)} %pad_maximum_fusion.4), calls=%async_computation.1 | async-start | bytes 557056 | tf_op jit(solution)/shard_map/all_to_all | solution.py:176
  52.7 19.0 %copy-start.8 = (f32[2,32,32,1]{2,1,0,3:T(8,128)S(1)}, f32[2,32,32,1]{2,1,0,3:T(8,128)}, u32[]{:S(2)}) copy-start(f32[2,32,32,1]{2,1,0,3:T(8,128)} %constant.98) | copy-start | bytes 24580
  71.7 0.7 copy-start.10
  71.7 0.7 copy-start.11
  72.5 0.9 copy-start.3
  74.5 0.8 copy-start.9
  76.6 25.6 %all-to-all-start.2 = ((f32[1,32,16,128]{3,2,0,1:T(8,128)}), f32[1,32,16,128]{3,2,0,1:T(8,128)S(1)}, u32[]{:S(2)}, u32[]{:S(2)}) async-start(f32[1,32,16,128]{3,2,0,1:T(8,128)} %copy.38), calls=%async_computation.2 | async-start | bytes 524288 | tf_op jit(solution)/shard_map/all_to_all | solution.py:182
  104.1 10.2 %copy-start.12 = (f32[2]{0:T(128)S(1)}, f32[2]{0:T(128)}, u32[]{:S(2)}) copy-start(f32[2]{0:T(128)} %param.20) | copy-start | bytes 28
  104.1 17.4 %all-to-all-start.3 = ((f32[1,16,33,128]{3,0,2,1:T(1,128)}), f32[1,16,33,128]{3,0,2,1:T(1,128)S(1)}, u32[]{:S(2)}, u32[]{:S(2)}) async-start(f32[1,16,33,128]{3,0,2,1:T(1,128)} %copy.40), calls=%async_computation.3 | async-start | bytes 540672 | tf_op jit(solution)/shard_map/all_to_all | solution.py:187
  121.6 0.9 copy-start.6
  121.7 1.0 copy-start.7
  124.1 0.8 copy-start.4

commit v12 on v9

--- a/solution.py
+++ b/solution.py
@@ -162,7 +162,9 @@
     return jnp.concatenate([data, jnp.broadcast_to(row.reshape([1] * (data.ndim - 2) + [1, -1]), shape)], axis=dim)
 
 
-def convolve_and_sum(source, interaction, local_sums, after_transform, primitive_tile_total):
+def convolve_and_sum(
+    source, interaction, local_sums, after_transform, before_return, primitive_tile_total
+):
     kx_devices = lax.axis_size("kx")
     ky_devices = lax.axis_size("ky")
     sum_count = 3
@@ -184,6 +186,7 @@
     final = contract("px,cpy->cxy", tables["cas_x"], returned)
     rows_local = x_length // kx_devices
     final = with_sums(final.reshape(components, kx_devices, rows_local, column_count), ky_sums, 2)
+    final = before_return(final)
     back = lax.all_to_all(final, "kx", split_axis=1, concat_axis=0, tiled=True)
     totals = jnp.sum(back[::components, 0, rows_local, 0:sum_count], axis=0) / primitive_tile_total
     convolved = back[:, 0, 0:rows_local].reshape(components * kx_devices, rows_local, column_count)
@@ -235,22 +238,27 @@
             ]
         )
 
+    early = []
+
+    def before_return(final):
+        field_x = driving_field[0]
+        field_y = driving_field[1]
+        gradient_x, gradient_y = gradients
+        dipole_field = field_x * dipole_x + field_y * dipole_y
+        drift = field_x * gradient_x[0:16] + field_y * gradient_y[0:16]
+        drift = jnp.concatenate([drift[0:4], drift[4:16] - DEPHASING * packed_state_matrix[4:16]])
+        final, dipole_field, drift = lax.optimization_barrier((final, dipole_field, drift))
+        early.extend([dipole_field, drift])
+        return final
+
     convolved, totals = convolve_and_sum(
-        packed_state_matrix, interaction, local_sums, after_transform, primitive_tile_total
-    )
-    gradient_x, gradient_y = gradients
+        packed_state_matrix, interaction, local_sums, after_transform, before_return, primitive_tile_total
+    )
+    dipole_field, drift = early
     shielding_multiplier = 1.0 / (1.0 + SHIELDING_LEVEL * totals[0])
     self_energy = -shielding_multiplier * convolved
-    section_slope = slope_terms(
-        packed_state_matrix,
-        energies,
-        self_energy,
-        gradient_x[0:16],
-        gradient_y[0:16],
-        dipole_x,
-        dipole_y,
-        driving_field,
-    )
+    coupled = jnp.concatenate([energies + self_energy[0:4], self_energy[4:16] + dipole_field])
+    section_slope = commutator(coupled, packed_state_matrix) + drift
     field_next = driving_field - COUPLING * totals[1:3]
     return (section_slope, field_next)
 

time: 117 us -> 113 us (0.966)
  blocking collectives: 29.3 us -> 17.8 us
  waiting for transfers between devices: 12.1 us -> 21.1 us
    all_to_all x1, blocking collectives: 29.3 us -> 17.8 us  [convolve_and_sum(): back = lax.all_to_all(final, 'kx', split_axis=1, concat_axis=0, tiled=True)]
    all_to_all x1, waiting for transfers between devices: 6.58 us -> 14.4 us  [convolve_and_sum(): lax.all_to_all(back_y, 'ky', split_axis=1, concat_axis=1, tiled=True)]
    ppermute x2, waiting for transfers between devices: 0.81 us -> 6.68 us  [neighbours(): before = lax.ppermute(last.reshape(dense), axis, up).reshape(last.shape)]
    all_to_all x1, waiting for transfers between devices: 3.32 us -> 0.01 us  [convolve_and_sum(): lax.all_to_all(split, 'ky', split_axis=1, concat_axis=1, tiled=True)]
    ppermute x2, starting transfers between devices: 8.11 us -> 5.35 us  [neighbours(): before = lax.ppermute(last.reshape(dense), axis, up).reshape(last.shape)]
    ppermute x2, starting transfers between devices: 6.25 us -> 8.9 us  [neighbours(): lax.ppermute(initial.reshape(dense), axis, down).reshape(initial.shape)]
    ppermute x2, waiting for transfers between devices: 1.36 us -> 0.01 us  [neighbours(): lax.ppermute(initial.reshape(dense), axis, down).reshape(initial.shape)]
    add x3 -> x5, other arithmetic: 2.76 us -> 3.43 us  [the longest x1 1.33 us: before_return(): drift = field_x * gradient_x[0:16] + field_y * gradient_y[0:16]]
  transfers between devices with their start and end apart: 7 -> 7, of which waited for: 5 -> 3; matrix products, arithmetic and copies ran while one was open for 7% -> 10% of each run, Pallas kernels for 0% -> 0%
where the time goes in v12:
time: 113 us; the launch traced here: 112 us
  starting transfers between devices  49.5 us (44%)
  waiting for transfers between devices  21.1 us (19%)
  blocking collectives  17.8 us (16%)
  other arithmetic  10.8 us (10%)
  local copies, waits for them, and re-layouts  6.31 us (6%)
  matrix products  5.61 us (5%)
  between operations  1.21 us (1%)
    all_to_all x1, blocking collectives, convolve_and_sum(): back = lax.all_to_all(final, 'kx', split_axis=1, concat_axis=0, tiled=True)  17.8 us
    all_to_all x1, waiting for transfers between devices, convolve_and_sum(): lax.all_to_all(back_y, 'ky', split_axis=1, concat_axis=1, tiled=True)  14.4 us
    all_to_all x1, starting transfers between devices, convolve_and_sum(): lax.all_to_all(split, 'ky', split_axis=1, concat_axis=1, tiled=True)  14.1 us
    all_to_all x1, starting transfers between devices, convolve_and_sum(): lax.all_to_all(back_y, 'ky', split_axis=1, concat_axis=1, tiled=True)  10.8 us
    all_to_all x1, starting transfers between devices, convolve_and_sum(): lax.all_to_all(source, 'kx', split_axis=0, concat_axis=1, tiled=True)  10.3 us
    ppermute x2, starting transfers between devices, neighbours(): lax.ppermute(initial.reshape(dense), axis, down).reshape(initial.shape)  8.9 us
    ppermute x2, waiting for transfers between devices, neighbours(): before = lax.ppermute(last.reshape(dense), axis, up).reshape(last.shape)  6.68 us
    dot_general x6, matrix products, contract(): jnp.einsum(einsum_form, left, right, precision=lax.Precision.HIGHEST, pre...  5.61 us
  transfers between devices with their start and end apart: 7, of which 3 were waited for; matrix products, arithmetic and copies ran while one was open for 10% of the time, Pallas kernels for 0%

profile of v12, /device:TPU:1, one launch (start us, length us, event | category | flops | bytes accessed | tf_op | source)
XLA Modules:
  0.0 112.4 jit_solution(12491904153467654411)
XLA Ops:
  0.6 10.3 %all-to-all-start = ((f32[16,32,128]{2,1,0:T(8,128)}), f32[16,32,128]{2,1,0:T(8,128)S(1)}, u32[]{:S(2)}, u32[]{:S(2)}) async-start(f32[16,32,128]{2,1,0:T(8,128)} %param.15), calls=%async_computation | async-start | bytes 524288 | tf_op jit(solution)/shard_map/all_to_all | solution.py:171
  11.0 0.8 copy-done.4
  11.9 2.1 %collective-permute-start = (f32[40,128]{1,0:T(8,128)S(1)}, f32[40,128]{1,0:T(8,128)S(1)}, u32[]{:S(2)}, u32[]{:S(2)}) collective-permute-start(f32[40,128]{1,0:T(8,128)S(1)} %bitcast.103), channel_id=1, source_target_pairs={{32,0},{64,32},{96,64},{128,96},{160,128},{192,160},{224,192},{256... | collective-permute-start | bytes 61448 | tf_op jit(solution)/shard_map/ppermute | solution.py:204
  14.0 3.4 %collective-permute-start.1 = (f32[40,128]{1,0:T(8,128)S(1)}, f32[40,128]{1,0:T(8,128)S(1)}, u32[]{:S(2)}, u32[]{:S(2)}) collective-permute-start(f32[40,128]{1,0:T(8,128)S(1)} %bitcast.102), channel_id=1, source_target_pairs={{0,32},{32,64},{64,96},{96,128},{128,160},{160,192},{192,224},{224... | collective-permute-start | bytes 61448 | tf_op jit(solution)/shard_map/ppermute | solution.py:203
  17.5 0.6 add_reduce_fusion
  18.5 1.0 copy.36
  19.5 0.6 compare_reduce_fusion
  20.5 1.7 %convolution_bitcast_fusion.5 = f32[1,512,128]{2,1,0:T(8,128)} fusion(f32[512,512]{1,0:T(8,128)S(1)} %copy-done.1, f32[512,128]{1,0:T(8,128)S(1)} %bitcast.97), kind=kOutput, calls=%fused_computation.7 | convolution fusion | flops 402653184 | bytes 1572864 | tf_op jit(solution)/shard_map/px,cxy->cpy/dot_general | solution.py:109
  22.2 14.1 %all-to-all-start.1 = ((f32[1,32,16,128]{3,2,0,1:T(8,128)}), f32[1,32,16,128]{3,2,0,1:T(8,128)}, u32[]{:S(2)}, u32[]{:S(2)}) async-start(f32[1,32,16,128]{3,2,0,1:T(8,128)} %bitcast.6), calls=%async_computation.1 | async-start | bytes 524288 | tf_op jit(solution)/shard_map/all_to_all | solution.py:178
  36.7 6.8 %collective-permute-start.2 = (f32[10,128]{1,0:T(8,128)S(1)}, f32[10,128]{1,0:T(8,128)S(1)}, u32[]{:S(2)}, u32[]{:S(2)}) collective-permute-start(f32[10,128]{1,0:T(8,128)S(1)} %reshape.233), channel_id=1, source_target_pairs={{1,0},{2,1},{3,2},{4,3},{5,4},{6,5},{7,6},{8,7},{9,8},{10,9},{11,1... | collective-permute-start | bytes 15368 | tf_op jit(solution)/shard_map/ppermute | solution.py:204
  43.7 1.9 %collective-permute-start.3 = (f32[10,128]{1,0:T(8,128)S(1)}, f32[10,128]{1,0:T(8,128)S(1)}, u32[]{:S(2)}, u32[]{:S(2)}) collective-permute-start(f32[10,128]{1,0:T(8,128)S(1)} %reshape.235), channel_id=1, source_target_pairs={{0,1},{1,2},{2,3},{3,4},{4,5},{5,6},{6,7},{7,8},{8,9},{9,10},{10,1... | collective-permute-start | bytes 15368 | tf_op jit(solution)/shard_map/ppermute | solution.py:203
  46.0 6.5 %collective-permute-done.3 = f32[10,128]{1,0:T(8,128)S(1)} collective-permute-done((f32[10,128]{1,0:T(8,128)S(1)}, f32[10,128]{1,0:T(8,128)S(1)}, u32[]{:S(2)}, u32[]{:S(2)}) %collective-permute-start.3) | collective-permute-done | bytes 5152 | tf_op jit(solution)/shard_map/ppermute | solution.py:203
  53.3 0.6 fusion.24
  53.9 2.5 %broadcast_select_fusion.1 = f32[1,1,1,3]{3,2,1,0:T(1,128)S(1)} fusion(pred[]{:T(512)} %compare_reduce_fusion, f32[1,1,1,1]{3,2,1,0:T(1,128)} %bitcast.35, f32[1,1,1,1]{3,2,1,0:T(1,128)} %bitcast.34, f32[1,1,1,1]{3,2,1,0:T(1,128)} %bitcast.29), kind=kLoop, calls=%fused_computation.87 | loop fusion | flops 9 | bytes 25 | tf_op jit(solution)/shard_map/reshape | solution.py:162
  56.5 1.6 %convolution_bitcast_fusion.1 = f32[2,1,32,16,128]{4,2,0,3,1:T(8,128)S(1)} fusion(f32[2,32,32,1]{2,1,0,3:T(8,128)S(1)} %copy-done.8, f32[1,32,16,128]{3,2,0,1:T(8,128)} %all-to-all-done.1), kind=kOutput, calls=%fused_computation.1 | convolution fusion | flops 50331648 | bytes 794624 | tf_op jit(solution)/shard_map/ska,capb->sckpb/dot_general | solution.py:109
  58.2 0.8 copy-done.2
  60.8 1.0 copy.39
  61.8 10.8 %all-to-all-start.2 = ((f32[1,32,17,128]{3,0,2,1:T(1,128)}), f32[1,32,17,128]{3,0,2,1:T(1,128)S(1)}, u32[]{:S(2)}, u32[]{:S(2)}) async-start(f32[1,32,17,128]{3,0,2,1:T(1,128)} %copy.39), calls=%async_computation.2 | async-start | bytes 557056 | tf_op jit(solution)/shard_map/all_to_all | solution.py:183
  73.2 1.3 %multiply_add_fusion.2 = f32[12,32,128]{2,1,0:T(8,128)S(1)} fusion(f32[12,32,128]{2,1,0:T(8,128)S(1)} %copy-done.6, f32[12,32,128]{2,1,0:T(8,128)S(1)} %copy-done.7, f32[]{:T(128)} %bitcast.44, f32[]{:T(128)} %bitcast.43), kind=kLoop, calls=%fused_computation.52 | loop fusion | flops 147456 | bytes 589832 | tf_op jit(solution)/shard_map/add | solution.py:247
  74.5 1.3 %fusion.19 = f32[16,32,128]{2,1,0:T(8,128)S(1)} fusion(f32[20,32,128]{2,1,0:T(8,128)S(1)} %fusion.16, f32[20,32,128]{2,1,0:T(8,128)S(1)} %fusion.10, f32[]{:T(128)} %bitcast.44, f32[]{:T(128)} %bitcast.43), kind=kLoop, calls=%fused_computation.40 | loop fusion | flops 196608 | bytes 786440 | tf_op jit(solution)/shard_map/add | solution.py:248
  75.9 14.4 %all-to-all-done.2 = f32[1,32,17,128]{3,0,2,1:T(1,128)S(1)} async-done(((f32[1,32,17,128]{3,0,2,1:T(1,128)}), f32[1,32,17,128]{3,0,2,1:T(1,128)S(1)}, u32[]{:S(2)}, u32[]{:S(2)}) %all-to-all-start.2) | async-done | bytes 278560 | tf_op jit(solution)/shard_map/all_to_all | solution.py:183
  91.0 0.8 convolution_bitcast_fusion.4
  92.2 17.8 %all_to_all.31 = f32[1,16,33,128]{3,0,2,1:T(1,128)S(1)} all-to-all(f32[1,16,33,128]{3,0,2,1:T(1,128)S(1)} %copy.42), channel_id=1, replica_groups=mesh['kx'=16,'ky'=32] {'kx'}, dimensions={1} | all-to-all | bytes 540672 | tf_op jit(solution)/shard_map/all_to_all | solution.py:190
  111.6 0.7 add.931
  (84 shorter events, 7.4 us)
Async XLA Ops:
  0.6 10.4 %copy-start = (f32[16,32,128]{2,1,0:T(8,128)S(1)}, f32[16,32,128]{2,1,0:T(8,128)}, u32[]{:S(2)}) copy-start(f32[16,32,128]{2,1,0:T(8,128)} %param.15) | copy-start | bytes 786436
  0.6 19.9 %all-to-all-start = ((f32[16,32,128]{2,1,0:T(8,128)}), f32[16,32,128]{2,1,0:T(8,128)S(1)}, u32[]{:S(2)}, u32[]{:S(2)}) async-start(f32[16,32,128]{2,1,0:T(8,128)} %param.15), calls=%async_computation | async-start | bytes 524288 | tf_op jit(solution)/shard_map/all_to_all | solution.py:171
  11.0 0.8 copy-start.4
  11.0 6.4 %copy-start.5 = (f32[16,4096]{1,0:T(8,128)S(1)}, f32[16,4096]{1,0:T(8,128)}, u32[]{:S(2)}) copy-start(f32[16,4096]{1,0:T(8,128)} %param.19) | copy-start | bytes 786436
  11.9 8.3 %collective-permute-start = (f32[40,128]{1,0:T(8,128)S(1)}, f32[40,128]{1,0:T(8,128)S(1)}, u32[]{:S(2)}, u32[]{:S(2)}) collective-permute-start(f32[40,128]{1,0:T(8,128)S(1)} %bitcast.103), channel_id=1, source_target_pairs={{32,0},{64,32},{96,64},{128,96},{160,128},{192,160},{224,192},{256... | collective-permute-start | bytes 61448 | tf_op jit(solution)/shard_map/ppermute | solution.py:204
  14.0 6.3 %collective-permute-start.1 = (f32[40,128]{1,0:T(8,128)S(1)}, f32[40,128]{1,0:T(8,128)S(1)}, u32[]{:S(2)}, u32[]{:S(2)}) collective-permute-start(f32[40,128]{1,0:T(8,128)S(1)} %bitcast.102), channel_id=1, source_target_pairs={{0,32},{32,64},{64,96},{96,128},{128,160},{160,192},{192,224},{224... | collective-permute-start | bytes 61448 | tf_op jit(solution)/shard_map/ppermute | solution.py:203
  18.5 2.1 %copy-start.1 = (f32[512,512]{1,0:T(8,128)S(1)}, f32[512,512]{1,0:T(8,128)}, u32[]{:S(2)}) copy-start(f32[512,512]{1,0:T(8,128)} %constant.85.clone) | copy-start | bytes 3145732
  22.2 34.2 %all-to-all-start.1 = ((f32[1,32,16,128]{3,2,0,1:T(8,128)}), f32[1,32,16,128]{3,2,0,1:T(8,128)}, u32[]{:S(2)}, u32[]{:S(2)}) async-start(f32[1,32,16,128]{3,2,0,1:T(8,128)} %bitcast.6), calls=%async_computation.1 | async-start | bytes 524288 | tf_op jit(solution)/shard_map/all_to_all | solution.py:178
  36.7 8.9 %collective-permute-start.2 = (f32[10,128]{1,0:T(8,128)S(1)}, f32[10,128]{1,0:T(8,128)S(1)}, u32[]{:S(2)}, u32[]{:S(2)}) collective-permute-start(f32[10,128]{1,0:T(8,128)S(1)} %reshape.233), channel_id=1, source_target_pairs={{1,0},{2,1},{3,2},{4,3},{5,4},{6,5},{7,6},{8,7},{9,8},{10,9},{11,1... | collective-permute-start | bytes 15368 | tf_op jit(solution)/shard_map/ppermute | solution.py:204
  43.7 8.7 %collective-permute-start.3 = (f32[10,128]{1,0:T(8,128)S(1)}, f32[10,128]{1,0:T(8,128)S(1)}, u32[]{:S(2)}, u32[]{:S(2)}) collective-permute-start(f32[10,128]{1,0:T(8,128)S(1)} %reshape.235), channel_id=1, source_target_pairs={{0,1},{1,2},{2,3},{3,4},{4,5},{5,6},{6,7},{7,8},{8,9},{9,10},{10,1... | collective-permute-start | bytes 15368 | tf_op jit(solution)/shard_map/ppermute | solution.py:203
  53.3 3.2 %copy-start.8 = (f32[2,32,32,1]{2,1,0,3:T(8,128)S(1)}, f32[2,32,32,1]{2,1,0,3:T(8,128)}, u32[]{:S(2)}) copy-start(f32[2,32,32,1]{2,1,0,3:T(8,128)} %constant.98) | copy-start | bytes 24580
  56.4 1.6 %copy-start.9 = (f32[32,128]{1,0:T(8,128)S(1)}, f32[32,128]{1,0:T(8,128)}, u32[]{:S(2)}) copy-start(f32[32,128]{1,0:T(8,128)} %constant.95) | copy-start | bytes 49156
  56.4 1.6 %copy-start.10 = (f32[32,128]{1,0:T(8,128)S(1)}, f32[32,128]{1,0:T(8,128)}, u32[]{:S(2)}) copy-start(f32[32,128]{1,0:T(8,128)} %constant.96) | copy-start | bytes 49156
  58.1 1.0 copy-start.2
  58.1 1.0 copy-start.3
  61.8 10.8 %copy-start.11 = (f32[2]{0:T(128)S(1)}, f32[2]{0:T(128)}, u32[]{:S(2)}) copy-start(f32[2]{0:T(128)} %param.20) | copy-start | bytes 28
  61.8 11.4 %copy-start.6 = (f32[12,32,128]{2,1,0:T(8,128)S(1)}, f32[12,32,128]{2,1,0:T(8,128)}, u32[]{:S(2)}) copy-start(f32[12,32,128]{2,1,0:T(8,128)} %param.18) | copy-start | bytes 589828
  61.8 11.4 %copy-start.7 = (f32[12,32,128]{2,1,0:T(8,128)S(1)}, f32[12,32,128]{2,1,0:T(8,128)}, u32[]{:S(2)}) copy-start(f32[12,32,128]{2,1,0:T(8,128)} %param.17) | copy-start | bytes 589828
  61.8 28.5 %all-to-all-start.2 = ((f32[1,32,17,128]{3,0,2,1:T(1,128)}), f32[1,32,17,128]{3,0,2,1:T(1,128)S(1)}, u32[]{:S(2)}, u32[]{:S(2)}) async-start(f32[1,32,17,128]{3,0,2,1:T(1,128)} %copy.39), calls=%async_computation.2 | async-start | bytes 557056 | tf_op jit(solution)/shard_map/all_to_all | solution.py:183

commit v13 on v12

--- a/solution.py
+++ b/solution.py
@@ -39,7 +39,7 @@
     return summed
 
 
-def commutator(coupled, packed_state_matrix):
+def commutator(coupled, packed_state_matrix, drift):
     coupled_real, coupled_imaginary = unpack(coupled)
     state_real, state_imaginary = unpack(packed_state_matrix)
 
@@ -82,27 +82,8 @@
         real_value, imaginary_value = element(upper_band, lower_band)
         upper_real.append(imaginary_value)
         upper_imaginary.append(-real_value)
-    return jnp.stack(diagonal + upper_real + upper_imaginary)
-
-
-def slope_terms(
-    packed_state_matrix,
-    energies,
-    self_energy,
-    gradient_x,
-    gradient_y,
-    dipole_x,
-    dipole_y,
-    driving_field,
-):
-    field_x = driving_field[0]
-    field_y = driving_field[1]
-    coupled = jnp.concatenate(
-        [energies + self_energy[0:4], self_energy[4:16] + field_x * dipole_x + field_y * dipole_y]
-    )
-    rotation = commutator(coupled, packed_state_matrix)
-    drift = rotation + field_x * gradient_x + field_y * gradient_y
-    return jnp.concatenate([drift[0:4], drift[4:16] - DEPHASING * packed_state_matrix[4:16]])
+    parts = diagonal + upper_real + upper_imaginary
+    return jnp.stack([part + drift[number] for number, part in enumerate(parts)])
 
 
 def contract(einsum_form, left, right):
@@ -258,7 +239,7 @@
     shielding_multiplier = 1.0 / (1.0 + SHIELDING_LEVEL * totals[0])
     self_energy = -shielding_multiplier * convolved
     coupled = jnp.concatenate([energies + self_energy[0:4], self_energy[4:16] + dipole_field])
-    section_slope = commutator(coupled, packed_state_matrix) + drift
+    section_slope = commutator(coupled, packed_state_matrix, drift)
     field_next = driving_field - COUPLING * totals[1:3]
     return (section_slope, field_next)
 

time: 113 us -> 113 us (level)
    unnamed x26 -> x28, local copies, waits for them, and re-layouts: 1.77 us -> 2.47 us
where the time goes in v13:
time: 113 us
  starting transfers between devices  49.5 us (44%)
  waiting for transfers between devices  21.2 us (19%)
  blocking collectives  17.7 us (16%)
  other arithmetic  10.3 us (9%)
  local copies, waits for them, and re-layouts  7 us (6%)
  matrix products  5.61 us (5%)
  between operations  1.21 us (1%)
    all_to_all x1, blocking collectives, convolve_and_sum(): back = lax.all_to_all(final, 'kx', split_axis=1, concat_axis=0, tiled=True)  17.7 us
    all_to_all x1, waiting for transfers between devices, convolve_and_sum(): lax.all_to_all(back_y, 'ky', split_axis=1, concat_axis=1, tiled=True)  14.5 us
    all_to_all x1, starting transfers between devices, convolve_and_sum(): lax.all_to_all(split, 'ky', split_axis=1, concat_axis=1, tiled=True)  14.1 us
    all_to_all x1, starting transfers between devices, convolve_and_sum(): lax.all_to_all(back_y, 'ky', split_axis=1, concat_axis=1, tiled=True)  10.8 us
    all_to_all x1, starting transfers between devices, convolve_and_sum(): lax.all_to_all(source, 'kx', split_axis=0, concat_axis=1, tiled=True)  10.3 us
    ppermute x2, starting transfers between devices, neighbours(): lax.ppermute(initial.reshape(dense), axis, down).reshape(initial.shape)  8.9 us
    ppermute x2, waiting for transfers between devices, neighbours(): before = lax.ppermute(last.reshape(dense), axis, up).reshape(last.shape)  6.68 us
    dot_general x6, matrix products, contract(): jnp.einsum(einsum_form, left, right, precision=lax.Precision.HIGHEST, pre...  5.61 us
  transfers between devices with their start and end apart: 7, of which 3 were waited for; matrix products, arithmetic and copies ran while one was open for 10% of the time, Pallas kernels for 0%

profile of v13, /device:TPU:1, one launch (start us, length us, event | category | flops | bytes accessed | tf_op | source)
XLA Modules:
  0.0 112.5 jit_solution(9769324590875746554)
XLA Ops:
  0.6 10.3 %all-to-all-start = ((f32[16,32,128]{2,1,0:T(8,128)}), f32[16,32,128]{2,1,0:T(8,128)S(1)}, u32[]{:S(2)}, u32[]{:S(2)}) async-start(f32[16,32,128]{2,1,0:T(8,128)} %param.15), calls=%async_computation | async-start | bytes 524288 | tf_op jit(solution)/shard_map/all_to_all | solution.py:152
  11.0 0.8 copy-done.4
  11.9 2.1 %collective-permute-start = (f32[40,128]{1,0:T(8,128)S(1)}, f32[40,128]{1,0:T(8,128)S(1)}, u32[]{:S(2)}, u32[]{:S(2)}) collective-permute-start(f32[40,128]{1,0:T(8,128)S(1)} %bitcast.103), channel_id=1, source_target_pairs={{32,0},{64,32},{96,64},{128,96},{160,128},{192,160},{224,192},{256... | collective-permute-start | bytes 61448 | tf_op jit(solution)/shard_map/ppermute | solution.py:185
  14.0 3.4 %collective-permute-start.1 = (f32[40,128]{1,0:T(8,128)S(1)}, f32[40,128]{1,0:T(8,128)S(1)}, u32[]{:S(2)}, u32[]{:S(2)}) collective-permute-start(f32[40,128]{1,0:T(8,128)S(1)} %bitcast.102), channel_id=1, source_target_pairs={{0,32},{32,64},{64,96},{96,128},{128,160},{160,192},{192,224},{224... | collective-permute-start | bytes 61448 | tf_op jit(solution)/shard_map/ppermute | solution.py:184
  18.4 1.0 copy.36
  19.5 0.7 compare_reduce_fusion
  20.5 1.7 %convolution_bitcast_fusion.5 = f32[1,512,128]{2,1,0:T(8,128)} fusion(f32[512,512]{1,0:T(8,128)S(1)} %copy-done.1, f32[512,128]{1,0:T(8,128)S(1)} %bitcast.97), kind=kOutput, calls=%fused_computation.7 | convolution fusion | flops 402653184 | bytes 1572864 | tf_op jit(solution)/shard_map/px,cxy->cpy/dot_general | solution.py:90
  22.2 14.1 %all-to-all-start.1 = ((f32[1,32,16,128]{3,2,0,1:T(8,128)}), f32[1,32,16,128]{3,2,0,1:T(8,128)}, u32[]{:S(2)}, u32[]{:S(2)}) async-start(f32[1,32,16,128]{3,2,0,1:T(8,128)} %bitcast.6), calls=%async_computation.1 | async-start | bytes 524288 | tf_op jit(solution)/shard_map/all_to_all | solution.py:159
  36.7 6.8 %collective-permute-start.2 = (f32[10,128]{1,0:T(8,128)S(1)}, f32[10,128]{1,0:T(8,128)S(1)}, u32[]{:S(2)}, u32[]{:S(2)}) collective-permute-start(f32[10,128]{1,0:T(8,128)S(1)} %reshape.233), channel_id=1, source_target_pairs={{1,0},{2,1},{3,2},{4,3},{5,4},{6,5},{7,6},{8,7},{9,8},{10,9},{11,1... | collective-permute-start | bytes 15368 | tf_op jit(solution)/shard_map/ppermute | solution.py:185
  43.7 1.9 %collective-permute-start.3 = (f32[10,128]{1,0:T(8,128)S(1)}, f32[10,128]{1,0:T(8,128)S(1)}, u32[]{:S(2)}, u32[]{:S(2)}) collective-permute-start(f32[10,128]{1,0:T(8,128)S(1)} %reshape.235), channel_id=1, source_target_pairs={{0,1},{1,2},{2,3},{3,4},{4,5},{5,6},{6,7},{7,8},{8,9},{9,10},{10,1... | collective-permute-start | bytes 15368 | tf_op jit(solution)/shard_map/ppermute | solution.py:184
  46.0 6.5 %collective-permute-done.3 = f32[10,128]{1,0:T(8,128)S(1)} collective-permute-done((f32[10,128]{1,0:T(8,128)S(1)}, f32[10,128]{1,0:T(8,128)S(1)}, u32[]{:S(2)}, u32[]{:S(2)}) %collective-permute-start.3) | collective-permute-done | bytes 5152 | tf_op jit(solution)/shard_map/ppermute | solution.py:184
  53.3 0.7 fusion.24
  54.0 2.6 %broadcast_select_fusion.1 = f32[1,1,1,3]{3,2,1,0:T(1,128)S(1)} fusion(pred[]{:T(512)} %compare_reduce_fusion, f32[1,1,1,1]{3,2,1,0:T(1,128)} %bitcast.35, f32[1,1,1,1]{3,2,1,0:T(1,128)} %bitcast.34, f32[1,1,1,1]{3,2,1,0:T(1,128)} %bitcast.29), kind=kLoop, calls=%fused_computation.87 | loop fusion | flops 9 | bytes 25 | tf_op jit(solution)/shard_map/reshape | solution.py:143
  56.6 1.6 %convolution_bitcast_fusion.1 = f32[2,1,32,16,128]{4,2,0,3,1:T(8,128)S(1)} fusion(f32[2,32,32,1]{2,1,0,3:T(8,128)S(1)} %copy-done.8, f32[1,32,16,128]{3,2,0,1:T(8,128)} %all-to-all-done.1), kind=kOutput, calls=%fused_computation.1 | convolution fusion | flops 50331648 | bytes 794624 | tf_op jit(solution)/shard_map/ska,capb->sckpb/dot_general | solution.py:90
  58.3 0.8 copy-done.2
  60.9 1.0 copy.39
  61.9 10.8 %all-to-all-start.2 = ((f32[1,32,17,128]{3,0,2,1:T(1,128)}), f32[1,32,17,128]{3,0,2,1:T(1,128)S(1)}, u32[]{:S(2)}, u32[]{:S(2)}) async-start(f32[1,32,17,128]{3,0,2,1:T(1,128)} %copy.39), calls=%async_computation.2 | async-start | bytes 557056 | tf_op jit(solution)/shard_map/all_to_all | solution.py:164
  73.3 1.3 %multiply_add_fusion.2 = f32[12,32,128]{2,1,0:T(8,128)S(1)} fusion(f32[12,32,128]{2,1,0:T(8,128)S(1)} %copy-done.6, f32[12,32,128]{2,1,0:T(8,128)S(1)} %copy-done.7, f32[]{:T(128)} %bitcast.44, f32[]{:T(128)} %bitcast.43), kind=kLoop, calls=%fused_computation.52 | loop fusion | flops 147456 | bytes 589832 | tf_op jit(solution)/shard_map/add | solution.py:228
  74.7 1.3 %fusion.19 = f32[16,32,128]{2,1,0:T(8,128)S(1)} fusion(f32[20,32,128]{2,1,0:T(8,128)S(1)} %fusion.16, f32[20,32,128]{2,1,0:T(8,128)S(1)} %fusion.10, f32[]{:T(128)} %bitcast.44, f32[]{:T(128)} %bitcast.43), kind=kLoop, calls=%fused_computation.40 | loop fusion | flops 196608 | bytes 786440 | tf_op jit(solution)/shard_map/add | solution.py:229
  76.1 14.5 %all-to-all-done.2 = f32[1,32,17,128]{3,0,2,1:T(1,128)S(1)} async-done(((f32[1,32,17,128]{3,0,2,1:T(1,128)}), f32[1,32,17,128]{3,0,2,1:T(1,128)S(1)}, u32[]{:S(2)}, u32[]{:S(2)}) %all-to-all-start.2) | async-done | bytes 278560 | tf_op jit(solution)/shard_map/all_to_all | solution.py:164
  90.6 0.6 fusion.25
  91.3 0.8 convolution_bitcast_fusion.4
  92.5 17.7 %all_to_all.31 = f32[1,16,33,128]{3,0,2,1:T(1,128)S(1)} all-to-all(f32[1,16,33,128]{3,0,2,1:T(1,128)S(1)} %copy.42), channel_id=1, replica_groups=mesh['kx'=16,'ky'=32] {'kx'}, dimensions={1} | all-to-all | bytes 540672 | tf_op jit(solution)/shard_map/all_to_all | solution.py:171
  111.8 0.7 copy-done.12
  (85 shorter events, 7.5 us)
Async XLA Ops:
  0.6 10.4 %copy-start = (f32[16,32,128]{2,1,0:T(8,128)S(1)}, f32[16,32,128]{2,1,0:T(8,128)}, u32[]{:S(2)}) copy-start(f32[16,32,128]{2,1,0:T(8,128)} %param.15) | copy-start | bytes 786436
  0.6 19.9 %all-to-all-start = ((f32[16,32,128]{2,1,0:T(8,128)}), f32[16,32,128]{2,1,0:T(8,128)S(1)}, u32[]{:S(2)}, u32[]{:S(2)}) async-start(f32[16,32,128]{2,1,0:T(8,128)} %param.15), calls=%async_computation | async-start | bytes 524288 | tf_op jit(solution)/shard_map/all_to_all | solution.py:152
  11.0 0.8 copy-start.4
  11.0 6.4 %copy-start.5 = (f32[16,4096]{1,0:T(8,128)S(1)}, f32[16,4096]{1,0:T(8,128)}, u32[]{:S(2)}) copy-start(f32[16,4096]{1,0:T(8,128)} %param.19) | copy-start | bytes 786436
  11.9 8.3 %collective-permute-start = (f32[40,128]{1,0:T(8,128)S(1)}, f32[40,128]{1,0:T(8,128)S(1)}, u32[]{:S(2)}, u32[]{:S(2)}) collective-permute-start(f32[40,128]{1,0:T(8,128)S(1)} %bitcast.103), channel_id=1, source_target_pairs={{32,0},{64,32},{96,64},{128,96},{160,128},{192,160},{224,192},{256... | collective-permute-start | bytes 61448 | tf_op jit(solution)/shard_map/ppermute | solution.py:185
  14.0 6.3 %collective-permute-start.1 = (f32[40,128]{1,0:T(8,128)S(1)}, f32[40,128]{1,0:T(8,128)S(1)}, u32[]{:S(2)}, u32[]{:S(2)}) collective-permute-start(f32[40,128]{1,0:T(8,128)S(1)} %bitcast.102), channel_id=1, source_target_pairs={{0,32},{32,64},{64,96},{96,128},{128,160},{160,192},{192,224},{224... | collective-permute-start | bytes 61448 | tf_op jit(solution)/shard_map/ppermute | solution.py:184
  18.4 2.1 %copy-start.1 = (f32[512,512]{1,0:T(8,128)S(1)}, f32[512,512]{1,0:T(8,128)}, u32[]{:S(2)}) copy-start(f32[512,512]{1,0:T(8,128)} %constant.85.clone) | copy-start | bytes 3145732
  22.2 34.4 %all-to-all-start.1 = ((f32[1,32,16,128]{3,2,0,1:T(8,128)}), f32[1,32,16,128]{3,2,0,1:T(8,128)}, u32[]{:S(2)}, u32[]{:S(2)}) async-start(f32[1,32,16,128]{3,2,0,1:T(8,128)} %bitcast.6), calls=%async_computation.1 | async-start | bytes 524288 | tf_op jit(solution)/shard_map/all_to_all | solution.py:159
  36.7 8.9 %collective-permute-start.2 = (f32[10,128]{1,0:T(8,128)S(1)}, f32[10,128]{1,0:T(8,128)S(1)}, u32[]{:S(2)}, u32[]{:S(2)}) collective-permute-start(f32[10,128]{1,0:T(8,128)S(1)} %reshape.233), channel_id=1, source_target_pairs={{1,0},{2,1},{3,2},{4,3},{5,4},{6,5},{7,6},{8,7},{9,8},{10,9},{11,1... | collective-permute-start | bytes 15368 | tf_op jit(solution)/shard_map/ppermute | solution.py:185
  43.7 8.7 %collective-permute-start.3 = (f32[10,128]{1,0:T(8,128)S(1)}, f32[10,128]{1,0:T(8,128)S(1)}, u32[]{:S(2)}, u32[]{:S(2)}) collective-permute-start(f32[10,128]{1,0:T(8,128)S(1)} %reshape.235), channel_id=1, source_target_pairs={{0,1},{1,2},{2,3},{3,4},{4,5},{5,6},{6,7},{7,8},{8,9},{9,10},{10,1... | collective-permute-start | bytes 15368 | tf_op jit(solution)/shard_map/ppermute | solution.py:184
  53.3 3.4 %copy-start.8 = (f32[2,32,32,1]{2,1,0,3:T(8,128)S(1)}, f32[2,32,32,1]{2,1,0,3:T(8,128)}, u32[]{:S(2)}) copy-start(f32[2,32,32,1]{2,1,0,3:T(8,128)} %constant.98) | copy-start | bytes 24580
  56.6 1.6 %copy-start.9 = (f32[32,128]{1,0:T(8,128)S(1)}, f32[32,128]{1,0:T(8,128)}, u32[]{:S(2)}) copy-start(f32[32,128]{1,0:T(8,128)} %constant.95) | copy-start | bytes 49156
  56.6 1.6 %copy-start.10 = (f32[32,128]{1,0:T(8,128)S(1)}, f32[32,128]{1,0:T(8,128)}, u32[]{:S(2)}) copy-start(f32[32,128]{1,0:T(8,128)} %constant.96) | copy-start | bytes 49156
  58.2 1.0 copy-start.2
  58.2 1.0 copy-start.3
  61.9 10.8 %copy-start.11 = (f32[2]{0:T(128)S(1)}, f32[2]{0:T(128)}, u32[]{:S(2)}) copy-start(f32[2]{0:T(128)} %param.20) | copy-start | bytes 28
  61.9 11.4 %copy-start.6 = (f32[12,32,128]{2,1,0:T(8,128)S(1)}, f32[12,32,128]{2,1,0:T(8,128)}, u32[]{:S(2)}) copy-start(f32[12,32,128]{2,1,0:T(8,128)} %param.18) | copy-start | bytes 589828
  61.9 11.4 %copy-start.7 = (f32[12,32,128]{2,1,0:T(8,128)S(1)}, f32[12,32,128]{2,1,0:T(8,128)}, u32[]{:S(2)}) copy-start(f32[12,32,128]{2,1,0:T(8,128)} %param.17) | copy-start | bytes 589828
  61.9 28.6 %all-to-all-start.2 = ((f32[1,32,17,128]{3,0,2,1:T(1,128)}), f32[1,32,17,128]{3,0,2,1:T(1,128)S(1)}, u32[]{:S(2)}, u32[]{:S(2)}) async-start(f32[1,32,17,128]{3,0,2,1:T(1,128)} %copy.39), calls=%async_computation.2 | async-start | bytes 557056 | tf_op jit(solution)/shard_map/all_to_all | solution.py:164
  111.8 0.7 copy-start.12

commit v14 on v12

--- a/solution.py
+++ b/solution.py
@@ -180,13 +180,12 @@
     weight = interaction.reshape(row_count, column_count, ky_devices).transpose(2, 0, 1)
     weighted = spectrum * (weight * (1.0 / primitive_tile_total))[None]
     back_y = with_sums(hartley_y_transposed(weighted, tables), local_sums(), 2)
-    returned = lax.all_to_all(back_y, "ky", split_axis=1, concat_axis=1, tiled=True)
+    returned = before_return(lax.all_to_all(back_y, "ky", split_axis=1, concat_axis=1, tiled=True))
     ky_sums = jnp.sum(returned[0, :, row_count, 0:sum_count], axis=0)
     returned = returned[:, :, 0:row_count].reshape(components, x_length, column_count)
     final = contract("px,cpy->cxy", tables["cas_x"], returned)
     rows_local = x_length // kx_devices
     final = with_sums(final.reshape(components, kx_devices, rows_local, column_count), ky_sums, 2)
-    final = before_return(final)
     back = lax.all_to_all(final, "kx", split_axis=1, concat_axis=0, tiled=True)
     totals = jnp.sum(back[::components, 0, rows_local, 0:sum_count], axis=0) / primitive_tile_total
     convolved = back[:, 0, 0:rows_local].reshape(components * kx_devices, rows_local, column_count)

time: 113 us -> 113 us (level)
  no operation moved by 1% of the time
where the time goes in v14:
time: 113 us; the launch traced here: 112 us
  starting transfers between devices  49.5 us (44%)
  waiting for transfers between devices  21.1 us (19%)
  blocking collectives  17.8 us (16%)
  other arithmetic  10.8 us (10%)
  local copies, waits for them, and re-layouts  6.34 us (6%)
  matrix products  5.61 us (5%)
  between operations  1.21 us (1%)
    all_to_all x1, blocking collectives, convolve_and_sum(): back = lax.all_to_all(final, 'kx', split_axis=1, concat_axis=0, tiled=True)  17.8 us
    all_to_all x1, waiting for transfers between devices, convolve_and_sum(): lax.all_to_all(back_y, 'ky', split_axis=1, concat_axis=1, tiled=True)  14.4 us
    all_to_all x1, starting transfers between devices, convolve_and_sum(): lax.all_to_all(split, 'ky', split_axis=1, concat_axis=1, tiled=True)  14.1 us
    all_to_all x1, starting transfers between devices, convolve_and_sum(): lax.all_to_all(back_y, 'ky', split_axis=1, concat_axis=1, tiled=True)  10.8 us
    all_to_all x1, starting transfers between devices, convolve_and_sum(): lax.all_to_all(source, 'kx', split_axis=0, concat_axis=1, tiled=True)  10.3 us
    ppermute x2, starting transfers between devices, neighbours(): lax.ppermute(initial.reshape(dense), axis, down).reshape(initial.shape)  8.9 us
    ppermute x2, waiting for transfers between devices, neighbours(): before = lax.ppermute(last.reshape(dense), axis, up).reshape(last.shape)  6.68 us
    dot_general x6, matrix products, contract(): jnp.einsum(einsum_form, left, right, precision=lax.Precision.HIGHEST, pre...  5.61 us
  transfers between devices with their start and end apart: 7, of which 3 were waited for; matrix products, arithmetic and copies ran while one was open for 10% of the time, Pallas kernels for 0%

profile of v14, /device:TPU:1, one launch (start us, length us, event | category | flops | bytes accessed | tf_op | source)
XLA Modules:
  0.0 112.4 jit_solution(16608190929234943852)
XLA Ops:
  0.6 10.3 %all-to-all-start = ((f32[16,32,128]{2,1,0:T(8,128)}), f32[16,32,128]{2,1,0:T(8,128)S(1)}, u32[]{:S(2)}, u32[]{:S(2)}) async-start(f32[16,32,128]{2,1,0:T(8,128)} %param.15), calls=%async_computation | async-start | bytes 524288 | tf_op jit(solution)/shard_map/all_to_all | solution.py:171
  11.0 0.8 copy-done.4
  11.9 2.1 %collective-permute-start = (f32[40,128]{1,0:T(8,128)S(1)}, f32[40,128]{1,0:T(8,128)S(1)}, u32[]{:S(2)}, u32[]{:S(2)}) collective-permute-start(f32[40,128]{1,0:T(8,128)S(1)} %bitcast.101), channel_id=1, source_target_pairs={{32,0},{64,32},{96,64},{128,96},{160,128},{192,160},{224,192},{256... | collective-permute-start | bytes 61448 | tf_op jit(solution)/shard_map/ppermute | solution.py:203
  14.0 3.4 %collective-permute-start.1 = (f32[40,128]{1,0:T(8,128)S(1)}, f32[40,128]{1,0:T(8,128)S(1)}, u32[]{:S(2)}, u32[]{:S(2)}) collective-permute-start(f32[40,128]{1,0:T(8,128)S(1)} %bitcast.100), channel_id=1, source_target_pairs={{0,32},{32,64},{64,96},{96,128},{128,160},{160,192},{192,224},{224... | collective-permute-start | bytes 61448 | tf_op jit(solution)/shard_map/ppermute | solution.py:202
  17.5 0.6 add_reduce_fusion
  18.5 1.0 copy.36
  19.5 0.6 compare_reduce_fusion
  20.5 1.7 %convolution_bitcast_fusion.5 = f32[1,512,128]{2,1,0:T(8,128)} fusion(f32[512,512]{1,0:T(8,128)S(1)} %copy-done.1, f32[512,128]{1,0:T(8,128)S(1)} %bitcast.95), kind=kOutput, calls=%fused_computation.7 | convolution fusion | flops 402653184 | bytes 1572864 | tf_op jit(solution)/shard_map/px,cxy->cpy/dot_general | solution.py:109
  22.2 14.1 %all-to-all-start.1 = ((f32[1,32,16,128]{3,2,0,1:T(8,128)}), f32[1,32,16,128]{3,2,0,1:T(8,128)}, u32[]{:S(2)}, u32[]{:S(2)}) async-start(f32[1,32,16,128]{3,2,0,1:T(8,128)} %bitcast.6), calls=%async_computation.1 | async-start | bytes 524288 | tf_op jit(solution)/shard_map/all_to_all | solution.py:178
  36.7 6.8 %collective-permute-start.2 = (f32[10,128]{1,0:T(8,128)S(1)}, f32[10,128]{1,0:T(8,128)S(1)}, u32[]{:S(2)}, u32[]{:S(2)}) collective-permute-start(f32[10,128]{1,0:T(8,128)S(1)} %reshape.233), channel_id=1, source_target_pairs={{1,0},{2,1},{3,2},{4,3},{5,4},{6,5},{7,6},{8,7},{9,8},{10,9},{11,1... | collective-permute-start | bytes 15368 | tf_op jit(solution)/shard_map/ppermute | solution.py:203
  43.7 1.9 %collective-permute-start.3 = (f32[10,128]{1,0:T(8,128)S(1)}, f32[10,128]{1,0:T(8,128)S(1)}, u32[]{:S(2)}, u32[]{:S(2)}) collective-permute-start(f32[10,128]{1,0:T(8,128)S(1)} %reshape.235), channel_id=1, source_target_pairs={{0,1},{1,2},{2,3},{3,4},{4,5},{5,6},{6,7},{7,8},{8,9},{9,10},{10,1... | collective-permute-start | bytes 15368 | tf_op jit(solution)/shard_map/ppermute | solution.py:202
  46.0 6.5 %collective-permute-done.3 = f32[10,128]{1,0:T(8,128)S(1)} collective-permute-done((f32[10,128]{1,0:T(8,128)S(1)}, f32[10,128]{1,0:T(8,128)S(1)}, u32[]{:S(2)}, u32[]{:S(2)}) %collective-permute-start.3) | collective-permute-done | bytes 5152 | tf_op jit(solution)/shard_map/ppermute | solution.py:202
  53.3 0.6 fusion.24
  53.9 2.5 %broadcast_select_fusion.1 = f32[1,1,1,3]{3,2,1,0:T(1,128)S(1)} fusion(pred[]{:T(512)} %compare_reduce_fusion, f32[1,1,1,1]{3,2,1,0:T(1,128)} %bitcast.35, f32[1,1,1,1]{3,2,1,0:T(1,128)} %bitcast.34, f32[1,1,1,1]{3,2,1,0:T(1,128)} %bitcast.29), kind=kLoop, calls=%fused_computation.87 | loop fusion | flops 9 | bytes 25 | tf_op jit(solution)/shard_map/reshape | solution.py:162
  56.5 1.6 %convolution_bitcast_fusion.1 = f32[2,1,32,16,128]{4,2,0,3,1:T(8,128)S(1)} fusion(f32[2,32,32,1]{2,1,0,3:T(8,128)S(1)} %copy-done.8, f32[1,32,16,128]{3,2,0,1:T(8,128)} %all-to-all-done.1), kind=kOutput, calls=%fused_computation.1 | convolution fusion | flops 50331648 | bytes 794624 | tf_op jit(solution)/shard_map/ska,capb->sckpb/dot_general | solution.py:109
  58.2 0.8 copy-done.2
  60.8 1.0 copy.39
  61.8 10.8 %all-to-all-start.2 = ((f32[1,32,17,128]{3,0,2,1:T(1,128)}), f32[1,32,17,128]{3,0,2,1:T(1,128)S(1)}, u32[]{:S(2)}, u32[]{:S(2)}) async-start(f32[1,32,17,128]{3,0,2,1:T(1,128)} %copy.39), calls=%async_computation.2 | async-start | bytes 557056 | tf_op jit(solution)/shard_map/all_to_all | solution.py:183
  73.2 1.3 %multiply_add_fusion.2 = f32[12,32,128]{2,1,0:T(8,128)S(1)} fusion(f32[12,32,128]{2,1,0:T(8,128)S(1)} %copy-done.6, f32[12,32,128]{2,1,0:T(8,128)S(1)} %copy-done.7, f32[]{:T(128)} %bitcast.38, f32[]{:T(128)} %bitcast.37), kind=kLoop, calls=%fused_computation.52 | loop fusion | flops 147456 | bytes 589832 | tf_op jit(solution)/shard_map/add | solution.py:246
  74.5 1.3 %fusion.19 = f32[16,32,128]{2,1,0:T(8,128)S(1)} fusion(f32[20,32,128]{2,1,0:T(8,128)S(1)} %fusion.16, f32[20,32,128]{2,1,0:T(8,128)S(1)} %fusion.10, f32[]{:T(128)} %bitcast.38, f32[]{:T(128)} %bitcast.37), kind=kLoop, calls=%fused_computation.40 | loop fusion | flops 196608 | bytes 786440 | tf_op jit(solution)/shard_map/add | solution.py:247
  75.9 14.4 %all-to-all-done.2 = f32[1,32,17,128]{3,0,2,1:T(1,128)S(1)} async-done(((f32[1,32,17,128]{3,0,2,1:T(1,128)}), f32[1,32,17,128]{3,0,2,1:T(1,128)S(1)}, u32[]{:S(2)}, u32[]{:S(2)}) %all-to-all-start.2) | async-done | bytes 278560 | tf_op jit(solution)/shard_map/all_to_all | solution.py:183
  90.4 0.8 convolution_bitcast_fusion.4
  92.3 17.8 %all_to_all.31 = f32[1,16,33,128]{3,0,2,1:T(1,128)S(1)} all-to-all(f32[1,16,33,128]{3,0,2,1:T(1,128)S(1)} %copy.42), channel_id=1, replica_groups=mesh['kx'=16,'ky'=32] {'kx'}, dimensions={1} | all-to-all | bytes 540672 | tf_op jit(solution)/shard_map/all_to_all | solution.py:189
  111.6 0.7 add.931
  (85 shorter events, 7.4 us)
Async XLA Ops:
  0.6 10.4 %copy-start = (f32[16,32,128]{2,1,0:T(8,128)S(1)}, f32[16,32,128]{2,1,0:T(8,128)}, u32[]{:S(2)}) copy-start(f32[16,32,128]{2,1,0:T(8,128)} %param.15) | copy-start | bytes 786436
  0.6 19.9 %all-to-all-start = ((f32[16,32,128]{2,1,0:T(8,128)}), f32[16,32,128]{2,1,0:T(8,128)S(1)}, u32[]{:S(2)}, u32[]{:S(2)}) async-start(f32[16,32,128]{2,1,0:T(8,128)} %param.15), calls=%async_computation | async-start | bytes 524288 | tf_op jit(solution)/shard_map/all_to_all | solution.py:171
  11.0 0.8 copy-start.4
  11.0 6.4 %copy-start.5 = (f32[16,4096]{1,0:T(8,128)S(1)}, f32[16,4096]{1,0:T(8,128)}, u32[]{:S(2)}) copy-start(f32[16,4096]{1,0:T(8,128)} %param.19) | copy-start | bytes 786436
  11.9 8.3 %collective-permute-start = (f32[40,128]{1,0:T(8,128)S(1)}, f32[40,128]{1,0:T(8,128)S(1)}, u32[]{:S(2)}, u32[]{:S(2)}) collective-permute-start(f32[40,128]{1,0:T(8,128)S(1)} %bitcast.101), channel_id=1, source_target_pairs={{32,0},{64,32},{96,64},{128,96},{160,128},{192,160},{224,192},{256... | collective-permute-start | bytes 61448 | tf_op jit(solution)/shard_map/ppermute | solution.py:203
  14.0 6.3 %collective-permute-start.1 = (f32[40,128]{1,0:T(8,128)S(1)}, f32[40,128]{1,0:T(8,128)S(1)}, u32[]{:S(2)}, u32[]{:S(2)}) collective-permute-start(f32[40,128]{1,0:T(8,128)S(1)} %bitcast.100), channel_id=1, source_target_pairs={{0,32},{32,64},{64,96},{96,128},{128,160},{160,192},{192,224},{224... | collective-permute-start | bytes 61448 | tf_op jit(solution)/shard_map/ppermute | solution.py:202
  18.5 2.1 %copy-start.1 = (f32[512,512]{1,0:T(8,128)S(1)}, f32[512,512]{1,0:T(8,128)}, u32[]{:S(2)}) copy-start(f32[512,512]{1,0:T(8,128)} %constant.85.clone) | copy-start | bytes 3145732
  22.2 34.2 %all-to-all-start.1 = ((f32[1,32,16,128]{3,2,0,1:T(8,128)}), f32[1,32,16,128]{3,2,0,1:T(8,128)}, u32[]{:S(2)}, u32[]{:S(2)}) async-start(f32[1,32,16,128]{3,2,0,1:T(8,128)} %bitcast.6), calls=%async_computation.1 | async-start | bytes 524288 | tf_op jit(solution)/shard_map/all_to_all | solution.py:178
  36.7 8.9 %collective-permute-start.2 = (f32[10,128]{1,0:T(8,128)S(1)}, f32[10,128]{1,0:T(8,128)S(1)}, u32[]{:S(2)}, u32[]{:S(2)}) collective-permute-start(f32[10,128]{1,0:T(8,128)S(1)} %reshape.233), channel_id=1, source_target_pairs={{1,0},{2,1},{3,2},{4,3},{5,4},{6,5},{7,6},{8,7},{9,8},{10,9},{11,1... | collective-permute-start | bytes 15368 | tf_op jit(solution)/shard_map/ppermute | solution.py:203
  43.7 8.7 %collective-permute-start.3 = (f32[10,128]{1,0:T(8,128)S(1)}, f32[10,128]{1,0:T(8,128)S(1)}, u32[]{:S(2)}, u32[]{:S(2)}) collective-permute-start(f32[10,128]{1,0:T(8,128)S(1)} %reshape.235), channel_id=1, source_target_pairs={{0,1},{1,2},{2,3},{3,4},{4,5},{5,6},{6,7},{7,8},{8,9},{9,10},{10,1... | collective-permute-start | bytes 15368 | tf_op jit(solution)/shard_map/ppermute | solution.py:202
  53.3 3.2 %copy-start.8 = (f32[2,32,32,1]{2,1,0,3:T(8,128)S(1)}, f32[2,32,32,1]{2,1,0,3:T(8,128)}, u32[]{:S(2)}) copy-start(f32[2,32,32,1]{2,1,0,3:T(8,128)} %constant.98) | copy-start | bytes 24580
  56.4 1.6 %copy-start.9 = (f32[32,128]{1,0:T(8,128)S(1)}, f32[32,128]{1,0:T(8,128)}, u32[]{:S(2)}) copy-start(f32[32,128]{1,0:T(8,128)} %constant.95) | copy-start | bytes 49156
  56.4 1.6 %copy-start.10 = (f32[32,128]{1,0:T(8,128)S(1)}, f32[32,128]{1,0:T(8,128)}, u32[]{:S(2)}) copy-start(f32[32,128]{1,0:T(8,128)} %constant.96) | copy-start | bytes 49156
  58.1 1.0 copy-start.2
  58.1 1.0 copy-start.3
  61.8 10.8 %copy-start.11 = (f32[2]{0:T(128)S(1)}, f32[2]{0:T(128)}, u32[]{:S(2)}) copy-start(f32[2]{0:T(128)} %param.20) | copy-start | bytes 28
  61.8 11.4 %copy-start.6 = (f32[12,32,128]{2,1,0:T(8,128)S(1)}, f32[12,32,128]{2,1,0:T(8,128)}, u32[]{:S(2)}) copy-start(f32[12,32,128]{2,1,0:T(8,128)} %param.18) | copy-start | bytes 589828
  61.8 11.4 %copy-start.7 = (f32[12,32,128]{2,1,0:T(8,128)S(1)}, f32[12,32,128]{2,1,0:T(8,128)}, u32[]{:S(2)}) copy-start(f32[12,32,128]{2,1,0:T(8,128)} %param.17) | copy-start | bytes 589828
  61.8 28.5 %all-to-all-start.2 = ((f32[1,32,17,128]{3,0,2,1:T(1,128)}), f32[1,32,17,128]{3,0,2,1:T(1,128)S(1)}, u32[]{:S(2)}, u32[]{:S(2)}) async-start(f32[1,32,17,128]{3,0,2,1:T(1,128)} %copy.39), calls=%async_computation.2 | async-start | bytes 557056 | tf_op jit(solution)/shard_map/all_to_all | solution.py:183

commit v15 on v14

--- a/solution.py
+++ b/solution.py
@@ -107,7 +107,7 @@
 
 def contract(einsum_form, left, right):
     return jnp.einsum(
-        einsum_form, left, right, precision=lax.Precision.HIGHEST, preferred_element_type=jnp.float32
+        einsum_form, left, right, precision=lax.Precision.HIGH, preferred_element_type=jnp.float32
     )
 
 

time: 113 us -> 112 us (level)
  matrix products: 5.61 us -> 4.15 us
    dot_general x6, matrix products: 5.61 us -> 4.15 us  [contract(): jnp.einsum(einsum_form, left, right, precision=lax.Precision.HIGH, prefer...]
where the time goes in v15:
time: 112 us; the launch traced here: 111 us
  starting transfers between devices  49.5 us (44%)
  waiting for transfers between devices  21.2 us (19%)
  blocking collectives  17.8 us (16%)
  other arithmetic  10.8 us (10%)
  local copies, waits for them, and re-layouts  6.34 us (6%)
  matrix products  4.15 us (4%)
  between operations  1.21 us (1%)
    all_to_all x1, blocking collectives, convolve_and_sum(): back = lax.all_to_all(final, 'kx', split_axis=1, concat_axis=0, tiled=True)  17.8 us
    all_to_all x1, waiting for transfers between devices, convolve_and_sum(): lax.all_to_all(back_y, 'ky', split_axis=1, concat_axis=1, tiled=True)  14.5 us
    all_to_all x1, starting transfers between devices, convolve_and_sum(): lax.all_to_all(split, 'ky', split_axis=1, concat_axis=1, tiled=True)  14.1 us
    all_to_all x1, starting transfers between devices, convolve_and_sum(): lax.all_to_all(back_y, 'ky', split_axis=1, concat_axis=1, tiled=True)  10.8 us
    all_to_all x1, starting transfers between devices, convolve_and_sum(): lax.all_to_all(source, 'kx', split_axis=0, concat_axis=1, tiled=True)  10.3 us
    ppermute x2, starting transfers between devices, neighbours(): lax.ppermute(initial.reshape(dense), axis, down).reshape(initial.shape)  8.9 us
    ppermute x2, waiting for transfers between devices, neighbours(): before = lax.ppermute(last.reshape(dense), axis, up).reshape(last.shape)  6.68 us
    ppermute x2, starting transfers between devices, neighbours(): before = lax.ppermute(last.reshape(dense), axis, up).reshape(last.shape)  5.35 us
  transfers between devices with their start and end apart: 7, of which 3 were waited for; matrix products, arithmetic and copies ran while one was open for 10% of the time, Pallas kernels for 0%

profile of v15, /device:TPU:1, one launch (start us, length us, event | category | flops | bytes accessed | tf_op | source)
XLA Modules:
  0.0 111.0 jit_solution(3121154324854691660)
XLA Ops:
  0.6 10.3 %all-to-all-start = ((f32[16,32,128]{2,1,0:T(8,128)}), f32[16,32,128]{2,1,0:T(8,128)S(1)}, u32[]{:S(2)}, u32[]{:S(2)}) async-start(f32[16,32,128]{2,1,0:T(8,128)} %param.15), calls=%async_computation | async-start | bytes 524288 | tf_op jit(solution)/shard_map/all_to_all | solution.py:171
  11.0 0.8 copy-done.4
  11.9 2.1 %collective-permute-start = (f32[40,128]{1,0:T(8,128)S(1)}, f32[40,128]{1,0:T(8,128)S(1)}, u32[]{:S(2)}, u32[]{:S(2)}) collective-permute-start(f32[40,128]{1,0:T(8,128)S(1)} %bitcast.101), channel_id=1, source_target_pairs={{32,0},{64,32},{96,64},{128,96},{160,128},{192,160},{224,192},{256... | collective-permute-start | bytes 61448 | tf_op jit(solution)/shard_map/ppermute | solution.py:203
  14.0 3.4 %collective-permute-start.1 = (f32[40,128]{1,0:T(8,128)S(1)}, f32[40,128]{1,0:T(8,128)S(1)}, u32[]{:S(2)}, u32[]{:S(2)}) collective-permute-start(f32[40,128]{1,0:T(8,128)S(1)} %bitcast.100), channel_id=1, source_target_pairs={{0,32},{32,64},{64,96},{96,128},{128,160},{160,192},{192,224},{224... | collective-permute-start | bytes 61448 | tf_op jit(solution)/shard_map/ppermute | solution.py:202
  17.5 0.6 add_reduce_fusion
  18.5 1.0 copy.36
  19.5 0.6 compare_reduce_fusion
  20.5 1.3 %convolution_bitcast_fusion.5 = f32[1,512,128]{2,1,0:T(8,128)} fusion(f32[512,512]{1,0:T(8,128)S(1)} %copy-done.1, f32[512,128]{1,0:T(8,128)S(1)} %bitcast.95), kind=kOutput, calls=%fused_computation.7 | convolution fusion | flops 201326592 | bytes 1572864 | tf_op jit(solution)/shard_map/px,cxy->cpy/dot_general | solution.py:109
  21.8 14.1 %all-to-all-start.1 = ((f32[1,32,16,128]{3,2,0,1:T(8,128)}), f32[1,32,16,128]{3,2,0,1:T(8,128)}, u32[]{:S(2)}, u32[]{:S(2)}) async-start(f32[1,32,16,128]{3,2,0,1:T(8,128)} %bitcast.6), calls=%async_computation.1 | async-start | bytes 524288 | tf_op jit(solution)/shard_map/all_to_all | solution.py:178
  36.3 6.8 %collective-permute-start.2 = (f32[10,128]{1,0:T(8,128)S(1)}, f32[10,128]{1,0:T(8,128)S(1)}, u32[]{:S(2)}, u32[]{:S(2)}) collective-permute-start(f32[10,128]{1,0:T(8,128)S(1)} %reshape.233), channel_id=1, source_target_pairs={{1,0},{2,1},{3,2},{4,3},{5,4},{6,5},{7,6},{8,7},{9,8},{10,9},{11,1... | collective-permute-start | bytes 15368 | tf_op jit(solution)/shard_map/ppermute | solution.py:203
  43.3 1.9 %collective-permute-start.3 = (f32[10,128]{1,0:T(8,128)S(1)}, f32[10,128]{1,0:T(8,128)S(1)}, u32[]{:S(2)}, u32[]{:S(2)}) collective-permute-start(f32[10,128]{1,0:T(8,128)S(1)} %reshape.235), channel_id=1, source_target_pairs={{0,1},{1,2},{2,3},{3,4},{4,5},{5,6},{6,7},{7,8},{8,9},{9,10},{10,1... | collective-permute-start | bytes 15368 | tf_op jit(solution)/shard_map/ppermute | solution.py:202
  45.6 6.5 %collective-permute-done.3 = f32[10,128]{1,0:T(8,128)S(1)} collective-permute-done((f32[10,128]{1,0:T(8,128)S(1)}, f32[10,128]{1,0:T(8,128)S(1)}, u32[]{:S(2)}, u32[]{:S(2)}) %collective-permute-start.3) | collective-permute-done | bytes 5152 | tf_op jit(solution)/shard_map/ppermute | solution.py:202
  52.9 0.6 fusion.24
  53.5 2.5 %broadcast_select_fusion.1 = f32[1,1,1,3]{3,2,1,0:T(1,128)S(1)} fusion(pred[]{:T(512)} %compare_reduce_fusion, f32[1,1,1,1]{3,2,1,0:T(1,128)} %bitcast.35, f32[1,1,1,1]{3,2,1,0:T(1,128)} %bitcast.34, f32[1,1,1,1]{3,2,1,0:T(1,128)} %bitcast.29), kind=kLoop, calls=%fused_computation.87 | loop fusion | flops 9 | bytes 25 | tf_op jit(solution)/shard_map/reshape | solution.py:162
  56.1 1.3 %convolution_bitcast_fusion.1 = f32[2,1,32,16,128]{4,2,0,3,1:T(8,128)S(1)} fusion(f32[2,32,32,1]{2,1,0,3:T(8,128)S(1)} %copy-done.8, f32[1,32,16,128]{3,2,0,1:T(8,128)} %all-to-all-done.1), kind=kOutput, calls=%fused_computation.1 | convolution fusion | flops 25165824 | bytes 794624 | tf_op jit(solution)/shard_map/ska,capb->sckpb/dot_general | solution.py:109
  57.5 0.8 copy-done.2
  59.6 1.0 copy.39
  60.6 10.8 %all-to-all-start.2 = ((f32[1,32,17,128]{3,0,2,1:T(1,128)}), f32[1,32,17,128]{3,0,2,1:T(1,128)S(1)}, u32[]{:S(2)}, u32[]{:S(2)}) async-start(f32[1,32,17,128]{3,0,2,1:T(1,128)} %copy.39), calls=%async_computation.2 | async-start | bytes 557056 | tf_op jit(solution)/shard_map/all_to_all | solution.py:183
  72.0 1.3 %multiply_add_fusion.2 = f32[12,32,128]{2,1,0:T(8,128)S(1)} fusion(f32[12,32,128]{2,1,0:T(8,128)S(1)} %copy-done.6, f32[12,32,128]{2,1,0:T(8,128)S(1)} %copy-done.7, f32[]{:T(128)} %bitcast.38, f32[]{:T(128)} %bitcast.37), kind=kLoop, calls=%fused_computation.52 | loop fusion | flops 147456 | bytes 589832 | tf_op jit(solution)/shard_map/add | solution.py:246
  73.4 1.3 %fusion.19 = f32[16,32,128]{2,1,0:T(8,128)S(1)} fusion(f32[20,32,128]{2,1,0:T(8,128)S(1)} %fusion.16, f32[20,32,128]{2,1,0:T(8,128)S(1)} %fusion.10, f32[]{:T(128)} %bitcast.38, f32[]{:T(128)} %bitcast.37), kind=kLoop, calls=%fused_computation.40 | loop fusion | flops 196608 | bytes 786440 | tf_op jit(solution)/shard_map/add | solution.py:247
  74.8 14.5 %all-to-all-done.2 = f32[1,32,17,128]{3,0,2,1:T(1,128)S(1)} async-done(((f32[1,32,17,128]{3,0,2,1:T(1,128)}), f32[1,32,17,128]{3,0,2,1:T(1,128)S(1)}, u32[]{:S(2)}, u32[]{:S(2)}) %all-to-all-start.2) | async-done | bytes 278560 | tf_op jit(solution)/shard_map/all_to_all | solution.py:183
  90.9 17.8 %all_to_all.31 = f32[1,16,33,128]{3,0,2,1:T(1,128)S(1)} all-to-all(f32[1,16,33,128]{3,0,2,1:T(1,128)S(1)} %copy.42), channel_id=1, replica_groups=mesh['kx'=16,'ky'=32] {'kx'}, dimensions={1} | all-to-all | bytes 540672 | tf_op jit(solution)/shard_map/all_to_all | solution.py:189
  108.7 0.6 multiply_subtract_fusion.2
  110.3 0.7 add.931
  (85 shorter events, 6.8 us)
Async XLA Ops:
  0.6 10.4 %copy-start = (f32[16,32,128]{2,1,0:T(8,128)S(1)}, f32[16,32,128]{2,1,0:T(8,128)}, u32[]{:S(2)}) copy-start(f32[16,32,128]{2,1,0:T(8,128)} %param.15) | copy-start | bytes 786436
  0.6 19.9 %all-to-all-start = ((f32[16,32,128]{2,1,0:T(8,128)}), f32[16,32,128]{2,1,0:T(8,128)S(1)}, u32[]{:S(2)}, u32[]{:S(2)}) async-start(f32[16,32,128]{2,1,0:T(8,128)} %param.15), calls=%async_computation | async-start | bytes 524288 | tf_op jit(solution)/shard_map/all_to_all | solution.py:171
  11.0 0.8 copy-start.4
  11.0 6.4 %copy-start.5 = (f32[16,4096]{1,0:T(8,128)S(1)}, f32[16,4096]{1,0:T(8,128)}, u32[]{:S(2)}) copy-start(f32[16,4096]{1,0:T(8,128)} %param.19) | copy-start | bytes 786436
  11.9 8.3 %collective-permute-start = (f32[40,128]{1,0:T(8,128)S(1)}, f32[40,128]{1,0:T(8,128)S(1)}, u32[]{:S(2)}, u32[]{:S(2)}) collective-permute-start(f32[40,128]{1,0:T(8,128)S(1)} %bitcast.101), channel_id=1, source_target_pairs={{32,0},{64,32},{96,64},{128,96},{160,128},{192,160},{224,192},{256... | collective-permute-start | bytes 61448 | tf_op jit(solution)/shard_map/ppermute | solution.py:203
  14.0 6.3 %collective-permute-start.1 = (f32[40,128]{1,0:T(8,128)S(1)}, f32[40,128]{1,0:T(8,128)S(1)}, u32[]{:S(2)}, u32[]{:S(2)}) collective-permute-start(f32[40,128]{1,0:T(8,128)S(1)} %bitcast.100), channel_id=1, source_target_pairs={{0,32},{32,64},{64,96},{96,128},{128,160},{160,192},{192,224},{224... | collective-permute-start | bytes 61448 | tf_op jit(solution)/shard_map/ppermute | solution.py:202
  18.5 2.1 %copy-start.1 = (f32[512,512]{1,0:T(8,128)S(1)}, f32[512,512]{1,0:T(8,128)}, u32[]{:S(2)}) copy-start(f32[512,512]{1,0:T(8,128)} %constant.85.clone) | copy-start | bytes 3145732
  21.8 34.2 %all-to-all-start.1 = ((f32[1,32,16,128]{3,2,0,1:T(8,128)}), f32[1,32,16,128]{3,2,0,1:T(8,128)}, u32[]{:S(2)}, u32[]{:S(2)}) async-start(f32[1,32,16,128]{3,2,0,1:T(8,128)} %bitcast.6), calls=%async_computation.1 | async-start | bytes 524288 | tf_op jit(solution)/shard_map/all_to_all | solution.py:178
  36.3 8.9 %collective-permute-start.2 = (f32[10,128]{1,0:T(8,128)S(1)}, f32[10,128]{1,0:T(8,128)S(1)}, u32[]{:S(2)}, u32[]{:S(2)}) collective-permute-start(f32[10,128]{1,0:T(8,128)S(1)} %reshape.233), channel_id=1, source_target_pairs={{1,0},{2,1},{3,2},{4,3},{5,4},{6,5},{7,6},{8,7},{9,8},{10,9},{11,1... | collective-permute-start | bytes 15368 | tf_op jit(solution)/shard_map/ppermute | solution.py:203
  43.3 8.7 %collective-permute-start.3 = (f32[10,128]{1,0:T(8,128)S(1)}, f32[10,128]{1,0:T(8,128)S(1)}, u32[]{:S(2)}, u32[]{:S(2)}) collective-permute-start(f32[10,128]{1,0:T(8,128)S(1)} %reshape.235), channel_id=1, source_target_pairs={{0,1},{1,2},{2,3},{3,4},{4,5},{5,6},{6,7},{7,8},{8,9},{9,10},{10,1... | collective-permute-start | bytes 15368 | tf_op jit(solution)/shard_map/ppermute | solution.py:202
  52.9 3.2 %copy-start.8 = (f32[2,32,32,1]{2,1,0,3:T(8,128)S(1)}, f32[2,32,32,1]{2,1,0,3:T(8,128)}, u32[]{:S(2)}) copy-start(f32[2,32,32,1]{2,1,0,3:T(8,128)} %constant.98) | copy-start | bytes 24580
  56.0 1.4 %copy-start.9 = (f32[32,128]{1,0:T(8,128)S(1)}, f32[32,128]{1,0:T(8,128)}, u32[]{:S(2)}) copy-start(f32[32,128]{1,0:T(8,128)} %constant.95) | copy-start | bytes 49156
  56.0 1.4 %copy-start.10 = (f32[32,128]{1,0:T(8,128)S(1)}, f32[32,128]{1,0:T(8,128)}, u32[]{:S(2)}) copy-start(f32[32,128]{1,0:T(8,128)} %constant.96) | copy-start | bytes 49156
  57.4 1.0 copy-start.2
  57.5 1.0 copy-start.3
  60.6 10.8 %copy-start.11 = (f32[2]{0:T(128)S(1)}, f32[2]{0:T(128)}, u32[]{:S(2)}) copy-start(f32[2]{0:T(128)} %param.20) | copy-start | bytes 28
  60.6 11.4 %copy-start.6 = (f32[12,32,128]{2,1,0:T(8,128)S(1)}, f32[12,32,128]{2,1,0:T(8,128)}, u32[]{:S(2)}) copy-start(f32[12,32,128]{2,1,0:T(8,128)} %param.18) | copy-start | bytes 589828
  60.6 11.4 %copy-start.7 = (f32[12,32,128]{2,1,0:T(8,128)S(1)}, f32[12,32,128]{2,1,0:T(8,128)}, u32[]{:S(2)}) copy-start(f32[12,32,128]{2,1,0:T(8,128)} %param.17) | copy-start | bytes 589828
  60.6 28.6 %all-to-all-start.2 = ((f32[1,32,17,128]{3,0,2,1:T(1,128)}), f32[1,32,17,128]{3,0,2,1:T(1,128)S(1)}, u32[]{:S(2)}, u32[]{:S(2)}) async-start(f32[1,32,17,128]{3,0,2,1:T(1,128)} %copy.39), calls=%async_computation.2 | async-start | bytes 557056 | tf_op jit(solution)/shard_map/all_to_all | solution.py:183
